TPU v7x, 512 devices: a whole 4x8x8 slice. The times are simulated.
512 devices in a mesh: dp: 64 (over z_lo, y, core), seq: 8 (over x, z_hi).
Axes of the slice: x: 4, y: 8, z: 8 (z_hi: 2, z_lo: 4; z = z_hi * 4 + z_lo), core: 2. Of those that a mesh axis runs over, the one named last changes fastest.
Arguments:
- queries: bfloat16 [65536, 3072], P(('dp', 'seq'))
- keys: bfloat16 [65536, 1024], P(('dp', 'seq'))
- values: bfloat16 [65536, 1024], P(('dp', 'seq')), may hold values from -6 to 6
- output_gradient: bfloat16 [65536, 3072], P(('dp', 'seq')), may hold values from -48 to 48
- seg_lengths: int32 [64, 4], P('dp'), may hold values from 2 to 512, as said below
- knocked: int32 [64, 2], replicated, may hold values from 0 to 7, all different within a row
- source: int32 [64], replicated, may hold values from 0 to 63, as said below
Outputs:
- query_grad: bfloat16 [65536, 3072], P(('dp', 'seq'))
- key_grad: bfloat16 [65536, 1024], P(('dp', 'seq'))
- value_grad: bfloat16 [65536, 1024], P(('dp', 'seq'))
Inputs may be any that keep to these rules, and one draw needn't show every extreme that they name: `knocked`: row p lists 2 different key-value heads of prompt p; every head is listed in some row. source is a permutation of the prompts with source[p] != p. `seg_lengths`: each row holds 4 even lengths that sum to 1024; one of them is exactly 512.
All inputs are finite; a program needn't handle non-finite values.
Results may differ from a plain program's by a relative error of at most 0.005.
Values may be sent and summed in bfloat16 or wider, within the bound.
No kernel may reach another device: no remote copies, remote signals or barrier semaphores. Data moves between devices by JAX's collectives and lax.ppermute only.
A program may use at most 64 MiB of HBM per device.

v0:
```python
import math

import jax
import jax.numpy as jnp
from jax import lax
from jax.sharding import PartitionSpec as P

KEY_VALUE_HEADS = 8
HEAD_WIDTH = 128


masked_score = -1e30


def document_mask(lengths, length):
    doc_ends = jnp.cumsum(lengths)
    position = jnp.arange(length, dtype=jnp.int32)
    segment = jnp.sum((position[:, None] >= doc_ends[None, :]).astype(jnp.int32), axis=1)
    causal = position[:, None] >= position[None, :]
    return jnp.logical_and(causal, segment[:, None] == segment[None, :])


def attend_back(query_side, key_side, value_side, grad_side, visible):
    length = query_side.shape[0]
    heads_of_query = query_side.shape[1] // HEAD_WIDTH
    scaling = 1.0 / math.sqrt(HEAD_WIDTH)

    def one_head(head_index, totals):
        query_grads, key_grads, value_gradient = totals
        query_rows = lax.dynamic_slice_in_dim(query_side, head_index * HEAD_WIDTH, HEAD_WIDTH, 1)
        grad_rows = lax.dynamic_slice_in_dim(grad_side, head_index * HEAD_WIDTH, HEAD_WIDTH, 1)
        scores = (
            jnp.einsum("id,jd->ij", query_rows, key_side, preferred_element_type=jnp.float32)
            * scaling
        )
        scores = jnp.where(visible, scores, masked_score)
        row_max = jnp.max(scores, axis=1, keepdims=True)
        weights = jnp.exp(scores - row_max)
        attn_probs = weights / jnp.sum(weights, axis=1, keepdims=True)
        probs_low = attn_probs.astype(jnp.bfloat16)
        value_part = jnp.einsum(
            "ij,id->jd", probs_low, grad_rows, preferred_element_type=jnp.float32
        )
        prob_grads = jnp.einsum(
            "id,jd->ij", grad_rows, value_side, preferred_element_type=jnp.float32
        )
        row_delta = jnp.sum(attn_probs * prob_grads, axis=1, keepdims=True)
        score_grads = (attn_probs * (prob_grads - row_delta) * scaling).astype(jnp.bfloat16)
        query_part = jnp.dot(score_grads, key_side, preferred_element_type=jnp.float32)
        key_part = jnp.einsum(
            "ij,id->jd", score_grads, query_rows, preferred_element_type=jnp.float32
        )
        query_grads = lax.dynamic_update_slice_in_dim(
            query_grads, query_part.astype(jnp.bfloat16), head_index * HEAD_WIDTH, 1
        )
        key_sum = key_grads + key_part
        key_grads = key_sum
        value_sum = value_gradient + value_part
        value_gradient = value_sum
        return (query_grads, key_grads, value_gradient)

    initial = (
        jnp.zeros((length, query_side.shape[1]), jnp.bfloat16),
        jnp.zeros((length, key_side.shape[1]), jnp.float32),
        jnp.zeros((length, value_side.shape[1]), jnp.float32),
    )
    return lax.fori_loop(0, heads_of_query, one_head, initial)


def per_device(queries, keys, values, output_gradient, seg_lengths, knocked, source):
    sequence_count = lax.axis_size("seq")
    prompt_count = lax.axis_size("dp")
    tok_rows = queries.shape[0]
    length = tok_rows * sequence_count
    local_key_value = KEY_VALUE_HEADS // sequence_count
    prompt_index = lax.axis_index("dp")
    seq_index = lax.axis_index("seq")
    prompt_ids = jnp.arange(prompt_count, dtype=jnp.int32)
    consumer = jnp.sum(
        jnp.where(source[None, :] == prompt_ids[:, None], prompt_ids[None, :], 0), axis=1
    )
    my_knock = knocked[prompt_index]
    visible = document_mask(seg_lengths[0], length)
    query_side, key_side, value_side, grad_side = (
        lax.all_to_all(queries, "seq", split_axis=1, concat_axis=0, tiled=True),
        lax.all_to_all(keys, "seq", split_axis=1, concat_axis=0, tiled=True),
        lax.all_to_all(values, "seq", split_axis=1, concat_axis=0, tiled=True),
        lax.all_to_all(output_gradient, "seq", split_axis=1, concat_axis=0, tiled=True),
    )
    local_heads = seq_index * local_key_value + jnp.arange(local_key_value, dtype=jnp.int32)
    local_knock = jnp.any(my_knock[:, None] == local_heads[None, :], axis=0)
    column_knock = jnp.repeat(local_knock, HEAD_WIDTH)
    rows_each = length // prompt_count
    spread = lax.all_to_all(key_side, "dp", split_axis=0, concat_axis=0, tiled=True)
    routed = jnp.take(spread.reshape(prompt_count, rows_each, -1), source, axis=0).reshape(
        length, -1
    )
    fetched = lax.all_to_all(routed, "dp", split_axis=0, concat_axis=0, tiled=True)
    key_side = jnp.where(column_knock[None, :], fetched, key_side)
    query_grads, key_grads, value_gradient = attend_back(
        query_side, key_side, value_side, grad_side, visible
    )
    value_low = value_gradient.astype(jnp.bfloat16)
    patch_grads = jnp.where(column_knock[None, :], key_grads, 0.0)
    spread = lax.all_to_all(patch_grads, "dp", split_axis=0, concat_axis=0, tiled=True)
    routed = jnp.take(spread.reshape(prompt_count, rows_each, -1), consumer, axis=0).reshape(
        length, -1
    )
    returned = lax.all_to_all(routed, "dp", split_axis=0, concat_axis=0, tiled=True)
    key_overall = (jnp.where(column_knock[None, :], 0.0, key_grads) + returned).astype(jnp.bfloat16)
    query_out, key_result, value_result = (
        lax.all_to_all(query_grads, "seq", split_axis=0, concat_axis=1, tiled=True),
        lax.all_to_all(key_overall, "seq", split_axis=0, concat_axis=1, tiled=True),
        lax.all_to_all(value_low, "seq", split_axis=0, concat_axis=1, tiled=True),
    )
    return (query_out, key_result, value_result)


def solution(mesh):
    placed = (
        P(("dp", "seq"), None),
        P(("dp", "seq"), None),
        P(("dp", "seq"), None),
        P(("dp", "seq"), None),
        P("dp", None),
        P(),
        P(),
    )
    return jax.shard_map(
        per_device,
        mesh=mesh,
        in_specs=placed,
        out_specs=(P(("dp", "seq"), None), P(("dp", "seq"), None), P(("dp", "seq"), None)),
        check_vma=False,
    )
```

profile of v0, /device:TPU:65, one launch (start us, length us, event | category | flops | bytes accessed | tf_op | source)
XLA Modules:
  0.0 290.0 jit_solution(7179095610386368778)
XLA Ops:
  0.7 0.9 copy-done
  2.3 11.6 %all-to-all-start.1 = ((bf16[128,8,128]{2,0,1:T(8,128)(2,1)}), bf16[128,8,128]{2,0,1:T(8,128)(2,1)}, u32[]{:S(2)}, u32[]{:S(2)}) async-start(bf16[128,8,128]{2,0,1:T(8,128)(2,1)} %copy_bitcast_fusion.3), calls=%async_computation.1 | async-start | bytes 524288 | tf_op jit(solution)/shard_map/all_to_all | solution.py:86
  13.9 1.0 copy_bitcast_fusion.2
  14.9 9.1 %all-to-all-done.1 = bf16[128,8,128]{2,0,1:T(8,128)(2,1)} async-done(((bf16[128,8,128]{2,0,1:T(8,128)(2,1)}), bf16[128,8,128]{2,0,1:T(8,128)(2,1)}, u32[]{:S(2)}, u32[]{:S(2)}) %all-to-all-start.1) | async-done | bytes 262176 | tf_op jit(solution)/shard_map/all_to_all | solution.py:86
  24.1 12.7 %all_to_all.169 = bf16[128,8,128]{2,0,1:T(8,128)(2,1)S(1)} all-to-all(bf16[128,8,128]{2,0,1:T(8,128)(2,1)S(1)} %copy_bitcast_fusion.2), channel_id=1, replica_groups=mesh['dp'=64,'seq'=8] {'seq'}, dimensions={1} | all-to-all | bytes 524288 | tf_op jit(solution)/shard_map/all_to_all | solution.py:87
  36.8 16.3 %all-to-all-start.2 = ((bf16[64,16,128]{2,1,0:T(8,128)(2,1)}), bf16[64,16,128]{2,1,0:T(8,128)(2,1)S(1)}, u32[]{:S(2)}, u32[]{:S(2)}) async-start(bf16[64,16,128]{2,1,0:T(8,128)(2,1)} %bitcast.3), calls=%async_computation.2 | async-start | bytes 524288 | tf_op jit(solution)/shard_map/all_to_all | solution.py:94
  53.1 2.1 copy.50
  55.2 9.4 %all-to-all-done.2 = bf16[64,16,128]{2,1,0:T(8,128)(2,1)S(1)} async-done(((bf16[64,16,128]{2,1,0:T(8,128)(2,1)}), bf16[64,16,128]{2,1,0:T(8,128)(2,1)S(1)}, u32[]{:S(2)}, u32[]{:S(2)}) %all-to-all-start.2) | async-done | bytes 262176 | tf_op jit(solution)/shard_map/all_to_all | solution.py:94
  64.7 3.5 %all-to-all-start = ((bf16[128,8,384]{2,0,1:T(8,128)(2,1)}), bf16[128,8,384]{2,0,1:T(8,128)(2,1)S(1)}, u32[]{:S(2)}, u32[]{:S(2)}) async-start(bf16[128,8,384]{2,0,1:T(8,128)(2,1)} %bitcast.62), calls=%async_computation | async-start | bytes 1572864 | tf_op jit(solution)/shard_map/all_to_all | solution.py:85
  69.8 23.4 %all-to-all-done = bf16[128,8,384]{2,0,1:T(8,128)(2,1)S(1)} async-done(((bf16[128,8,384]{2,0,1:T(8,128)(2,1)}), bf16[128,8,384]{2,0,1:T(8,128)(2,1)S(1)}, u32[]{:S(2)}, u32[]{:S(2)}) %all-to-all-start) | async-done | bytes 786464 | tf_op jit(solution)/shard_map/all_to_all | solution.py:85
  93.1 6.8 %all-to-all-start.3 = ((bf16[64,16,128]{2,1,0:T(8,128)(2,1)}), bf16[64,16,128]{2,1,0:T(8,128)(2,1)S(1)}, u32[]{:S(2)}, u32[]{:S(2)}) async-start(bf16[64,16,128]{2,1,0:T(8,128)(2,1)} %broadcast_select_fusion.2), calls=%async_computation.3 | async-start | bytes 524288 | tf_op jit(solution)/shard_map/all_to_all | solution.py:98
  99.9 1.0 copy.49
  100.9 10.6 %all-to-all-done.3 = bf16[64,16,128]{2,1,0:T(8,128)(2,1)S(1)} async-done(((bf16[64,16,128]{2,1,0:T(8,128)(2,1)}), bf16[64,16,128]{2,1,0:T(8,128)(2,1)S(1)}, u32[]{:S(2)}, u32[]{:S(2)}) %all-to-all-start.3) | async-done | bytes 262176 | tf_op jit(solution)/shard_map/all_to_all | solution.py:98
  111.5 3.5 %all-to-all-start.4 = ((bf16[128,8,384]{2,0,1:T(8,128)(2,1)}), bf16[128,8,384]{2,0,1:T(8,128)(2,1)S(1)}, u32[]{:S(2)}, u32[]{:S(2)}) async-start(bf16[128,8,384]{2,0,1:T(8,128)(2,1)} %bitcast.61), calls=%async_computation.4 | async-start | bytes 1572864 | tf_op jit(solution)/shard_map/all_to_all | solution.py:88
  116.0 2.3 bitcast_select_fusion
  118.3 21.6 %all-to-all-done.4 = bf16[128,8,384]{2,0,1:T(8,128)(2,1)S(1)} async-done(((bf16[128,8,384]{2,0,1:T(8,128)(2,1)}), bf16[128,8,384]{2,0,1:T(8,128)(2,1)S(1)}, u32[]{:S(2)}, u32[]{:S(2)}) %all-to-all-start.4) | async-done | bytes 786464 | tf_op jit(solution)/shard_map/all_to_all | solution.py:88
  139.9 0.9 broadcast_in_dim.88
  140.8 37.1 %while.18 = (s32[]{:T(128)}, bf16[1024,384]{1,0:T(8,128)(2,1)}, f32[1024,128]{1,0:T(8,128)S(1)}, f32[1024,128]{1,0:T(8,128)S(1)}, bf16[1024,384]{1,0:T(8,128)(2,...) while((s32[]{:T(128)}, bf16[1024,384]{1,0:T(8,128)(2,1)}, ...), condition=%wide.region_7.8_spmd.clone, body=%wide.region_3.0_spmd.clone.sunk | while | flops 1364849664 | bytes 74502432 | solution.py:67
  140.8 1.8 fusion.51
  142.7 1.9 copy-done.1
  145.3 3.2 %fusion.54 = f32[1024,128]{1,0:T(8,128)S(1)} fusion(f32[1024,128]{1,0:T(8,128)S(1)} %get-tuple-element.302, pred[]{:T(512)S(6)} %compare.3, bf16[1024,384]{1,0:T(8,128)(2,1)S(1)} %get-tuple-element.318, s32[]{:T(128)S(6)} %select_n.97, f32[1024,1024]{0,1:T(8,128)} %copy-done.1, f32[1024]{0:T(1024)S(1)} %fusion.52, f32[1024]{0:T(1024)S(1)} %get-tuple-element.283), kind=kOutput, calls=%fused_computation.13.clone.1 | convolution fusion | flops 271843328 | bytes 5513221 | tf_op jit(solution)/shard_map/while/body/eval_jaxpr/ij,id->jd/dot_general | solution.py:41
  148.7 1.0 multiply_reduce_fusion.2
  149.7 1.2 multiply_convert_fusion.2
  150.9 1.5 fusion.53
  153.2 1.9 fusion.51
  155.1 1.9 copy-done.1
  157.6 3.2 %fusion.54 = f32[1024,128]{1,0:T(8,128)S(1)} fusion(f32[1024,128]{1,0:T(8,128)S(1)} %get-tuple-element.302, pred[]{:T(512)S(6)} %compare.3, bf16[1024,384]{1,0:T(8,128)(2,1)S(1)} %get-tuple-element.318, s32[]{:T(128)S(6)} %select_n.97, f32[1024,1024]{0,1:T(8,128)} %copy-done.1, f32[1024]{0:T(1024)S(1)} %fusion.52, f32[1024]{0:T(1024)S(1)} %get-tuple-element.283), kind=kOutput, calls=%fused_computation.13.clone.1 | convolution fusion | flops 271843328 | bytes 5513221 | tf_op jit(solution)/shard_map/while/body/eval_jaxpr/ij,id->jd/dot_general | solution.py:41
  161.1 1.0 multiply_reduce_fusion.2
  162.1 1.2 multiply_convert_fusion.2
  163.3 1.5 fusion.53
  165.6 1.9 fusion.51
  167.4 1.9 copy-done.1
  170.0 3.2 %fusion.54 = f32[1024,128]{1,0:T(8,128)S(1)} fusion(f32[1024,128]{1,0:T(8,128)S(1)} %get-tuple-element.302, pred[]{:T(512)S(6)} %compare.3, bf16[1024,384]{1,0:T(8,128)(2,1)S(1)} %get-tuple-element.318, s32[]{:T(128)S(6)} %select_n.97, f32[1024,1024]{0,1:T(8,128)} %copy-done.1, f32[1024]{0:T(1024)S(1)} %fusion.52, f32[1024]{0:T(1024)S(1)} %get-tuple-element.283), kind=kOutput, calls=%fused_computation.13.clone.1 | convolution fusion | flops 271843328 | bytes 5513221 | tf_op jit(solution)/shard_map/while/body/eval_jaxpr/ij,id->jd/dot_general | solution.py:41
  173.4 1.0 multiply_reduce_fusion.2
  174.4 1.2 multiply_convert_fusion.2
  175.6 1.5 fusion.53
  177.9 1.5 broadcast_select_fusion.1
  179.4 6.8 %all-to-all-start.7 = ((f32[64,16,128]{2,1,0:T(8,128)}), f32[64,16,128]{2,1,0:T(8,128)S(1)}, u32[]{:S(2)}, u32[]{:S(2)}) async-start(f32[64,16,128]{2,1,0:T(8,128)} %bitcast.15), calls=%async_computation.7 | async-start | bytes 1048576 | tf_op jit(solution)/shard_map/all_to_all | solution.py:105
  187.1 16.3 %all-to-all-done.7 = f32[64,16,128]{2,1,0:T(8,128)S(1)} async-done(((f32[64,16,128]{2,1,0:T(8,128)}), f32[64,16,128]{2,1,0:T(8,128)S(1)}, u32[]{:S(2)}, u32[]{:S(2)}) %all-to-all-start.7) | async-done | bytes 524320 | tf_op jit(solution)/shard_map/all_to_all | solution.py:105
  203.4 3.4 %all-to-all-start.10 = ((bf16[8,128,128]{2,1,0:T(8,128)(2,1)}), bf16[8,128,128]{2,1,0:T(8,128)(2,1)S(1)}, u32[]{:S(2)}, u32[]{:S(2)}) async-start(bf16[8,128,128]{2,1,0:T(8,128)(2,1)} %bitcast.22), calls=%async_computation.10 | async-start | bytes 524288 | tf_op jit(solution)/shard_map/all_to_all | solution.py:114
  207.6 13.0 %all-to-all-done.10 = bf16[8,128,128]{2,1,0:T(8,128)(2,1)S(1)} async-done(((bf16[8,128,128]{2,1,0:T(8,128)(2,1)}), bf16[8,128,128]{2,1,0:T(8,128)(2,1)S(1)}, u32[]{:S(2)}, u32[]{:S(2)}) %all-to-all-start.10) | async-done | bytes 262176 | tf_op jit(solution)/shard_map/all_to_all | solution.py:114
  220.6 23.4 %all_to_all.170 = f32[64,16,128]{2,1,0:T(8,128)S(1)} all-to-all(f32[64,16,128]{2,1,0:T(8,128)S(1)} %broadcast_select_fusion), channel_id=1, replica_groups=mesh['dp'=64,'seq'=8] {'dp'}, dimensions={0} | all-to-all | bytes 1048576 | tf_op jit(solution)/shard_map/all_to_all | solution.py:109
  244.1 3.5 %all-to-all-start.6 = ((bf16[8,128,384]{2,1,0:T(8,128)(2,1)}), bf16[8,128,384]{2,1,0:T(8,128)(2,1)S(1)}, u32[]{:S(2)}, u32[]{:S(2)}) async-start(bf16[8,128,384]{2,1,0:T(8,128)(2,1)} %bitcast.12), calls=%async_computation.6 | async-start | bytes 1572864 | tf_op jit(solution)/shard_map/all_to_all | solution.py:112
  247.6 1.4 fusion.21
  249.0 24.0 %all-to-all-done.6 = bf16[8,128,384]{2,1,0:T(8,128)(2,1)S(1)} async-done(((bf16[8,128,384]{2,1,0:T(8,128)(2,1)}), bf16[8,128,384]{2,1,0:T(8,128)(2,1)S(1)}, u32[]{:S(2)}, u32[]{:S(2)}) %all-to-all-start.6) | async-done | bytes 786464 | tf_op jit(solution)/shard_map/all_to_all | solution.py:112
  273.0 3.4 %all-to-all-start.9 = ((bf16[8,128,128]{2,1,0:T(8,128)(2,1)}), bf16[8,128,128]{2,1,0:T(8,128)(2,1)S(1)}, u32[]{:S(2)}, u32[]{:S(2)}) async-start(bf16[8,128,128]{2,1,0:T(8,128)(2,1)} %bitcast.19), calls=%async_computation.9 | async-start | bytes 524288 | tf_op jit(solution)/shard_map/all_to_all | solution.py:113
  277.8 1.2 copy.38
  279.0 10.0 %all-to-all-done.9 = bf16[8,128,128]{2,1,0:T(8,128)(2,1)S(1)} async-done(((bf16[8,128,128]{2,1,0:T(8,128)(2,1)}), bf16[8,128,128]{2,1,0:T(8,128)(2,1)S(1)}, u32[]{:S(2)}, u32[]{:S(2)}) %all-to-all-start.9) | async-done | bytes 262176 | tf_op jit(solution)/shard_map/all_to_all | solution.py:113
  (53 shorter events, 12.3 us)
Async XLA Ops:
  0.6 1.0 copy-start
  0.6 67.6 %copy-start.7 = (s32[64]{0:T(128)S(1)}, s32[64]{0:T(128)}, u32[]{:S(2)}) copy-start(s32[64]{0:T(128)} %param.15) | copy-start | bytes 772
  0.7 99.3 %copy-start.3 = (bf16[128,3072]{1,0:T(8,128)(2,1)S(1)}, bf16[128,3072]{1,0:T(8,128)(2,1)}, u32[]{:S(2)}) copy-start(bf16[128,3072]{1,0:T(8,128)(2,1)} %param.12) | copy-start | bytes 2359300
  2.3 21.7 %all-to-all-start.1 = ((bf16[128,8,128]{2,0,1:T(8,128)(2,1)}), bf16[128,8,128]{2,0,1:T(8,128)(2,1)}, u32[]{:S(2)}, u32[]{:S(2)}) async-start(bf16[128,8,128]{2,0,1:T(8,128)(2,1)} %copy_bitcast_fusion.3), calls=%async_computation.1 | async-start | bytes 524288 | tf_op jit(solution)/shard_map/all_to_all | solution.py:86
  36.8 78.2 %copy-start.6 = (s32[1,4]{1,0:T(1,128)S(1)}, s32[1,4]{1,0:T(1,128)}, u32[]{:S(2)}) copy-start(s32[1,4]{1,0:T(1,128)} %param.13) | copy-start | bytes 52
  36.8 78.4 %copy-start.5 = (s32[64,2]{0,1:T(2,128)S(1)}, s32[64,2]{0,1:T(2,128)}, u32[]{:S(2)}) copy-start(s32[64,2]{0,1:T(2,128)} %param.14) | copy-start | bytes 1540
  36.8 27.9 %all-to-all-start.2 = ((bf16[64,16,128]{2,1,0:T(8,128)(2,1)}), bf16[64,16,128]{2,1,0:T(8,128)(2,1)S(1)}, u32[]{:S(2)}, u32[]{:S(2)}) async-start(bf16[64,16,128]{2,1,0:T(8,128)(2,1)} %bitcast.3), calls=%async_computation.2 | async-start | bytes 524288 | tf_op jit(solution)/shard_map/all_to_all | solution.py:94
  64.7 28.4 %all-to-all-start = ((bf16[128,8,384]{2,0,1:T(8,128)(2,1)}), bf16[128,8,384]{2,0,1:T(8,128)(2,1)S(1)}, u32[]{:S(2)}, u32[]{:S(2)}) async-start(bf16[128,8,384]{2,0,1:T(8,128)(2,1)} %bitcast.62), calls=%async_computation | async-start | bytes 1572864 | tf_op jit(solution)/shard_map/all_to_all | solution.py:85
  93.1 18.3 %all-to-all-start.3 = ((bf16[64,16,128]{2,1,0:T(8,128)(2,1)}), bf16[64,16,128]{2,1,0:T(8,128)(2,1)S(1)}, u32[]{:S(2)}, u32[]{:S(2)}) async-start(bf16[64,16,128]{2,1,0:T(8,128)(2,1)} %broadcast_select_fusion.2), calls=%async_computation.3 | async-start | bytes 524288 | tf_op jit(solution)/shard_map/all_to_all | solution.py:98
  111.5 28.4 %all-to-all-start.4 = ((bf16[128,8,384]{2,0,1:T(8,128)(2,1)}), bf16[128,8,384]{2,0,1:T(8,128)(2,1)S(1)}, u32[]{:S(2)}, u32[]{:S(2)}) async-start(bf16[128,8,384]{2,0,1:T(8,128)(2,1)} %bitcast.61), calls=%async_computation.4 | async-start | bytes 1572864 | tf_op jit(solution)/shard_map/all_to_all | solution.py:88
  142.7 1.9 copy-start.1
  145.3 3.4 %copy-start.2 = (f32[1024,1024]{0,1:T(8,128)S(1)}, f32[1024,1024]{0,1:T(8,128)}, u32[]{:S(2)}) copy-start(f32[1024,1024]{0,1:T(8,128)} %copy-done.1) | copy-start | bytes 12582916 | tf_op jit(solution)/shard_map/while
  149.7 1.2 copy-start.4
  155.1 1.9 copy-start.1
  157.6 3.4 %copy-start.2 = (f32[1024,1024]{0,1:T(8,128)S(1)}, f32[1024,1024]{0,1:T(8,128)}, u32[]{:S(2)}) copy-start(f32[1024,1024]{0,1:T(8,128)} %copy-done.1) | copy-start | bytes 12582916 | tf_op jit(solution)/shard_map/while
  162.0 1.2 copy-start.4
  167.4 1.9 copy-start.1
  170.0 3.4 %copy-start.2 = (f32[1024,1024]{0,1:T(8,128)S(1)}, f32[1024,1024]{0,1:T(8,128)}, u32[]{:S(2)}) copy-start(f32[1024,1024]{0,1:T(8,128)} %copy-done.1) | copy-start | bytes 12582916 | tf_op jit(solution)/shard_map/while
  174.4 1.2 copy-start.4
  179.4 24.0 %all-to-all-start.7 = ((f32[64,16,128]{2,1,0:T(8,128)}), f32[64,16,128]{2,1,0:T(8,128)S(1)}, u32[]{:S(2)}, u32[]{:S(2)}) async-start(f32[64,16,128]{2,1,0:T(8,128)} %bitcast.15), calls=%async_computation.7 | async-start | bytes 1048576 | tf_op jit(solution)/shard_map/all_to_all | solution.py:105
  203.4 17.2 %all-to-all-start.10 = ((bf16[8,128,128]{2,1,0:T(8,128)(2,1)}), bf16[8,128,128]{2,1,0:T(8,128)(2,1)S(1)}, u32[]{:S(2)}, u32[]{:S(2)}) async-start(bf16[8,128,128]{2,1,0:T(8,128)(2,1)} %bitcast.22), calls=%async_computation.10 | async-start | bytes 524288 | tf_op jit(solution)/shard_map/all_to_all | solution.py:114
  244.1 28.9 %all-to-all-start.6 = ((bf16[8,128,384]{2,1,0:T(8,128)(2,1)}), bf16[8,128,384]{2,1,0:T(8,128)(2,1)S(1)}, u32[]{:S(2)}, u32[]{:S(2)}) async-start(bf16[8,128,384]{2,1,0:T(8,128)(2,1)} %bitcast.12), calls=%async_computation.6 | async-start | bytes 1572864 | tf_op jit(solution)/shard_map/all_to_all | solution.py:112
  273.0 16.0 %all-to-all-start.9 = ((bf16[8,128,128]{2,1,0:T(8,128)(2,1)}), bf16[8,128,128]{2,1,0:T(8,128)(2,1)S(1)}, u32[]{:S(2)}, u32[]{:S(2)}) async-start(bf16[8,128,128]{2,1,0:T(8,128)(2,1)} %bitcast.19), calls=%async_computation.9 | async-start | bytes 524288 | tf_op jit(solution)/shard_map/all_to_all | solution.py:113
where the time goes:
time: 291 us; the launch traced here: 290 us
  waiting for transfers between devices  137 us (47%)
  starting transfers between devices  59 us (20%)
  blocking collectives  36.2 us (12%)
  matrix products  24.8 us (9%)
  local copies, waits for them, and re-layouts  18.1 us (6%)
  other arithmetic  13.5 us (5%)
    all_to_all x1, waiting for transfers between devices, per_device(): lax.all_to_all(query_grads, 'seq', split_axis=0, concat_axis=1, tiled=True)  24 us
    all_to_all x1, blocking collectives, per_device(): lax.all_to_all(routed, 'dp', split_axis=0, concat_axis=0, tiled=True)  23.4 us
    all_to_all x1, waiting for transfers between devices, per_device(): lax.all_to_all(queries, 'seq', split_axis=1, concat_axis=0, tiled=True)  23.4 us
    all_to_all x1, waiting for transfers between devices, per_device(): lax.all_to_all(output_gradient, 'seq', split_axis=1, concat_axis=0, tiled...  21.6 us
    all_to_all x1, starting transfers between devices, per_device(): lax.all_to_all(key_side, 'dp', split_axis=0, concat_axis=0, tiled=True)  16.3 us
    all_to_all x1, waiting for transfers between devices, per_device(): lax.all_to_all(patch_grads, 'dp', split_axis=0, concat_axis=0, tiled=True)  16.3 us
    all_to_all x1, waiting for transfers between devices, per_device(): lax.all_to_all(value_low, 'seq', split_axis=0, concat_axis=1, tiled=True)  13 us
    all_to_all x1, blocking collectives, per_device(): lax.all_to_all(values, 'seq', split_axis=1, concat_axis=0, tiled=True)  12.7 us
  transfers between devices with their start and end apart: 9, of which 9 were waited for; matrix products, arithmetic and copies ran while one was open for 5% of the time, Pallas kernels for 0%

commit v1 on v0

--- a/solution.py
+++ b/solution.py
@@ -7,6 +7,7 @@
 
 KEY_VALUE_HEADS = 8
 HEAD_WIDTH = 128
+KNOCKOUT_COUNT = 2
 
 
 masked_score = -1e30
@@ -53,10 +54,8 @@
         query_grads = lax.dynamic_update_slice_in_dim(
             query_grads, query_part.astype(jnp.bfloat16), head_index * HEAD_WIDTH, 1
         )
-        key_sum = key_grads + key_part
-        key_grads = key_sum
-        value_sum = value_gradient + value_part
-        value_gradient = value_sum
+        key_grads = key_grads + key_part
+        value_gradient = value_gradient + value_part
         return (query_grads, key_grads, value_gradient)
 
     initial = (
@@ -67,53 +66,89 @@
     return lax.fori_loop(0, heads_of_query, one_head, initial)
 
 
+def route(payload, order):
+    prompt_count = lax.axis_size("dp")
+    flat = payload.reshape(prompt_count, -1)
+    spread = lax.all_to_all(flat, "dp", 0, 0, tiled=True)
+    routed = jnp.take(spread, order, axis=0)
+    back = lax.all_to_all(routed, "dp", 0, 0, tiled=True)
+    return back.reshape(payload.shape)
+
+
+def pick_heads(block, heads):
+    parts = [
+        lax.dynamic_slice_in_dim(block, heads[k] * HEAD_WIDTH, HEAD_WIDTH, 1)
+        for k in range(KNOCKOUT_COUNT)
+    ]
+    return jnp.stack(parts, axis=1)
+
+
 def per_device(queries, keys, values, output_gradient, seg_lengths, knocked, source):
     sequence_count = lax.axis_size("seq")
     prompt_count = lax.axis_size("dp")
     tok_rows = queries.shape[0]
     length = tok_rows * sequence_count
-    local_key_value = KEY_VALUE_HEADS // sequence_count
     prompt_index = lax.axis_index("dp")
-    seq_index = lax.axis_index("seq")
     prompt_ids = jnp.arange(prompt_count, dtype=jnp.int32)
     consumer = jnp.sum(
         jnp.where(source[None, :] == prompt_ids[:, None], prompt_ids[None, :], 0), axis=1
     )
     my_knock = knocked[prompt_index]
+    their_knock = knocked[consumer[prompt_index]]
+    head_ids = jnp.arange(KEY_VALUE_HEADS, dtype=jnp.int32)[None, :, None]
     visible = document_mask(seg_lengths[0], length)
-    query_side, key_side, value_side, grad_side = (
-        lax.all_to_all(queries, "seq", split_axis=1, concat_axis=0, tiled=True),
-        lax.all_to_all(keys, "seq", split_axis=1, concat_axis=0, tiled=True),
-        lax.all_to_all(values, "seq", split_axis=1, concat_axis=0, tiled=True),
-        lax.all_to_all(output_gradient, "seq", split_axis=1, concat_axis=0, tiled=True),
+
+    outgoing = pick_heads(keys, their_knock)
+    fetched = route(outgoing, source)
+    keys3 = keys.reshape(tok_rows, KEY_VALUE_HEADS, HEAD_WIDTH)
+    used3 = keys3
+    for k in range(KNOCKOUT_COUNT - 1, -1, -1):
+        used3 = jnp.where(head_ids == my_knock[k], fetched[:, k : k + 1, :], used3)
+    used_keys = used3.reshape(tok_rows, -1)
+
+    def cols(x):
+        return x.reshape(tok_rows, sequence_count, -1)
+
+    packed = jnp.concatenate(
+        [cols(queries), cols(output_gradient), cols(used_keys), cols(values)], axis=2
     )
-    local_heads = seq_index * local_key_value + jnp.arange(local_key_value, dtype=jnp.int32)
-    local_knock = jnp.any(my_knock[:, None] == local_heads[None, :], axis=0)
-    column_knock = jnp.repeat(local_knock, HEAD_WIDTH)
-    rows_each = length // prompt_count
-    spread = lax.all_to_all(key_side, "dp", split_axis=0, concat_axis=0, tiled=True)
-    routed = jnp.take(spread.reshape(prompt_count, rows_each, -1), source, axis=0).reshape(
-        length, -1
+    widths = (
+        queries.shape[1] // sequence_count,
+        output_gradient.shape[1] // sequence_count,
+        keys.shape[1] // sequence_count,
+        values.shape[1] // sequence_count,
     )
-    fetched = lax.all_to_all(routed, "dp", split_axis=0, concat_axis=0, tiled=True)
-    key_side = jnp.where(column_knock[None, :], fetched, key_side)
+    gathered = lax.all_to_all(packed, "seq", split_axis=1, concat_axis=0, tiled=True)
+    gathered = gathered.reshape(length, -1)
+    offsets = [0]
+    for w in widths:
+        offsets.append(offsets[-1] + w)
+    query_side, grad_side, key_side, value_side = (
+        gathered[:, offsets[i] : offsets[i + 1]] for i in range(4)
+    )
+
     query_grads, key_grads, value_gradient = attend_back(
         query_side, key_side, value_side, grad_side, visible
     )
-    value_low = value_gradient.astype(jnp.bfloat16)
-    patch_grads = jnp.where(column_knock[None, :], key_grads, 0.0)
-    spread = lax.all_to_all(patch_grads, "dp", split_axis=0, concat_axis=0, tiled=True)
-    routed = jnp.take(spread.reshape(prompt_count, rows_each, -1), consumer, axis=0).reshape(
-        length, -1
-    )
-    returned = lax.all_to_all(routed, "dp", split_axis=0, concat_axis=0, tiled=True)
-    key_overall = (jnp.where(column_knock[None, :], 0.0, key_grads) + returned).astype(jnp.bfloat16)
-    query_out, key_result, value_result = (
-        lax.all_to_all(query_grads, "seq", split_axis=0, concat_axis=1, tiled=True),
-        lax.all_to_all(key_overall, "seq", split_axis=0, concat_axis=1, tiled=True),
-        lax.all_to_all(value_low, "seq", split_axis=0, concat_axis=1, tiled=True),
-    )
-    return (query_out, key_result, value_result)
+
+    low = jnp.concatenate([query_grads, value_gradient.astype(jnp.bfloat16)], axis=1)
+    low_back = lax.all_to_all(low, "seq", split_axis=0, concat_axis=1, tiled=True)
+    low_back = low_back.reshape(tok_rows, sequence_count, -1)
+    query_out = low_back[:, :, : widths[0]].reshape(tok_rows, -1)
+    value_out = low_back[:, :, widths[0] :].reshape(tok_rows, -1)
+    key_back = lax.all_to_all(key_grads, "seq", split_axis=0, concat_axis=1, tiled=True)
+
+    returning = pick_heads(key_back, my_knock)
+    returned = route(returning, consumer)
+    key3 = key_back.reshape(tok_rows, KEY_VALUE_HEADS, HEAD_WIDTH)
+    own = key3
+    for k in range(KNOCKOUT_COUNT):
+        own = jnp.where(head_ids == my_knock[k], 0.0, own)
+    extra = jnp.zeros_like(key3)
+    for k in range(KNOCKOUT_COUNT):
+        extra = jnp.where(head_ids == their_knock[k], returned[:, k : k + 1, :], extra)
+    key_out = (own + extra).astype(jnp.bfloat16).reshape(tok_rows, -1)
+    return (query_out, key_out, value_out)
 
 
 def solution(mesh):

time: 291 us -> 251 us (0.86)
  the two profiles are of different devices: /device:TPU:65 before, /device:TPU:64 now
where the time goes in v1:
time: 251 us; the launch traced here: 250 us
  waiting for transfers between devices  129 us (51%)
  starting transfers between devices  46.8 us (19%)
  matrix products  30.2 us (12%)
  local copies, waits for them, and re-layouts  21.8 us (9%)
  other arithmetic  16 us (6%)
  between operations  5.59 us (2%)
    all_to_all x1, waiting for transfers between devices, per_device(): lax.all_to_all(packed, 'seq', split_axis=1, concat_axis=0, tiled=True)  53.3 us
    all_to_all x1, waiting for transfers between devices, per_device(): lax.all_to_all(low, 'seq', split_axis=0, concat_axis=1, tiled=True)  27.6 us
    all_to_all x2, starting transfers between devices, route(): spread = lax.all_to_all(flat, 'dp', 0, 0, tiled=True)  18.9 us
    all_to_all x2, waiting for transfers between devices, route(): spread = lax.all_to_all(flat, 'dp', 0, 0, tiled=True)  16.4 us
    all_to_all x2, waiting for transfers between devices, route(): back = lax.all_to_all(routed, 'dp', 0, 0, tiled=True)  16.3 us
    all_to_all x1, waiting for transfers between devices, per_device(): lax.all_to_all(key_grads, 'seq', split_axis=0, concat_axis=1, tiled=True)  15.4 us
    dot_general x3, matrix products, one_head(): jnp.einsum('ij,id->jd', probs_low, grad_rows, preferred_element_type=jnp....  12.2 us
    all_to_all x2, starting transfers between devices, route(): back = lax.all_to_all(routed, 'dp', 0, 0, tiled=True)  10.7 us
  transfers between devices with their start and end apart: 7, of which 7 were waited for; matrix products, arithmetic and copies ran while one was open for 3% of the time, Pallas kernels for 0%

profile of v1, /device:TPU:64, one launch (start us, length us, event | category | flops | bytes accessed | tf_op | source)
XLA Modules:
  0.0 249.7 jit_solution(16823457062131391346)
XLA Ops:
  0.7 0.8 select_reduce_fusion
  4.0 0.8 constant_dynamic-slice_fusion.2
  8.2 1.0 reduce.1
  9.8 12.7 %all-to-all-start = ((bf16[64,2,256]{2,1,0:T(2,128)(2,1)}), bf16[64,2,256]{2,1,0:T(2,128)(2,1)S(1)}, u32[]{:S(2)}, u32[]{:S(2)}) async-start(bf16[64,2,256]{2,1,0:T(2,128)(2,1)} %reshape.226), calls=%async_computation | async-start | bytes 131072 | tf_op jit(solution)/shard_map/all_to_all | solution.py:72
  23.3 1.6 copy_bitcast_fusion
  24.9 6.7 %all-to-all-done = bf16[64,2,256]{2,1,0:T(2,128)(2,1)S(1)} async-done(((bf16[64,2,256]{2,1,0:T(2,128)(2,1)}), bf16[64,2,256]{2,1,0:T(2,128)(2,1)S(1)}, u32[]{:S(2)}, u32[]{:S(2)}) %all-to-all-start) | async-done | bytes 65568 | tf_op jit(solution)/shard_map/all_to_all | solution.py:72
  33.9 5.5 %all-to-all-start.1 = ((bf16[64,2,256]{2,1,0:T(2,128)(2,1)}), bf16[64,2,256]{2,1,0:T(2,128)(2,1)S(1)}, u32[]{:S(2)}, u32[]{:S(2)}) async-start(bf16[64,2,256]{2,1,0:T(2,128)(2,1)} %reshape.228), calls=%async_computation.1 | async-start | bytes 131072 | tf_op jit(solution)/shard_map/all_to_all | solution.py:74
  40.7 7.8 %all-to-all-done.1 = bf16[64,2,256]{2,1,0:T(2,128)(2,1)S(1)} async-done(((bf16[64,2,256]{2,1,0:T(2,128)(2,1)}), bf16[64,2,256]{2,1,0:T(2,128)(2,1)S(1)}, u32[]{:S(2)}, u32[]{:S(2)}) %all-to-all-start.1) | async-done | bytes 65568 | tf_op jit(solution)/shard_map/all_to_all | solution.py:74
  49.3 1.7 pad_maximum_fusion
  50.9 10.0 %all-to-all-start.2 = ((bf16[128,8,1024]{2,0,1:T(8,128)(2,1)}), bf16[128,8,1024]{2,0,1:T(8,128)(2,1)S(1)}, u32[]{:S(2)}, u32[]{:S(2)}) async-start(bf16[128,8,1024]{2,0,1:T(8,128)(2,1)} %pad_maximum_fusion), calls=%async_computation.2 | async-start | bytes 4194304 | tf_op jit(solution)/shard_map/all_to_all | solution.py:121
  61.3 53.3 %all-to-all-done.2 = bf16[128,8,1024]{2,0,1:T(8,128)(2,1)S(1)} async-done(((bf16[128,8,1024]{2,0,1:T(8,128)(2,1)}), bf16[128,8,1024]{2,0,1:T(8,128)(2,1)S(1)}, u32[]{:S(2)}, u32[]{:S(2)}) %all-to-all-start.2) | async-done | bytes 2097184 | tf_op jit(solution)/shard_map/all_to_all | solution.py:121
  114.5 1.0 fusion.28
  116.4 41.8 %while.18 = (s32[]{:T(128)}, bf16[1024,384]{1,0:T(8,128)(2,1)S(1)}, f32[1024,128]{1,0:T(8,128)}, f32[1024,128]{1,0:T(8,128)}, bf16[1024,384]{1,0:T(8,128)(2,1)S(...) while((s32[]{:T(128)}, bf16[1024,384]{1,0:T(8,128)(2,1)S(1)}, ...), condition=%wide.region_7.8_spmd.clone, body=%wide.region_3.7_spmd.clone.sunk | while | flops 1364849664 | bytes 77648192 | solution.py:66
  116.4 1.9 fusion.60
  118.4 1.9 copy-done.1
  121.0 4.0 %fusion.63 = f32[1024,128]{1,0:T(8,128)} fusion(f32[1024,128]{1,0:T(8,128)} %get-tuple-element.330, pred[]{:T(512)S(6)} %compare.3, bf16[1024,384]{1,0:T(8,128)(2,1)S(1)} %copy-done.3, s32[]{:T(128)S(6)} %select_n.159, f32[1024,1024]{0,1:T(8,128)} %copy-done.1, f32[1024]{0:T(1024)S(1)} %fusion.61, f32[1024]{0:T(1024)S(1)} %get-tuple-element.311), kind=kOutput, calls=%fused_computation.13.clone.1 | convolution fusion | flops 271843328 | bytes 5513221 | tf_op jit(solution)/shard_map/while/body/eval_jaxpr/ij,id->jd/dot_general | solution.py:42
  124.9 1.0 multiply_reduce_fusion.2
  125.9 1.2 multiply_convert_fusion.2
  127.1 0.9 fusion.62
  128.0 1.6 convolution_add_fusion.2
  129.6 1.9 fusion.60
  131.5 1.9 copy-done.1
  134.1 4.1 %fusion.63 = f32[1024,128]{1,0:T(8,128)} fusion(f32[1024,128]{1,0:T(8,128)} %get-tuple-element.330, pred[]{:T(512)S(6)} %compare.3, bf16[1024,384]{1,0:T(8,128)(2,1)S(1)} %copy-done.3, s32[]{:T(128)S(6)} %select_n.159, f32[1024,1024]{0,1:T(8,128)} %copy-done.1, f32[1024]{0:T(1024)S(1)} %fusion.61, f32[1024]{0:T(1024)S(1)} %get-tuple-element.311), kind=kOutput, calls=%fused_computation.13.clone.1 | convolution fusion | flops 271843328 | bytes 5513221 | tf_op jit(solution)/shard_map/while/body/eval_jaxpr/ij,id->jd/dot_general | solution.py:42
  138.2 1.0 multiply_reduce_fusion.2
  139.2 1.2 multiply_convert_fusion.2
  140.4 0.9 fusion.62
  141.3 2.6 %convolution_add_fusion.2 = f32[1024,128]{1,0:T(8,128)} fusion(bf16[1024,1024]{0,1:T(8,128)(2,1)S(1)} %multiply_convert_fusion.2, f32[1024,128]{1,0:T(8,128)} %get-tuple-element.329, pred[]{:T(512)S(6)} %compare.3, bf16[1024,384]{1,0:T(8,128)(2,1)S(1)} %get-tuple-element.344, s32[]{:T(128)S(6)} %select_n.159), kind=kOutput, calls=%fused_computation.14.clone.1 | convolution fusion | flops 268697600 | bytes 3407877 | tf_op jit(solution)/shard_map/while/body/eval_jaxpr/ij,id->jd/dot_general | solution.py:51
  143.9 1.9 fusion.60
  145.8 1.9 copy-done.1
  148.4 4.1 %fusion.63 = f32[1024,128]{1,0:T(8,128)} fusion(f32[1024,128]{1,0:T(8,128)} %get-tuple-element.330, pred[]{:T(512)S(6)} %compare.3, bf16[1024,384]{1,0:T(8,128)(2,1)S(1)} %copy-done.3, s32[]{:T(128)S(6)} %select_n.159, f32[1024,1024]{0,1:T(8,128)} %copy-done.1, f32[1024]{0:T(1024)S(1)} %fusion.61, f32[1024]{0:T(1024)S(1)} %get-tuple-element.311), kind=kOutput, calls=%fused_computation.13.clone.1 | convolution fusion | flops 271843328 | bytes 5513221 | tf_op jit(solution)/shard_map/while/body/eval_jaxpr/ij,id->jd/dot_general | solution.py:42
  152.5 1.0 multiply_reduce_fusion.2
  153.5 1.2 multiply_convert_fusion.2
  154.7 0.9 fusion.62
  155.6 2.6 %convolution_add_fusion.2 = f32[1024,128]{1,0:T(8,128)} fusion(bf16[1024,1024]{0,1:T(8,128)(2,1)S(1)} %multiply_convert_fusion.2, f32[1024,128]{1,0:T(8,128)} %get-tuple-element.329, pred[]{:T(512)S(6)} %compare.3, bf16[1024,384]{1,0:T(8,128)(2,1)S(1)} %get-tuple-element.344, s32[]{:T(128)S(6)} %select_n.159), kind=kOutput, calls=%fused_computation.14.clone.1 | convolution fusion | flops 268697600 | bytes 3407877 | tf_op jit(solution)/shard_map/while/body/eval_jaxpr/ij,id->jd/dot_general | solution.py:51
  158.2 3.6 %all-to-all-start.4 = ((f32[8,128,128]{2,1,0:T(8,128)}), f32[8,128,128]{2,1,0:T(8,128)S(1)}, u32[]{:S(2)}, u32[]{:S(2)}) async-start(f32[8,128,128]{2,1,0:T(8,128)} %bitcast.20), calls=%async_computation.4 | async-start | bytes 1048576 | tf_op jit(solution)/shard_map/all_to_all | solution.py:139
  163.2 15.4 %all-to-all-done.4 = f32[8,128,128]{2,1,0:T(8,128)S(1)} async-done(((f32[8,128,128]{2,1,0:T(8,128)}), f32[8,128,128]{2,1,0:T(8,128)S(1)}, u32[]{:S(2)}, u32[]{:S(2)}) %all-to-all-start.4) | async-done | bytes 524320 | tf_op jit(solution)/shard_map/all_to_all | solution.py:139
  179.8 6.1 %all-to-all-start.5 = ((f32[64,1,512]{2,1,0:T(1,128)}), f32[64,1,512]{2,1,0:T(1,128)S(1)}, u32[]{:S(2)}, u32[]{:S(2)}) async-start(f32[64,1,512]{2,1,0:T(1,128)} %bitcast.27), calls=%async_computation.5 | async-start | bytes 262144 | tf_op jit(solution)/shard_map/all_to_all | solution.py:72
  186.0 9.6 %all-to-all-done.5 = f32[64,1,512]{2,1,0:T(1,128)S(1)} async-done(((f32[64,1,512]{2,1,0:T(1,128)}), f32[64,1,512]{2,1,0:T(1,128)S(1)}, u32[]{:S(2)}, u32[]{:S(2)}) %all-to-all-start.5) | async-done | bytes 131104 | tf_op jit(solution)/shard_map/all_to_all | solution.py:72
  196.4 0.8 copy.95
  197.1 5.2 %all-to-all-start.6 = ((f32[64,1,512]{2,1,0:T(1,128)}), f32[64,1,512]{2,1,0:T(1,128)S(1)}, u32[]{:S(2)}, u32[]{:S(2)}) async-start(f32[64,1,512]{2,1,0:T(1,128)} %copy.95), calls=%async_computation.6 | async-start | bytes 262144 | tf_op jit(solution)/shard_map/all_to_all | solution.py:74
  202.4 1.1 pad_maximum_fusion.1
  203.5 8.6 %all-to-all-done.6 = f32[64,1,512]{2,1,0:T(1,128)S(1)} async-done(((f32[64,1,512]{2,1,0:T(1,128)}), f32[64,1,512]{2,1,0:T(1,128)S(1)}, u32[]{:S(2)}, u32[]{:S(2)}) %all-to-all-start.6) | async-done | bytes 131104 | tf_op jit(solution)/shard_map/all_to_all | solution.py:74
  212.1 3.6 %all-to-all-start.3 = ((bf16[8,128,512]{2,1,0:T(8,128)(2,1)}), bf16[8,128,512]{2,1,0:T(8,128)(2,1)S(1)}, u32[]{:S(2)}, u32[]{:S(2)}) async-start(bf16[8,128,512]{2,1,0:T(8,128)(2,1)} %bitcast.15), calls=%async_computation.3 | async-start | bytes 2097152 | tf_op jit(solution)/shard_map/all_to_all | solution.py:135
  217.5 1.0 fusion.23
  218.5 0.9 copy.99
  219.4 27.6 %all-to-all-done.3 = bf16[8,128,512]{2,1,0:T(8,128)(2,1)S(1)} async-done(((bf16[8,128,512]{2,1,0:T(8,128)(2,1)}), bf16[8,128,512]{2,1,0:T(8,128)(2,1)S(1)}, u32[]{:S(2)}, u32[]{:S(2)}) %all-to-all-start.3) | async-done | bytes 1048608 | tf_op jit(solution)/shard_map/all_to_all | solution.py:135
  247.7 1.2 copy.98
  248.9 0.8 copy.100
  (92 shorter events, 15.8 us)
Async XLA Ops:
  0.6 22.6 %copy-start = (bf16[128,1024]{1,0:T(8,128)(2,1)S(1)}, bf16[128,1024]{1,0:T(8,128)(2,1)}, u32[]{:S(2)}) copy-start(bf16[128,1024]{1,0:T(8,128)(2,1)} %param.11) | copy-start | bytes 786436
  0.6 24.3 %copy-start.7 = (s32[64]{0:T(128)S(1)}, s32[64]{0:T(128)}, u32[]{:S(2)}) copy-start(s32[64]{0:T(128)} %param.15) | copy-start | bytes 772
  0.7 48.4 %copy-start.5 = (bf16[128,1024]{1,0:T(8,128)(2,1)S(1)}, bf16[128,1024]{1,0:T(8,128)(2,1)}, u32[]{:S(2)}) copy-start(bf16[128,1024]{1,0:T(8,128)(2,1)} %param.10) | copy-start | bytes 786436
  9.8 21.9 %all-to-all-start = ((bf16[64,2,256]{2,1,0:T(2,128)(2,1)}), bf16[64,2,256]{2,1,0:T(2,128)(2,1)S(1)}, u32[]{:S(2)}, u32[]{:S(2)}) async-start(bf16[64,2,256]{2,1,0:T(2,128)(2,1)} %reshape.226), calls=%async_computation | async-start | bytes 131072 | tf_op jit(solution)/shard_map/all_to_all | solution.py:72
  33.9 14.6 %all-to-all-start.1 = ((bf16[64,2,256]{2,1,0:T(2,128)(2,1)}), bf16[64,2,256]{2,1,0:T(2,128)(2,1)S(1)}, u32[]{:S(2)}, u32[]{:S(2)}) async-start(bf16[64,2,256]{2,1,0:T(2,128)(2,1)} %reshape.228), calls=%async_computation.1 | async-start | bytes 131072 | tf_op jit(solution)/shard_map/all_to_all | solution.py:74
  49.3 11.7 %copy-start.8 = (s32[1,4]{1,0:T(1,128)S(1)}, s32[1,4]{1,0:T(1,128)}, u32[]{:S(2)}) copy-start(s32[1,4]{1,0:T(1,128)} %param.13) | copy-start | bytes 52
  50.9 63.6 %all-to-all-start.2 = ((bf16[128,8,1024]{2,0,1:T(8,128)(2,1)}), bf16[128,8,1024]{2,0,1:T(8,128)(2,1)S(1)}, u32[]{:S(2)}, u32[]{:S(2)}) async-start(bf16[128,8,1024]{2,0,1:T(8,128)(2,1)} %pad_maximum_fusion), calls=%async_computation.2 | async-start | bytes 4194304 | tf_op jit(solution)/shard_map/all_to_all | solution.py:121
  116.4 4.5 %copy-start.3 = (bf16[1024,384]{1,0:T(8,128)(2,1)S(1)}, bf16[1024,384]{1,0:T(8,128)(2,1)}, u32[]{:S(2)}) copy-start(bf16[1024,384]{1,0:T(8,128)(2,1)} %get-tuple-element.346) | copy-start | bytes 2359300 | tf_op jit(solution)/shard_map/while
  118.4 1.9 copy-start.1
  120.9 4.0 %copy-start.2 = (f32[1024,1024]{0,1:T(8,128)S(1)}, f32[1024,1024]{0,1:T(8,128)}, u32[]{:S(2)}) copy-start(f32[1024,1024]{0,1:T(8,128)} %copy-done.1) | copy-start | bytes 12582916 | tf_op jit(solution)/shard_map/while
  125.9 1.2 copy-start.6
  129.6 4.5 %copy-start.3 = (bf16[1024,384]{1,0:T(8,128)(2,1)S(1)}, bf16[1024,384]{1,0:T(8,128)(2,1)}, u32[]{:S(2)}) copy-start(bf16[1024,384]{1,0:T(8,128)(2,1)} %get-tuple-element.346) | copy-start | bytes 2359300 | tf_op jit(solution)/shard_map/while
  131.5 1.9 copy-start.1
  134.1 4.1 %copy-start.2 = (f32[1024,1024]{0,1:T(8,128)S(1)}, f32[1024,1024]{0,1:T(8,128)}, u32[]{:S(2)}) copy-start(f32[1024,1024]{0,1:T(8,128)} %copy-done.1) | copy-start | bytes 12582916 | tf_op jit(solution)/shard_map/while
  139.2 1.2 copy-start.6
  143.9 4.5 %copy-start.3 = (bf16[1024,384]{1,0:T(8,128)(2,1)S(1)}, bf16[1024,384]{1,0:T(8,128)(2,1)}, u32[]{:S(2)}) copy-start(bf16[1024,384]{1,0:T(8,128)(2,1)} %get-tuple-element.346) | copy-start | bytes 2359300 | tf_op jit(solution)/shard_map/while
  145.8 1.9 copy-start.1
  148.4 4.1 %copy-start.2 = (f32[1024,1024]{0,1:T(8,128)S(1)}, f32[1024,1024]{0,1:T(8,128)}, u32[]{:S(2)}) copy-start(f32[1024,1024]{0,1:T(8,128)} %copy-done.1) | copy-start | bytes 12582916 | tf_op jit(solution)/shard_map/while
  153.5 1.2 copy-start.6
  158.2 44.2 %copy-start.4 = (f32[1024,128]{1,0:T(8,128)S(1)}, f32[1024,128]{1,0:T(8,128)}, u32[]{:S(2)}) copy-start(f32[1024,128]{1,0:T(8,128)} %get-tuple-element.160) | copy-start | bytes 1572868
  158.2 20.4 %all-to-all-start.4 = ((f32[8,128,128]{2,1,0:T(8,128)}), f32[8,128,128]{2,1,0:T(8,128)S(1)}, u32[]{:S(2)}, u32[]{:S(2)}) async-start(f32[8,128,128]{2,1,0:T(8,128)} %bitcast.20), calls=%async_computation.4 | async-start | bytes 1048576 | tf_op jit(solution)/shard_map/all_to_all | solution.py:139
  179.8 15.8 %all-to-all-start.5 = ((f32[64,1,512]{2,1,0:T(1,128)}), f32[64,1,512]{2,1,0:T(1,128)S(1)}, u32[]{:S(2)}, u32[]{:S(2)}) async-start(f32[64,1,512]{2,1,0:T(1,128)} %bitcast.27), calls=%async_computation.5 | async-start | bytes 262144 | tf_op jit(solution)/shard_map/all_to_all | solution.py:72
  197.1 14.9 %all-to-all-start.6 = ((f32[64,1,512]{2,1,0:T(1,128)}), f32[64,1,512]{2,1,0:T(1,128)S(1)}, u32[]{:S(2)}, u32[]{:S(2)}) async-start(f32[64,1,512]{2,1,0:T(1,128)} %copy.95), calls=%async_computation.6 | async-start | bytes 262144 | tf_op jit(solution)/shard_map/all_to_all | solution.py:74
  212.1 34.9 %all-to-all-start.3 = ((bf16[8,128,512]{2,1,0:T(8,128)(2,1)}), bf16[8,128,512]{2,1,0:T(8,128)(2,1)S(1)}, u32[]{:S(2)}, u32[]{:S(2)}) async-start(bf16[8,128,512]{2,1,0:T(8,128)(2,1)} %bitcast.15), calls=%async_computation.3 | async-start | bytes 2097152 | tf_op jit(solution)/shard_map/all_to_all | solution.py:135

commit v2 on v1

--- a/solution.py
+++ b/solution.py
@@ -13,12 +13,36 @@
 masked_score = -1e30
 
 
-def document_mask(lengths, length):
+def document_mask(lengths, position):
     doc_ends = jnp.cumsum(lengths)
-    position = jnp.arange(length, dtype=jnp.int32)
     segment = jnp.sum((position[:, None] >= doc_ends[None, :]).astype(jnp.int32), axis=1)
     causal = position[:, None] >= position[None, :]
     return jnp.logical_and(causal, segment[:, None] == segment[None, :])
+
+
+def seq_send(blocks, axis, by_destination=True):
+    count = lax.axis_size("seq")
+    me = lax.axis_index("seq")
+    received = []
+    for k in range(count):
+        index = me ^ k if by_destination else k
+        part = lax.dynamic_index_in_dim(blocks, index, axis, keepdims=True)
+        if k == 0:
+            received.append(part)
+            continue
+        pairs = [(d, d ^ k) for d in range(count)]
+        received.append(lax.ppermute(part, "seq", pairs))
+    return jnp.concatenate(received, axis=axis)
+
+
+def seq_place(received, axis):
+    count = lax.axis_size("seq")
+    me = lax.axis_index("seq")
+    out = jnp.zeros_like(received)
+    for k in range(count):
+        part = lax.dynamic_index_in_dim(received, k, axis, keepdims=True)
+        out = lax.dynamic_update_index_in_dim(out, part, me ^ k, axis)
+    return out
 
 
 def attend_back(query_side, key_side, value_side, grad_side, visible):
@@ -96,7 +120,6 @@
     my_knock = knocked[prompt_index]
     their_knock = knocked[consumer[prompt_index]]
     head_ids = jnp.arange(KEY_VALUE_HEADS, dtype=jnp.int32)[None, :, None]
-    visible = document_mask(seg_lengths[0], length)
 
     outgoing = pick_heads(keys, their_knock)
     fetched = route(outgoing, source)
@@ -109,34 +132,34 @@
     def cols(x):
         return x.reshape(tok_rows, sequence_count, -1)
 
-    packed = jnp.concatenate(
-        [cols(queries), cols(output_gradient), cols(used_keys), cols(values)], axis=2
-    )
-    widths = (
-        queries.shape[1] // sequence_count,
-        output_gradient.shape[1] // sequence_count,
-        keys.shape[1] // sequence_count,
-        values.shape[1] // sequence_count,
-    )
-    gathered = lax.all_to_all(packed, "seq", split_axis=1, concat_axis=0, tiled=True)
-    gathered = gathered.reshape(length, -1)
-    offsets = [0]
-    for w in widths:
-        offsets.append(offsets[-1] + w)
-    query_side, grad_side, key_side, value_side = (
-        gathered[:, offsets[i] : offsets[i + 1]] for i in range(4)
-    )
+    seq_index = lax.axis_index("seq")
+    packed = jnp.concatenate([cols(queries), cols(output_gradient), cols(values)], axis=2)
+    q_width = queries.shape[1] // sequence_count
+    g_width = output_gradient.shape[1] // sequence_count
+    gathered = seq_send(packed, 1)
+    gathered = jnp.swapaxes(gathered, 0, 1).reshape(length, -1)
+    query_side = gathered[:, :q_width]
+    grad_side = gathered[:, q_width : q_width + g_width]
+    value_side = gathered[:, q_width + g_width :]
+    key_side = seq_send(cols(used_keys), 1)
+    key_side = jnp.swapaxes(key_side, 0, 1).reshape(length, -1)
+
+    rows = jnp.arange(length, dtype=jnp.int32)
+    position = ((rows // tok_rows) ^ seq_index) * tok_rows + rows % tok_rows
+    visible = document_mask(seg_lengths[0], position)
 
     query_grads, key_grads, value_gradient = attend_back(
         query_side, key_side, value_side, grad_side, visible
     )
 
     low = jnp.concatenate([query_grads, value_gradient.astype(jnp.bfloat16)], axis=1)
-    low_back = lax.all_to_all(low, "seq", split_axis=0, concat_axis=1, tiled=True)
-    low_back = low_back.reshape(tok_rows, sequence_count, -1)
-    query_out = low_back[:, :, : widths[0]].reshape(tok_rows, -1)
-    value_out = low_back[:, :, widths[0] :].reshape(tok_rows, -1)
-    key_back = lax.all_to_all(key_grads, "seq", split_axis=0, concat_axis=1, tiled=True)
+    low = low.reshape(sequence_count, tok_rows, -1)
+    low_back = seq_place(seq_send(low, 0, False), 0)
+    low_back = jnp.swapaxes(low_back, 0, 1)
+    query_out = low_back[:, :, :q_width].reshape(tok_rows, -1)
+    value_out = low_back[:, :, q_width:].reshape(tok_rows, -1)
+    key_back = seq_place(seq_send(key_grads.reshape(sequence_count, tok_rows, -1), 0, False), 0)
+    key_back = jnp.swapaxes(key_back, 0, 1).reshape(tok_rows, -1)
 
     returning = pick_heads(key_back, my_knock)
     returned = route(returning, consumer)

time: 251 us -> 291 us (1.16)
  the two profiles are of different devices: /device:TPU:64 before, /device:TPU:1 now
where the time goes in v2:
time: 291 us; the launch traced here: 289 us
  starting transfers between devices  172 us (59%)
  local copies, waits for them, and re-layouts  61.8 us (21%)
  matrix products  26.8 us (9%)
  other arithmetic  12.5 us (4%)
  waiting for transfers between devices  9.32 us (3%)
  between operations  6.24 us (2%)
    ppermute x28, starting transfers between devices, seq_send(): received.append(lax.ppermute(part, 'seq', pairs))  123 us
    all_to_all x2, starting transfers between devices, route(): spread = lax.all_to_all(flat, 'dp', 0, 0, tiled=True)  30.5 us
    dynamic_update_slice x16, local copies, waits for them, and re-layouts, seq_place(): out = lax.dynamic_update_index_in_dim(out, part, me ^ k, axis)  29.8 us
    all_to_all x2, starting transfers between devices, route(): back = lax.all_to_all(routed, 'dp', 0, 0, tiled=True)  18.1 us
    dot_general x3, matrix products, one_head(): jnp.einsum('ij,id->jd', probs_low, grad_rows, preferred_element_type=jnp....  12.2 us
    unnamed x33, local copies, waits for them, and re-layouts  9.79 us
    dot_general x3, matrix products, one_head(): jnp.einsum('id,jd->ij', query_rows, key_side, preferred_element_type=jnp....  6.71 us
    while x18, local copies, waits for them, and re-layouts  5.9 us
  transfers between devices with their start and end apart: 32, of which 3 were waited for; matrix products, arithmetic and copies ran while one was open for 18% of the time, Pallas kernels for 0%

profile of v2, /device:TPU:1, one launch (start us, length us, event | category | flops | bytes accessed | tf_op | source)
XLA Modules:
  0.0 288.8 jit_solution(6904869375826655090)
XLA Ops:
  9.9 14.6 %all-to-all-start = ((bf16[64,2,256]{2,1,0:T(2,128)(2,1)}), bf16[64,2,256]{2,1,0:T(2,128)(2,1)S(1)}, u32[]{:S(2)}, u32[]{:S(2)}) async-start(bf16[64,2,256]{2,1,0:T(2,128)(2,1)} %reshape.280), calls=%async_computation | async-start | bytes 131072 | tf_op jit(solution)/shard_map/all_to_all | solution.py:96
  27.3 7.9 %collective-permute-start = (bf16[128,1,896]{2,0,1:T(8,128)(2,1)}, bf16[128,1,896]{2,0,1:T(8,128)(2,1)S(1)}, u32[]{:S(2)}, u32[]{:S(2)}) collective-permute-start(bf16[128,1,896]{2,0,1:T(8,128)(2,1)} %get-tuple-element.231), channel_id=1, source_target_pairs={{0,1},{1,0},{2,3},{3,2},{4,5},{5,4},{6,7},{7,6},{8,9},{9,8},{10,11... | collective-permute-start | bytes 688136 | tf_op jit(solution)/shard_map/ppermute | solution.py:34
  35.2 3.1 %collective-permute-start.1 = (bf16[128,1,896]{2,0,1:T(8,128)(2,1)}, bf16[128,1,896]{2,0,1:T(8,128)(2,1)S(1)}, u32[]{:S(2)}, u32[]{:S(2)}) collective-permute-start(bf16[128,1,896]{2,0,1:T(8,128)(2,1)} %get-tuple-element.230), channel_id=1, source_target_pairs={{0,2},{1,3},{2,0},{3,1},{4,6},{5,7},{6,4},{7,5},{8,10},{9,11},{10,... | collective-permute-start | bytes 688136 | tf_op jit(solution)/shard_map/ppermute | solution.py:34
  40.3 4.6 %collective-permute-start.3 = (bf16[128,1,896]{2,0,1:T(8,128)(2,1)}, bf16[128,1,896]{2,0,1:T(8,128)(2,1)S(1)}, u32[]{:S(2)}, u32[]{:S(2)}) collective-permute-start(bf16[128,1,896]{2,0,1:T(8,128)(2,1)} %get-tuple-element.228), channel_id=1, source_target_pairs={{0,4},{1,5},{2,6},{3,7},{4,0},{5,1},{6,2},{7,3},{8,12},{9,13},{10,... | collective-permute-start | bytes 688136 | tf_op jit(solution)/shard_map/ppermute | solution.py:34
  44.9 7.2 %collective-permute-start.4 = (bf16[128,1,896]{2,0,1:T(8,128)(2,1)}, bf16[128,1,896]{2,0,1:T(8,128)(2,1)S(1)}, u32[]{:S(2)}, u32[]{:S(2)}) collective-permute-start(bf16[128,1,896]{2,0,1:T(8,128)(2,1)} %get-tuple-element.227), channel_id=1, source_target_pairs={{0,5},{1,4},{2,7},{3,6},{4,1},{5,0},{6,3},{7,2},{8,13},{9,12},{10,... | collective-permute-start | bytes 688136 | tf_op jit(solution)/shard_map/ppermute | solution.py:34
  55.9 12.1 %all-to-all-start.1 = ((bf16[64,2,256]{2,1,0:T(2,128)(2,1)}), bf16[64,2,256]{2,1,0:T(2,128)(2,1)S(1)}, u32[]{:S(2)}, u32[]{:S(2)}) async-start(bf16[64,2,256]{2,1,0:T(2,128)(2,1)} %reshape.282), calls=%async_computation.1 | async-start | bytes 131072 | tf_op jit(solution)/shard_map/all_to_all | solution.py:98
  68.1 4.4 %collective-permute-start.5 = (bf16[128,1,896]{2,0,1:T(8,128)(2,1)}, bf16[128,1,896]{2,0,1:T(8,128)(2,1)S(1)}, u32[]{:S(2)}, u32[]{:S(2)}) collective-permute-start(bf16[128,1,896]{2,0,1:T(8,128)(2,1)} %get-tuple-element.226), channel_id=1, source_target_pairs={{0,6},{1,7},{2,4},{3,5},{4,2},{5,3},{6,0},{7,1},{8,14},{9,15},{10,... | collective-permute-start | bytes 688136 | tf_op jit(solution)/shard_map/ppermute | solution.py:34
  80.3 3.7 %collective-permute-start.10 = (bf16[128,1,128]{2,1,0:T(2,128)(2,1)S(1)}, bf16[128,1,128]{2,1,0:T(2,128)(2,1)S(1)}, u32[]{:S(2)}, u32[]{:S(2)}) collective-permute-start(bf16[128,1,128]{2,1,0:T(2,128)(2,1)S(1)} %get-tuple-element.254), channel_id=1, source_target_pairs={{0,4},{1,5},{2,6},{3,7},{4,0},{5,1},{6,2},{7,3},{8,12},{9,13},{10,... | collective-permute-start | bytes 98312 | tf_op jit(solution)/shard_map/ppermute | solution.py:34
  84.1 7.7 %collective-permute-start.11 = (bf16[128,1,128]{2,1,0:T(2,128)(2,1)S(1)}, bf16[128,1,128]{2,1,0:T(2,128)(2,1)S(1)}, u32[]{:S(2)}, u32[]{:S(2)}) collective-permute-start(bf16[128,1,128]{2,1,0:T(2,128)(2,1)S(1)} %get-tuple-element.253), channel_id=1, source_target_pairs={{0,5},{1,4},{2,7},{3,6},{4,1},{5,0},{6,3},{7,2},{8,13},{9,12},{10,... | collective-permute-start | bytes 98312 | tf_op jit(solution)/shard_map/ppermute | solution.py:34
  92.5 4.4 %collective-permute-start.12 = (bf16[128,1,128]{2,1,0:T(2,128)(2,1)S(1)}, bf16[128,1,128]{2,1,0:T(2,128)(2,1)S(1)}, u32[]{:S(2)}, u32[]{:S(2)}) collective-permute-start(bf16[128,1,128]{2,1,0:T(2,128)(2,1)S(1)} %get-tuple-element.252), channel_id=1, source_target_pairs={{0,6},{1,7},{2,4},{3,5},{4,2},{5,3},{6,0},{7,1},{8,14},{9,15},{10,... | collective-permute-start | bytes 98312 | tf_op jit(solution)/shard_map/ppermute | solution.py:34
  96.9 2.2 collective-permute-start.13
  99.2 6.9 %collective-permute-start.7 = (bf16[128,1,128]{2,1,0:T(2,128)(2,1)S(1)}, bf16[128,1,128]{2,1,0:T(2,128)(2,1)S(1)}, u32[]{:S(2)}, u32[]{:S(2)}) collective-permute-start(bf16[128,1,128]{2,1,0:T(2,128)(2,1)S(1)} %get-tuple-element.257), channel_id=1, source_target_pairs={{0,1},{1,0},{2,3},{3,2},{4,5},{5,4},{6,7},{7,6},{8,9},{9,8},{10,11... | collective-permute-start | bytes 98312 | tf_op jit(solution)/shard_map/ppermute | solution.py:34
  108.0 3.7 %collective-permute-start.9 = (bf16[128,1,128]{2,1,0:T(2,128)(2,1)S(1)}, bf16[128,1,128]{2,1,0:T(2,128)(2,1)S(1)}, u32[]{:S(2)}, u32[]{:S(2)}) collective-permute-start(bf16[128,1,128]{2,1,0:T(2,128)(2,1)S(1)} %get-tuple-element.255), channel_id=1, source_target_pairs={{0,3},{1,2},{2,1},{3,0},{4,7},{5,6},{6,5},{7,4},{8,11},{9,10},{10,... | collective-permute-start | bytes 98312 | tf_op jit(solution)/shard_map/ppermute | solution.py:34
  114.2 3.6 %collective-permute-done.9 = bf16[128,1,128]{2,1,0:T(2,128)(2,1)S(1)} collective-permute-done((bf16[128,1,128]{2,1,0:T(2,128)(2,1)S(1)}, bf16[128,1,128]{2,1,0:T(2,128)(2,1)S(1)}, u32[]{:S(2)}, u32[]{:S(2)}) %collective-permute-start.9) | collective-permute-done | bytes 32800 | tf_op jit(solution)/shard_map/ppermute | solution.py:34
  119.5 38.4 %while.18 = (s32[]{:T(128)}, bf16[1024,384]{1,0:T(8,128)(2,1)S(1)}, f32[1024,128]{1,0:T(8,128)S(1)}, f32[1024,128]{1,0:T(8,128)}, bf16[1024,384]{1,0:T(8,128)(2,...) while((s32[]{:T(128)}, bf16[1024,384]{1,0:T(8,128)(2,1)S(1)}, ...), condition=%wide.region_7.8_spmd.clone, body=%wide.region_3.7_spmd.clone.sunk | while | flops 1364849664 | bytes 74510632 | solution.py:90
  119.5 2.2 fusion.82
  121.7 2.0 copy-done.1
  124.3 4.0 %fusion.85 = f32[1024,128]{1,0:T(8,128)} fusion(f32[1024,128]{1,0:T(8,128)} %get-tuple-element.359, pred[]{:T(512)S(6)} %compare.11, bf16[1024,384]{1,0:T(8,128)(2,1)S(1)} %get-tuple-element.376, s32[]{:T(128)S(6)} %select_n.289, f32[1024,1024]{0,1:T(8,128)} %copy-done.1, f32[1024]{0:T(1024)S(1)} %fusion.83, f32[1024]{0:T(1024)S(1)} %get-tuple-element.339), kind=kOutput, calls=%fused_computation.11.clone.1 | convolution fusion | flops 271843328 | bytes 5513221 | tf_op jit(solution)/shard_map/while/body/eval_jaxpr/ij,id->jd/dot_general | solution.py:66
  132.2 2.2 fusion.82
  134.5 2.0 copy-done.1
  137.1 4.1 %fusion.85 = f32[1024,128]{1,0:T(8,128)} fusion(f32[1024,128]{1,0:T(8,128)} %get-tuple-element.359, pred[]{:T(512)S(6)} %compare.11, bf16[1024,384]{1,0:T(8,128)(2,1)S(1)} %get-tuple-element.376, s32[]{:T(128)S(6)} %select_n.289, f32[1024,1024]{0,1:T(8,128)} %copy-done.1, f32[1024]{0:T(1024)S(1)} %fusion.83, f32[1024]{0:T(1024)S(1)} %get-tuple-element.339), kind=kOutput, calls=%fused_computation.11.clone.1 | convolution fusion | flops 271843328 | bytes 5513221 | tf_op jit(solution)/shard_map/while/body/eval_jaxpr/ij,id->jd/dot_general | solution.py:66
  145.1 2.2 fusion.82
  149.9 4.1 %fusion.85 = f32[1024,128]{1,0:T(8,128)} fusion(f32[1024,128]{1,0:T(8,128)} %get-tuple-element.359, pred[]{:T(512)S(6)} %compare.11, bf16[1024,384]{1,0:T(8,128)(2,1)S(1)} %get-tuple-element.376, s32[]{:T(128)S(6)} %select_n.289, f32[1024,1024]{0,1:T(8,128)} %copy-done.1, f32[1024]{0:T(1024)S(1)} %fusion.83, f32[1024]{0:T(1024)S(1)} %get-tuple-element.339), kind=kOutput, calls=%fused_computation.11.clone.1 | convolution fusion | flops 271843328 | bytes 5513221 | tf_op jit(solution)/shard_map/while/body/eval_jaxpr/ij,id->jd/dot_general | solution.py:66
  158.0 3.4 %collective-permute-start.21 = (f32[1,128,128]{2,1,0:T(8,128)S(1)}, f32[1,128,128]{2,1,0:T(8,128)S(1)}, u32[]{:S(2)}, u32[]{:S(2)}) collective-permute-start(f32[1,128,128]{2,1,0:T(8,128)S(1)} %get-tuple-element.248), channel_id=1, source_target_pairs={{0,1},{1,0},{2,3},{3,2},{4,5},{5,4},{6,7},{7,6},{8,9},{9,8},{10,11... | collective-permute-start | bytes 196616 | tf_op jit(solution)/shard_map/ppermute | solution.py:34
  161.4 2.4 collective-permute-start.22
  163.8 6.6 %collective-permute-start.23 = (f32[1,128,128]{2,1,0:T(8,128)S(1)}, f32[1,128,128]{2,1,0:T(8,128)S(1)}, u32[]{:S(2)}, u32[]{:S(2)}) collective-permute-start(f32[1,128,128]{2,1,0:T(8,128)S(1)} %get-tuple-element.246), channel_id=1, source_target_pairs={{0,3},{1,2},{2,1},{3,0},{4,7},{5,6},{6,5},{7,4},{8,11},{9,10},{10,... | collective-permute-start | bytes 196616 | tf_op jit(solution)/shard_map/ppermute | solution.py:34
  170.4 5.6 %collective-permute-start.24 = (f32[1,128,128]{2,1,0:T(8,128)S(1)}, f32[1,128,128]{2,1,0:T(8,128)S(1)}, u32[]{:S(2)}, u32[]{:S(2)}) collective-permute-start(f32[1,128,128]{2,1,0:T(8,128)S(1)} %get-tuple-element.245), channel_id=1, source_target_pairs={{0,4},{1,5},{2,6},{3,7},{4,0},{5,1},{6,2},{7,3},{8,12},{9,13},{10,... | collective-permute-start | bytes 196616 | tf_op jit(solution)/shard_map/ppermute | solution.py:34
  176.0 2.3 collective-permute-start.25
  178.3 4.4 %collective-permute-start.26 = (f32[1,128,128]{2,1,0:T(8,128)S(1)}, f32[1,128,128]{2,1,0:T(8,128)S(1)}, u32[]{:S(2)}, u32[]{:S(2)}) collective-permute-start(f32[1,128,128]{2,1,0:T(8,128)S(1)} %get-tuple-element.250), channel_id=1, source_target_pairs={{0,6},{1,7},{2,4},{3,5},{4,2},{5,3},{6,0},{7,1},{8,14},{9,15},{10,... | collective-permute-start | bytes 196616 | tf_op jit(solution)/shard_map/ppermute | solution.py:34
  182.7 6.5 %collective-permute-start.27 = (f32[1,128,128]{2,1,0:T(8,128)S(1)}, f32[1,128,128]{2,1,0:T(8,128)S(1)}, u32[]{:S(2)}, u32[]{:S(2)}) collective-permute-start(f32[1,128,128]{2,1,0:T(8,128)S(1)} %get-tuple-element.243), channel_id=1, source_target_pairs={{0,7},{1,6},{2,5},{3,4},{4,3},{5,2},{6,1},{7,0},{8,15},{9,14},{10,... | collective-permute-start | bytes 196616 | tf_op jit(solution)/shard_map/ppermute | solution.py:34
  203.1 16.0 %all-to-all-start.2 = ((f32[64,1,512]{2,1,0:T(1,128)}), f32[64,1,512]{2,1,0:T(1,128)S(1)}, u32[]{:S(2)}, u32[]{:S(2)}) async-start(f32[64,1,512]{2,1,0:T(1,128)} %bitcast.43), calls=%async_computation.2 | async-start | bytes 262144 | tf_op jit(solution)/shard_map/all_to_all | solution.py:96
  219.2 2.6 collective-permute-start.14
  221.8 2.0 collective-permute-start.15
  223.8 5.4 %all-to-all-done.2 = f32[64,1,512]{2,1,0:T(1,128)S(1)} async-done(((f32[64,1,512]{2,1,0:T(1,128)}), f32[64,1,512]{2,1,0:T(1,128)S(1)}, u32[]{:S(2)}, u32[]{:S(2)}) %all-to-all-start.2) | async-done | bytes 131104 | tf_op jit(solution)/shard_map/all_to_all | solution.py:96
  230.7 6.0 %all-to-all-start.3 = ((f32[64,1,512]{2,1,0:T(1,128)}), f32[64,1,512]{2,1,0:T(1,128)S(1)}, u32[]{:S(2)}, u32[]{:S(2)}) async-start(f32[64,1,512]{2,1,0:T(1,128)} %copy.122), calls=%async_computation.3 | async-start | bytes 262144 | tf_op jit(solution)/shard_map/all_to_all | solution.py:98
  236.7 7.7 %collective-permute-start.16 = (bf16[1,128,512]{2,1,0:T(8,128)(2,1)S(1)}, bf16[1,128,512]{2,1,0:T(8,128)(2,1)}, u32[]{:S(2)}, u32[]{:S(2)}) collective-permute-start(bf16[1,128,512]{2,1,0:T(8,128)(2,1)S(1)} %get-tuple-element.237), channel_id=1, source_target_pairs={{0,3},{1,2},{2,1},{3,0},{4,7},{5,6},{6,5},{7,4},{8,11},{9,10},{10,... | collective-permute-start | bytes 393224 | tf_op jit(solution)/shard_map/ppermute | solution.py:34
  244.4 3.9 %collective-permute-start.17 = (bf16[1,128,512]{2,1,0:T(8,128)(2,1)S(1)}, bf16[1,128,512]{2,1,0:T(8,128)(2,1)}, u32[]{:S(2)}, u32[]{:S(2)}) collective-permute-start(bf16[1,128,512]{2,1,0:T(8,128)(2,1)S(1)} %get-tuple-element.238), channel_id=1, source_target_pairs={{0,4},{1,5},{2,6},{3,7},{4,0},{5,1},{6,2},{7,3},{8,12},{9,13},{10,... | collective-permute-start | bytes 393224 | tf_op jit(solution)/shard_map/ppermute | solution.py:34
  248.3 3.3 %collective-permute-start.18 = (bf16[1,128,512]{2,1,0:T(8,128)(2,1)S(1)}, bf16[1,128,512]{2,1,0:T(8,128)(2,1)S(1)}, u32[]{:S(2)}, u32[]{:S(2)}) collective-permute-start(bf16[1,128,512]{2,1,0:T(8,128)(2,1)S(1)} %get-tuple-element.239), channel_id=1, source_target_pairs={{0,5},{1,4},{2,7},{3,6},{4,1},{5,0},{6,3},{7,2},{8,13},{9,12},{10,... | collective-permute-start | bytes 393224 | tf_op jit(solution)/shard_map/ppermute | solution.py:34
  251.6 4.0 %collective-permute-start.19 = (bf16[1,128,512]{2,1,0:T(8,128)(2,1)S(1)}, bf16[1,128,512]{2,1,0:T(8,128)(2,1)S(1)}, u32[]{:S(2)}, u32[]{:S(2)}) collective-permute-start(bf16[1,128,512]{2,1,0:T(8,128)(2,1)S(1)} %get-tuple-element.240), channel_id=1, source_target_pairs={{0,6},{1,7},{2,4},{3,5},{4,2},{5,3},{6,0},{7,1},{8,14},{9,15},{10,... | collective-permute-start | bytes 393224 | tf_op jit(solution)/shard_map/ppermute | solution.py:34
  255.6 6.9 %collective-permute-start.20 = (bf16[1,128,512]{2,1,0:T(8,128)(2,1)S(1)}, bf16[1,128,512]{2,1,0:T(8,128)(2,1)S(1)}, u32[]{:S(2)}, u32[]{:S(2)}) collective-permute-start(bf16[1,128,512]{2,1,0:T(8,128)(2,1)S(1)} %get-tuple-element.233), channel_id=1, source_target_pairs={{0,7},{1,6},{2,5},{3,4},{4,3},{5,2},{6,1},{7,0},{8,15},{9,14},{10,... | collective-permute-start | bytes 393224 | tf_op jit(solution)/shard_map/ppermute | solution.py:34
  264.1 2.3 dynamic_update_slice.57
  266.6 2.3 dynamic_update_slice.58
  269.2 2.3 dynamic_update_slice.59
  272.6 2.3 dynamic_update_slice.60
  276.0 2.3 dynamic_update_slice.61
  278.5 2.3 dynamic_update_slice.62
  281.0 2.3 dynamic_update_slice.63
  283.6 2.3 dynamic_update_slice.64
  (168 shorter events, 66.1 us)
Async XLA Ops:
  0.6 25.3 %copy-start = (bf16[128,1024]{1,0:T(8,128)(2,1)S(1)}, bf16[128,1024]{1,0:T(8,128)(2,1)}, u32[]{:S(2)}) copy-start(bf16[128,1024]{1,0:T(8,128)(2,1)} %param.11) | copy-start | bytes 786436
  0.6 25.1 %copy-start.3 = (bf16[128,3072]{1,0:T(8,128)(2,1)S(1)}, bf16[128,3072]{1,0:T(8,128)(2,1)}, u32[]{:S(2)}) copy-start(bf16[128,3072]{1,0:T(8,128)(2,1)} %param.12) | copy-start | bytes 2359300
  9.9 43.9 %all-to-all-start = ((bf16[64,2,256]{2,1,0:T(2,128)(2,1)}), bf16[64,2,256]{2,1,0:T(2,128)(2,1)S(1)}, u32[]{:S(2)}, u32[]{:S(2)}) async-start(bf16[64,2,256]{2,1,0:T(2,128)(2,1)} %reshape.280), calls=%async_computation | async-start | bytes 131072 | tf_op jit(solution)/shard_map/all_to_all | solution.py:96
  26.0 26.2 %copy-start.7 = (s32[64]{0:T(128)S(1)}, s32[64]{0:T(128)}, u32[]{:S(2)}) copy-start(s32[64]{0:T(128)} %param.15) | copy-start | bytes 772
  26.0 26.2 %copy-start.8 = (s32[1,4]{1,0:T(1,128)S(1)}, s32[1,4]{1,0:T(1,128)}, u32[]{:S(2)}) copy-start(s32[1,4]{1,0:T(1,128)} %param.13) | copy-start | bytes 52
  26.0 27.7 %copy-start.5 = (bf16[128,1024]{1,0:T(8,128)(2,1)S(1)}, bf16[128,1024]{1,0:T(8,128)(2,1)}, u32[]{:S(2)}) copy-start(bf16[128,1024]{1,0:T(8,128)(2,1)} %param.10) | copy-start | bytes 786436
  27.3 40.8 %collective-permute-start = (bf16[128,1,896]{2,0,1:T(8,128)(2,1)}, bf16[128,1,896]{2,0,1:T(8,128)(2,1)S(1)}, u32[]{:S(2)}, u32[]{:S(2)}) collective-permute-start(bf16[128,1,896]{2,0,1:T(8,128)(2,1)} %get-tuple-element.231), channel_id=1, source_target_pairs={{0,1},{1,0},{2,3},{3,2},{4,5},{5,4},{6,7},{7,6},{8,9},{9,8},{10,11... | collective-permute-start | bytes 688136 | tf_op jit(solution)/shard_map/ppermute | solution.py:34
  35.2 38.0 %collective-permute-start.1 = (bf16[128,1,896]{2,0,1:T(8,128)(2,1)}, bf16[128,1,896]{2,0,1:T(8,128)(2,1)S(1)}, u32[]{:S(2)}, u32[]{:S(2)}) collective-permute-start(bf16[128,1,896]{2,0,1:T(8,128)(2,1)} %get-tuple-element.230), channel_id=1, source_target_pairs={{0,2},{1,3},{2,0},{3,1},{4,6},{5,7},{6,4},{7,5},{8,10},{9,11},{10,... | collective-permute-start | bytes 688136 | tf_op jit(solution)/shard_map/ppermute | solution.py:34
  38.4 37.5 %collective-permute-start.2 = (bf16[128,1,896]{2,0,1:T(8,128)(2,1)}, bf16[128,1,896]{2,0,1:T(8,128)(2,1)S(1)}, u32[]{:S(2)}, u32[]{:S(2)}) collective-permute-start(bf16[128,1,896]{2,0,1:T(8,128)(2,1)} %get-tuple-element.229), channel_id=1, source_target_pairs={{0,3},{1,2},{2,1},{3,0},{4,7},{5,6},{6,5},{7,4},{8,11},{9,10},{10,... | collective-permute-start | bytes 688136 | tf_op jit(solution)/shard_map/ppermute | solution.py:34
  40.3 36.3 %collective-permute-start.3 = (bf16[128,1,896]{2,0,1:T(8,128)(2,1)}, bf16[128,1,896]{2,0,1:T(8,128)(2,1)S(1)}, u32[]{:S(2)}, u32[]{:S(2)}) collective-permute-start(bf16[128,1,896]{2,0,1:T(8,128)(2,1)} %get-tuple-element.228), channel_id=1, source_target_pairs={{0,4},{1,5},{2,6},{3,7},{4,0},{5,1},{6,2},{7,3},{8,12},{9,13},{10,... | collective-permute-start | bytes 688136 | tf_op jit(solution)/shard_map/ppermute | solution.py:34
  44.9 32.3 %collective-permute-start.4 = (bf16[128,1,896]{2,0,1:T(8,128)(2,1)}, bf16[128,1,896]{2,0,1:T(8,128)(2,1)S(1)}, u32[]{:S(2)}, u32[]{:S(2)}) collective-permute-start(bf16[128,1,896]{2,0,1:T(8,128)(2,1)} %get-tuple-element.227), channel_id=1, source_target_pairs={{0,5},{1,4},{2,7},{3,6},{4,1},{5,0},{6,3},{7,2},{8,13},{9,12},{10,... | collective-permute-start | bytes 688136 | tf_op jit(solution)/shard_map/ppermute | solution.py:34
  55.9 23.0 %all-to-all-start.1 = ((bf16[64,2,256]{2,1,0:T(2,128)(2,1)}), bf16[64,2,256]{2,1,0:T(2,128)(2,1)S(1)}, u32[]{:S(2)}, u32[]{:S(2)}) async-start(bf16[64,2,256]{2,1,0:T(2,128)(2,1)} %reshape.282), calls=%async_computation.1 | async-start | bytes 131072 | tf_op jit(solution)/shard_map/all_to_all | solution.py:98
  68.1 10.2 %collective-permute-start.5 = (bf16[128,1,896]{2,0,1:T(8,128)(2,1)}, bf16[128,1,896]{2,0,1:T(8,128)(2,1)S(1)}, u32[]{:S(2)}, u32[]{:S(2)}) collective-permute-start(bf16[128,1,896]{2,0,1:T(8,128)(2,1)} %get-tuple-element.226), channel_id=1, source_target_pairs={{0,6},{1,7},{2,4},{3,5},{4,2},{5,3},{6,0},{7,1},{8,14},{9,15},{10,... | collective-permute-start | bytes 688136 | tf_op jit(solution)/shard_map/ppermute | solution.py:34
  73.2 18.6 %collective-permute-start.6 = (bf16[128,1,896]{2,0,1:T(8,128)(2,1)S(1)}, bf16[128,1,896]{2,0,1:T(8,128)(2,1)S(1)}, u32[]{:S(2)}, u32[]{:S(2)}) collective-permute-start(bf16[128,1,896]{2,0,1:T(8,128)(2,1)S(1)} %get-tuple-element.225), channel_id=1, source_target_pairs={{0,7},{1,6},{2,5},{3,4},{4,3},{5,2},{6,1},{7,0},{8,15},{9,14},{10,... | collective-permute-start | bytes 688136 | tf_op jit(solution)/shard_map/ppermute | solution.py:34
  80.3 25.7 %collective-permute-start.10 = (bf16[128,1,128]{2,1,0:T(2,128)(2,1)S(1)}, bf16[128,1,128]{2,1,0:T(2,128)(2,1)S(1)}, u32[]{:S(2)}, u32[]{:S(2)}) collective-permute-start(bf16[128,1,128]{2,1,0:T(2,128)(2,1)S(1)} %get-tuple-element.254), channel_id=1, source_target_pairs={{0,4},{1,5},{2,6},{3,7},{4,0},{5,1},{6,2},{7,3},{8,12},{9,13},{10,... | collective-permute-start | bytes 98312 | tf_op jit(solution)/shard_map/ppermute | solution.py:34
  84.1 23.9 %collective-permute-start.11 = (bf16[128,1,128]{2,1,0:T(2,128)(2,1)S(1)}, bf16[128,1,128]{2,1,0:T(2,128)(2,1)S(1)}, u32[]{:S(2)}, u32[]{:S(2)}) collective-permute-start(bf16[128,1,128]{2,1,0:T(2,128)(2,1)S(1)} %get-tuple-element.253), channel_id=1, source_target_pairs={{0,5},{1,4},{2,7},{3,6},{4,1},{5,0},{6,3},{7,2},{8,13},{9,12},{10,... | collective-permute-start | bytes 98312 | tf_op jit(solution)/shard_map/ppermute | solution.py:34
  92.5 21.6 %collective-permute-start.12 = (bf16[128,1,128]{2,1,0:T(2,128)(2,1)S(1)}, bf16[128,1,128]{2,1,0:T(2,128)(2,1)S(1)}, u32[]{:S(2)}, u32[]{:S(2)}) collective-permute-start(bf16[128,1,128]{2,1,0:T(2,128)(2,1)S(1)} %get-tuple-element.252), channel_id=1, source_target_pairs={{0,6},{1,7},{2,4},{3,5},{4,2},{5,3},{6,0},{7,1},{8,14},{9,15},{10,... | collective-permute-start | bytes 98312 | tf_op jit(solution)/shard_map/ppermute | solution.py:34
  96.9 17.3 %collective-permute-start.13 = (bf16[128,1,128]{2,1,0:T(2,128)(2,1)S(1)}, bf16[128,1,128]{2,1,0:T(2,128)(2,1)S(1)}, u32[]{:S(2)}, u32[]{:S(2)}) collective-permute-start(bf16[128,1,128]{2,1,0:T(2,128)(2,1)S(1)} %get-tuple-element.251), channel_id=1, source_target_pairs={{0,7},{1,6},{2,5},{3,4},{4,3},{5,2},{6,1},{7,0},{8,15},{9,14},{10,... | collective-permute-start | bytes 98312 | tf_op jit(solution)/shard_map/ppermute | solution.py:34
  99.2 15.0 %collective-permute-start.7 = (bf16[128,1,128]{2,1,0:T(2,128)(2,1)S(1)}, bf16[128,1,128]{2,1,0:T(2,128)(2,1)S(1)}, u32[]{:S(2)}, u32[]{:S(2)}) collective-permute-start(bf16[128,1,128]{2,1,0:T(2,128)(2,1)S(1)} %get-tuple-element.257), channel_id=1, source_target_pairs={{0,1},{1,0},{2,3},{3,2},{4,5},{5,4},{6,7},{7,6},{8,9},{9,8},{10,11... | collective-permute-start | bytes 98312 | tf_op jit(solution)/shard_map/ppermute | solution.py:34
  106.1 8.2 %collective-permute-start.8 = (bf16[128,1,128]{2,1,0:T(2,128)(2,1)S(1)}, bf16[128,1,128]{2,1,0:T(2,128)(2,1)S(1)}, u32[]{:S(2)}, u32[]{:S(2)}) collective-permute-start(bf16[128,1,128]{2,1,0:T(2,128)(2,1)S(1)} %get-tuple-element.256), channel_id=1, source_target_pairs={{0,2},{1,3},{2,0},{3,1},{4,6},{5,7},{6,4},{7,5},{8,10},{9,11},{10,... | collective-permute-start | bytes 98312 | tf_op jit(solution)/shard_map/ppermute | solution.py:34
  108.0 9.8 %collective-permute-start.9 = (bf16[128,1,128]{2,1,0:T(2,128)(2,1)S(1)}, bf16[128,1,128]{2,1,0:T(2,128)(2,1)S(1)}, u32[]{:S(2)}, u32[]{:S(2)}) collective-permute-start(bf16[128,1,128]{2,1,0:T(2,128)(2,1)S(1)} %get-tuple-element.255), channel_id=1, source_target_pairs={{0,3},{1,2},{2,1},{3,0},{4,7},{5,6},{6,5},{7,4},{8,11},{9,10},{10,... | collective-permute-start | bytes 98312 | tf_op jit(solution)/shard_map/ppermute | solution.py:34
  121.7 2.0 copy-start.1
  124.3 4.0 %copy-start.2 = (f32[1024,1024]{0,1:T(8,128)S(1)}, f32[1024,1024]{0,1:T(8,128)}, u32[]{:S(2)}) copy-start(f32[1024,1024]{0,1:T(8,128)} %copy-done.1) | copy-start | bytes 12582916 | tf_op jit(solution)/shard_map/while
  129.3 1.2 copy-start.6
  134.5 2.0 copy-start.1
  137.1 4.1 %copy-start.2 = (f32[1024,1024]{0,1:T(8,128)S(1)}, f32[1024,1024]{0,1:T(8,128)}, u32[]{:S(2)}) copy-start(f32[1024,1024]{0,1:T(8,128)} %copy-done.1) | copy-start | bytes 12582916 | tf_op jit(solution)/shard_map/while
  142.1 1.2 copy-start.6
  147.3 2.0 copy-start.1
  149.9 4.1 %copy-start.2 = (f32[1024,1024]{0,1:T(8,128)S(1)}, f32[1024,1024]{0,1:T(8,128)}, u32[]{:S(2)}) copy-start(f32[1024,1024]{0,1:T(8,128)} %copy-done.1) | copy-start | bytes 12582916 | tf_op jit(solution)/shard_map/while
  155.0 1.2 copy-start.6
  157.9 61.2 %copy-start.4 = (f32[1024,128]{1,0:T(8,128)S(1)}, f32[1024,128]{1,0:T(8,128)}, u32[]{:S(2)}) copy-start(f32[1024,128]{1,0:T(8,128)} %get-tuple-element.160) | copy-start | bytes 1572868
  158.0 20.4 %collective-permute-start.21 = (f32[1,128,128]{2,1,0:T(8,128)S(1)}, f32[1,128,128]{2,1,0:T(8,128)S(1)}, u32[]{:S(2)}, u32[]{:S(2)}) collective-permute-start(f32[1,128,128]{2,1,0:T(8,128)S(1)} %get-tuple-element.248), channel_id=1, source_target_pairs={{0,1},{1,0},{2,3},{3,2},{4,5},{5,4},{6,7},{7,6},{8,9},{9,8},{10,11... | collective-permute-start | bytes 196616 | tf_op jit(solution)/shard_map/ppermute | solution.py:34
  161.4 21.3 %collective-permute-start.22 = (f32[1,128,128]{2,1,0:T(8,128)S(1)}, f32[1,128,128]{2,1,0:T(8,128)S(1)}, u32[]{:S(2)}, u32[]{:S(2)}) collective-permute-start(f32[1,128,128]{2,1,0:T(8,128)S(1)} %get-tuple-element.247), channel_id=1, source_target_pairs={{0,2},{1,3},{2,0},{3,1},{4,6},{5,7},{6,4},{7,5},{8,10},{9,11},{10,... | collective-permute-start | bytes 196616 | tf_op jit(solution)/shard_map/ppermute | solution.py:34
  163.8 31.1 %collective-permute-start.23 = (f32[1,128,128]{2,1,0:T(8,128)S(1)}, f32[1,128,128]{2,1,0:T(8,128)S(1)}, u32[]{:S(2)}, u32[]{:S(2)}) collective-permute-start(f32[1,128,128]{2,1,0:T(8,128)S(1)} %get-tuple-element.246), channel_id=1, source_target_pairs={{0,3},{1,2},{2,1},{3,0},{4,7},{5,6},{6,5},{7,4},{8,11},{9,10},{10,... | collective-permute-start | bytes 196616 | tf_op jit(solution)/shard_map/ppermute | solution.py:34
  170.4 25.9 %collective-permute-start.24 = (f32[1,128,128]{2,1,0:T(8,128)S(1)}, f32[1,128,128]{2,1,0:T(8,128)S(1)}, u32[]{:S(2)}, u32[]{:S(2)}) collective-permute-start(f32[1,128,128]{2,1,0:T(8,128)S(1)} %get-tuple-element.245), channel_id=1, source_target_pairs={{0,4},{1,5},{2,6},{3,7},{4,0},{5,1},{6,2},{7,3},{8,12},{9,13},{10,... | collective-permute-start | bytes 196616 | tf_op jit(solution)/shard_map/ppermute | solution.py:34
  176.0 21.8 %collective-permute-start.25 = (f32[1,128,128]{2,1,0:T(8,128)S(1)}, f32[1,128,128]{2,1,0:T(8,128)S(1)}, u32[]{:S(2)}, u32[]{:S(2)}) collective-permute-start(f32[1,128,128]{2,1,0:T(8,128)S(1)} %get-tuple-element.244), channel_id=1, source_target_pairs={{0,5},{1,4},{2,7},{3,6},{4,1},{5,0},{6,3},{7,2},{8,13},{9,12},{10,... | collective-permute-start | bytes 196616 | tf_op jit(solution)/shard_map/ppermute | solution.py:34
  178.3 20.9 %collective-permute-start.26 = (f32[1,128,128]{2,1,0:T(8,128)S(1)}, f32[1,128,128]{2,1,0:T(8,128)S(1)}, u32[]{:S(2)}, u32[]{:S(2)}) collective-permute-start(f32[1,128,128]{2,1,0:T(8,128)S(1)} %get-tuple-element.250), channel_id=1, source_target_pairs={{0,6},{1,7},{2,4},{3,5},{4,2},{5,3},{6,0},{7,1},{8,14},{9,15},{10,... | collective-permute-start | bytes 196616 | tf_op jit(solution)/shard_map/ppermute | solution.py:34
  182.7 17.9 %collective-permute-start.27 = (f32[1,128,128]{2,1,0:T(8,128)S(1)}, f32[1,128,128]{2,1,0:T(8,128)S(1)}, u32[]{:S(2)}, u32[]{:S(2)}) collective-permute-start(f32[1,128,128]{2,1,0:T(8,128)S(1)} %get-tuple-element.243), channel_id=1, source_target_pairs={{0,7},{1,6},{2,5},{3,4},{4,3},{5,2},{6,1},{7,0},{8,15},{9,14},{10,... | collective-permute-start | bytes 196616 | tf_op jit(solution)/shard_map/ppermute | solution.py:34
  203.1 26.1 %all-to-all-start.2 = ((f32[64,1,512]{2,1,0:T(1,128)}), f32[64,1,512]{2,1,0:T(1,128)S(1)}, u32[]{:S(2)}, u32[]{:S(2)}) async-start(f32[64,1,512]{2,1,0:T(1,128)} %bitcast.43), calls=%async_computation.2 | async-start | bytes 262144 | tf_op jit(solution)/shard_map/all_to_all | solution.py:96
  219.2 32.4 %collective-permute-start.14 = (bf16[1,128,512]{2,1,0:T(8,128)(2,1)S(1)}, bf16[1,128,512]{2,1,0:T(8,128)(2,1)S(1)}, u32[]{:S(2)}, u32[]{:S(2)}) collective-permute-start(bf16[1,128,512]{2,1,0:T(8,128)(2,1)S(1)} %get-tuple-element.235), channel_id=1, source_target_pairs={{0,1},{1,0},{2,3},{3,2},{4,5},{5,4},{6,7},{7,6},{8,9},{9,8},{10,11... | collective-permute-start | bytes 393224 | tf_op jit(solution)/shard_map/ppermute | solution.py:34
  221.8 33.8 %collective-permute-start.15 = (bf16[1,128,512]{2,1,0:T(8,128)(2,1)S(1)}, bf16[1,128,512]{2,1,0:T(8,128)(2,1)S(1)}, u32[]{:S(2)}, u32[]{:S(2)}) collective-permute-start(bf16[1,128,512]{2,1,0:T(8,128)(2,1)S(1)} %get-tuple-element.236), channel_id=1, source_target_pairs={{0,2},{1,3},{2,0},{3,1},{4,6},{5,7},{6,4},{7,5},{8,10},{9,11},{10,... | collective-permute-start | bytes 393224 | tf_op jit(solution)/shard_map/ppermute | solution.py:34
  230.7 57.0 %all-to-all-start.3 = ((f32[64,1,512]{2,1,0:T(1,128)}), f32[64,1,512]{2,1,0:T(1,128)S(1)}, u32[]{:S(2)}, u32[]{:S(2)}) async-start(f32[64,1,512]{2,1,0:T(1,128)} %copy.122), calls=%async_computation.3 | async-start | bytes 262144 | tf_op jit(solution)/shard_map/all_to_all | solution.py:98
  236.7 34.8 %collective-permute-start.16 = (bf16[1,128,512]{2,1,0:T(8,128)(2,1)S(1)}, bf16[1,128,512]{2,1,0:T(8,128)(2,1)}, u32[]{:S(2)}, u32[]{:S(2)}) collective-permute-start(bf16[1,128,512]{2,1,0:T(8,128)(2,1)S(1)} %get-tuple-element.237), channel_id=1, source_target_pairs={{0,3},{1,2},{2,1},{3,0},{4,7},{5,6},{6,5},{7,4},{8,11},{9,10},{10,... | collective-permute-start | bytes 393224 | tf_op jit(solution)/shard_map/ppermute | solution.py:34
  244.4 30.5 %collective-permute-start.17 = (bf16[1,128,512]{2,1,0:T(8,128)(2,1)S(1)}, bf16[1,128,512]{2,1,0:T(8,128)(2,1)}, u32[]{:S(2)}, u32[]{:S(2)}) collective-permute-start(bf16[1,128,512]{2,1,0:T(8,128)(2,1)S(1)} %get-tuple-element.238), channel_id=1, source_target_pairs={{0,4},{1,5},{2,6},{3,7},{4,0},{5,1},{6,2},{7,3},{8,12},{9,13},{10,... | collective-permute-start | bytes 393224 | tf_op jit(solution)/shard_map/ppermute | solution.py:34
  248.3 30.0 %collective-permute-start.18 = (bf16[1,128,512]{2,1,0:T(8,128)(2,1)S(1)}, bf16[1,128,512]{2,1,0:T(8,128)(2,1)S(1)}, u32[]{:S(2)}, u32[]{:S(2)}) collective-permute-start(bf16[1,128,512]{2,1,0:T(8,128)(2,1)S(1)} %get-tuple-element.239), channel_id=1, source_target_pairs={{0,5},{1,4},{2,7},{3,6},{4,1},{5,0},{6,3},{7,2},{8,13},{9,12},{10,... | collective-permute-start | bytes 393224 | tf_op jit(solution)/shard_map/ppermute | solution.py:34
  251.6 29.2 %collective-permute-start.19 = (bf16[1,128,512]{2,1,0:T(8,128)(2,1)S(1)}, bf16[1,128,512]{2,1,0:T(8,128)(2,1)S(1)}, u32[]{:S(2)}, u32[]{:S(2)}) collective-permute-start(bf16[1,128,512]{2,1,0:T(8,128)(2,1)S(1)} %get-tuple-element.240), channel_id=1, source_target_pairs={{0,6},{1,7},{2,4},{3,5},{4,2},{5,3},{6,0},{7,1},{8,14},{9,15},{10,... | collective-permute-start | bytes 393224 | tf_op jit(solution)/shard_map/ppermute | solution.py:34
  255.6 27.7 %collective-permute-start.20 = (bf16[1,128,512]{2,1,0:T(8,128)(2,1)S(1)}, bf16[1,128,512]{2,1,0:T(8,128)(2,1)S(1)}, u32[]{:S(2)}, u32[]{:S(2)}) collective-permute-start(bf16[1,128,512]{2,1,0:T(8,128)(2,1)S(1)} %get-tuple-element.233), channel_id=1, source_target_pairs={{0,7},{1,6},{2,5},{3,4},{4,3},{5,2},{6,1},{7,0},{8,15},{9,14},{10,... | collective-permute-start | bytes 393224 | tf_op jit(solution)/shard_map/ppermute | solution.py:34

commit v3 on v1

--- a/solution.py
+++ b/solution.py
@@ -131,23 +131,26 @@
         query_side, key_side, value_side, grad_side, visible
     )
 
-    low = jnp.concatenate([query_grads, value_gradient.astype(jnp.bfloat16)], axis=1)
+    low = jnp.concatenate(
+        [query_grads, value_gradient.astype(jnp.bfloat16), key_grads.astype(jnp.bfloat16)], axis=1
+    )
     low_back = lax.all_to_all(low, "seq", split_axis=0, concat_axis=1, tiled=True)
     low_back = low_back.reshape(tok_rows, sequence_count, -1)
+    v_end = widths[0] + widths[3]
     query_out = low_back[:, :, : widths[0]].reshape(tok_rows, -1)
-    value_out = low_back[:, :, widths[0] :].reshape(tok_rows, -1)
-    key_back = lax.all_to_all(key_grads, "seq", split_axis=0, concat_axis=1, tiled=True)
+    value_out = low_back[:, :, widths[0] : v_end].reshape(tok_rows, -1)
+    key_back = low_back[:, :, v_end:].reshape(tok_rows, -1)
 
     returning = pick_heads(key_back, my_knock)
     returned = route(returning, consumer)
     key3 = key_back.reshape(tok_rows, KEY_VALUE_HEADS, HEAD_WIDTH)
     own = key3
     for k in range(KNOCKOUT_COUNT):
-        own = jnp.where(head_ids == my_knock[k], 0.0, own)
+        own = jnp.where(head_ids == my_knock[k], jnp.zeros_like(own), own)
     extra = jnp.zeros_like(key3)
     for k in range(KNOCKOUT_COUNT):
         extra = jnp.where(head_ids == their_knock[k], returned[:, k : k + 1, :], extra)
-    key_out = (own + extra).astype(jnp.bfloat16).reshape(tok_rows, -1)
+    key_out = (own.astype(jnp.float32) + extra.astype(jnp.float32)).astype(jnp.bfloat16).reshape(tok_rows, -1)
     return (query_out, key_out, value_out)
 
 

time: 251 us -> 235 us (0.936)
  the two profiles are of different devices: /device:TPU:64 before, /device:TPU:1 now
where the time goes in v3:
time: 235 us; the launch traced here: 234 us
  waiting for transfers between devices  86.5 us (37%)
  starting transfers between devices  74.7 us (32%)
  matrix products  26.3 us (11%)
  local copies, waits for them, and re-layouts  23.3 us (10%)
  other arithmetic  17.3 us (7%)
  between operations  5.42 us (2%)
    all_to_all x2, starting transfers between devices, route(): spread = lax.all_to_all(flat, 'dp', 0, 0, tiled=True)  50.6 us
    all_to_all x1, waiting for transfers between devices, per_device(): lax.all_to_all(packed, 'seq', split_axis=1, concat_axis=0, tiled=True)  38.7 us
    all_to_all x2, waiting for transfers between devices, route(): spread = lax.all_to_all(flat, 'dp', 0, 0, tiled=True)  17.7 us
    all_to_all x2, waiting for transfers between devices, route(): back = lax.all_to_all(routed, 'dp', 0, 0, tiled=True)  15.6 us
    all_to_all x1, waiting for transfers between devices, per_device(): lax.all_to_all(low, 'seq', split_axis=0, concat_axis=1, tiled=True)  14.6 us
    all_to_all x1, starting transfers between devices, per_device(): lax.all_to_all(packed, 'seq', split_axis=1, concat_axis=0, tiled=True)  9.77 us
    dot_general x3, matrix products, one_head(): jnp.einsum('ij,id->jd', probs_low, grad_rows, preferred_element_type=jnp....  9.6 us
    all_to_all x2, starting transfers between devices, route(): back = lax.all_to_all(routed, 'dp', 0, 0, tiled=True)  8.89 us
  transfers between devices with their start and end apart: 6, of which 6 were waited for; matrix products, arithmetic and copies ran while one was open for 3% of the time, Pallas kernels for 0%

profile of v3, /device:TPU:1, one launch (start us, length us, event | category | flops | bytes accessed | tf_op | source)
XLA Modules:
  0.0 233.9 jit_solution(4329311517841781602)
XLA Ops:
  0.7 0.8 select_reduce_fusion
  4.0 0.8 constant_dynamic-slice_fusion.2
  6.7 0.8 dynamic-slice_bitcast_fusion.1
  8.2 1.1 reduce.2
  9.9 14.6 %all-to-all-start = ((bf16[64,2,256]{2,1,0:T(2,128)(2,1)}), bf16[64,2,256]{2,1,0:T(2,128)(2,1)S(1)}, u32[]{:S(2)}, u32[]{:S(2)}) async-start(bf16[64,2,256]{2,1,0:T(2,128)(2,1)} %reshape.159), calls=%async_computation | async-start | bytes 131072 | tf_op jit(solution)/shard_map/all_to_all | solution.py:72
  25.2 1.6 copy_bitcast_fusion
  26.9 7.7 %all-to-all-done = bf16[64,2,256]{2,1,0:T(2,128)(2,1)S(1)} async-done(((bf16[64,2,256]{2,1,0:T(2,128)(2,1)}), bf16[64,2,256]{2,1,0:T(2,128)(2,1)S(1)}, u32[]{:S(2)}, u32[]{:S(2)}) %all-to-all-start) | async-done | bytes 65568 | tf_op jit(solution)/shard_map/all_to_all | solution.py:72
  36.7 4.4 %all-to-all-start.1 = ((bf16[64,2,256]{2,1,0:T(2,128)(2,1)}), bf16[64,2,256]{2,1,0:T(2,128)(2,1)S(1)}, u32[]{:S(2)}, u32[]{:S(2)}) async-start(bf16[64,2,256]{2,1,0:T(2,128)(2,1)} %reshape.161), calls=%async_computation.1 | async-start | bytes 131072 | tf_op jit(solution)/shard_map/all_to_all | solution.py:74
  42.5 8.8 %all-to-all-done.1 = bf16[64,2,256]{2,1,0:T(2,128)(2,1)S(1)} async-done(((bf16[64,2,256]{2,1,0:T(2,128)(2,1)}), bf16[64,2,256]{2,1,0:T(2,128)(2,1)S(1)}, u32[]{:S(2)}, u32[]{:S(2)}) %all-to-all-start.1) | async-done | bytes 65568 | tf_op jit(solution)/shard_map/all_to_all | solution.py:74
  52.4 1.7 pad_maximum_fusion
  54.1 9.8 %all-to-all-start.2 = ((bf16[128,8,1024]{2,0,1:T(8,128)(2,1)}), bf16[128,8,1024]{2,0,1:T(8,128)(2,1)S(1)}, u32[]{:S(2)}, u32[]{:S(2)}) async-start(bf16[128,8,1024]{2,0,1:T(8,128)(2,1)} %pad_maximum_fusion), calls=%async_computation.2 | async-start | bytes 4194304 | tf_op jit(solution)/shard_map/all_to_all | solution.py:121
  64.2 38.7 %all-to-all-done.2 = bf16[128,8,1024]{2,0,1:T(8,128)(2,1)S(1)} async-done(((bf16[128,8,1024]{2,0,1:T(8,128)(2,1)}), bf16[128,8,1024]{2,0,1:T(8,128)(2,1)S(1)}, u32[]{:S(2)}, u32[]{:S(2)}) %all-to-all-start.2) | async-done | bytes 2097184 | tf_op jit(solution)/shard_map/all_to_all | solution.py:121
  102.9 1.3 fusion.23
  104.1 0.9 fusion.22
  105.1 38.7 %while.18 = (s32[]{:T(128)}, bf16[1024,384]{1,0:T(8,128)(2,1)S(1)}, f32[1024,128]{1,0:T(8,128)S(1)}, f32[1024,128]{1,0:T(8,128)S(1)}, bf16[1024,384]{1,0:T(8,128...) while((s32[]{:T(128)}, bf16[1024,384]{1,0:T(8,128)(2,1)S(1)}, ...), condition=%wide.region_7.9_spmd.clone, body=%wide.region_3.0_spmd.clone.sunk | while | flops 1364849664 | bytes 78696792 | solution.py:66
  105.1 2.0 fusion.55
  107.1 1.9 copy-done.1
  109.7 3.2 %fusion.58 = f32[1024,128]{1,0:T(8,128)S(1)} fusion(f32[1024,128]{1,0:T(8,128)S(1)} %get-tuple-element.329, pred[]{:T(512)S(6)} %compare.3, bf16[1024,384]{1,0:T(8,128)(2,1)S(1)} %copy-done.3, s32[]{:T(128)S(6)} %select_n.105, f32[1024,1024]{0,1:T(8,128)} %copy-done.1, f32[1024]{0:T(1024)S(1)} %fusion.56, f32[1024]{0:T(1024)S(1)} %get-tuple-element.310), kind=kOutput, calls=%fused_computation.13.clone.1 | convolution fusion | flops 271843328 | bytes 5513221 | tf_op jit(solution)/shard_map/while/body/eval_jaxpr/ij,id->jd/dot_general | solution.py:42
  113.1 1.0 multiply_reduce_fusion.2
  114.1 1.2 multiply_convert_fusion.2
  115.3 0.9 fusion.57
  116.2 1.7 convolution_add_fusion.2
  118.0 2.0 fusion.55
  120.0 1.9 copy-done.1
  122.6 3.2 %fusion.58 = f32[1024,128]{1,0:T(8,128)S(1)} fusion(f32[1024,128]{1,0:T(8,128)S(1)} %get-tuple-element.329, pred[]{:T(512)S(6)} %compare.3, bf16[1024,384]{1,0:T(8,128)(2,1)S(1)} %copy-done.3, s32[]{:T(128)S(6)} %select_n.105, f32[1024,1024]{0,1:T(8,128)} %copy-done.1, f32[1024]{0:T(1024)S(1)} %fusion.56, f32[1024]{0:T(1024)S(1)} %get-tuple-element.310), kind=kOutput, calls=%fused_computation.13.clone.1 | convolution fusion | flops 271843328 | bytes 5513221 | tf_op jit(solution)/shard_map/while/body/eval_jaxpr/ij,id->jd/dot_general | solution.py:42
  126.0 1.0 multiply_reduce_fusion.2
  127.0 1.2 multiply_convert_fusion.2
  128.2 0.9 fusion.57
  129.1 1.7 convolution_add_fusion.2
  130.9 2.0 fusion.55
  132.9 1.9 copy-done.1
  135.5 3.2 %fusion.58 = f32[1024,128]{1,0:T(8,128)S(1)} fusion(f32[1024,128]{1,0:T(8,128)S(1)} %get-tuple-element.329, pred[]{:T(512)S(6)} %compare.3, bf16[1024,384]{1,0:T(8,128)(2,1)S(1)} %copy-done.3, s32[]{:T(128)S(6)} %select_n.105, f32[1024,1024]{0,1:T(8,128)} %copy-done.1, f32[1024]{0:T(1024)S(1)} %fusion.56, f32[1024]{0:T(1024)S(1)} %get-tuple-element.310), kind=kOutput, calls=%fused_computation.13.clone.1 | convolution fusion | flops 271843328 | bytes 5513221 | tf_op jit(solution)/shard_map/while/body/eval_jaxpr/ij,id->jd/dot_general | solution.py:42
  138.9 1.0 multiply_reduce_fusion.2
  139.9 1.2 multiply_convert_fusion.2
  141.1 0.9 fusion.57
  142.0 1.7 convolution_add_fusion.2
  143.8 1.2 pad_maximum_fusion.1
  145.0 5.5 %all-to-all-start.3 = ((bf16[8,128,640]{2,1,0:T(8,128)(2,1)}), bf16[8,128,640]{2,1,0:T(8,128)(2,1)S(1)}, u32[]{:S(2)}, u32[]{:S(2)}) async-start(bf16[8,128,640]{2,1,0:T(8,128)(2,1)} %bitcast.18), calls=%async_computation.3 | async-start | bytes 2621440 | tf_op jit(solution)/shard_map/all_to_all | solution.py:137
  151.6 14.6 %all-to-all-done.3 = bf16[8,128,640]{2,1,0:T(8,128)(2,1)S(1)} async-done(((bf16[8,128,640]{2,1,0:T(8,128)(2,1)}), bf16[8,128,640]{2,1,0:T(8,128)(2,1)S(1)}, u32[]{:S(2)}, u32[]{:S(2)}) %all-to-all-start.3) | async-done | bytes 1310752 | tf_op jit(solution)/shard_map/all_to_all | solution.py:137
  166.2 0.8 copy.63
  167.5 1.1 reduce.4
  169.2 36.0 %all-to-all-start.4 = ((bf16[64,2,256]{2,1,0:T(2,128)(2,1)}), bf16[64,2,256]{2,1,0:T(2,128)(2,1)S(1)}, u32[]{:S(2)}, u32[]{:S(2)}) async-start(bf16[64,2,256]{2,1,0:T(2,128)(2,1)} %reshape.163), calls=%async_computation.4 | async-start | bytes 131072 | tf_op jit(solution)/shard_map/all_to_all | solution.py:72
  205.2 10.0 %all-to-all-done.4 = bf16[64,2,256]{2,1,0:T(2,128)(2,1)S(1)} async-done(((bf16[64,2,256]{2,1,0:T(2,128)(2,1)}), bf16[64,2,256]{2,1,0:T(2,128)(2,1)S(1)}, u32[]{:S(2)}, u32[]{:S(2)}) %all-to-all-start.4) | async-done | bytes 65568 | tf_op jit(solution)/shard_map/all_to_all | solution.py:72
  217.4 4.4 %all-to-all-start.5 = ((bf16[64,2,256]{2,1,0:T(2,128)(2,1)}), bf16[64,2,256]{2,1,0:T(2,128)(2,1)S(1)}, u32[]{:S(2)}, u32[]{:S(2)}) async-start(bf16[64,2,256]{2,1,0:T(2,128)(2,1)} %reshape.165), calls=%async_computation.5 | async-start | bytes 131072 | tf_op jit(solution)/shard_map/all_to_all | solution.py:74
  223.2 1.2 copy.71
  224.4 0.8 copy.73
  225.2 6.8 %all-to-all-done.5 = bf16[64,2,256]{2,1,0:T(2,128)(2,1)S(1)} async-done(((bf16[64,2,256]{2,1,0:T(2,128)(2,1)}), bf16[64,2,256]{2,1,0:T(2,128)(2,1)S(1)}, u32[]{:S(2)}, u32[]{:S(2)}) %all-to-all-start.5) | async-done | bytes 65568 | tf_op jit(solution)/shard_map/all_to_all | solution.py:74
  233.0 0.9 copy.72
  (99 shorter events, 16.4 us)
Async XLA Ops:
  0.6 24.5 %copy-start = (bf16[128,1024]{1,0:T(8,128)(2,1)S(1)}, bf16[128,1024]{1,0:T(8,128)(2,1)}, u32[]{:S(2)}) copy-start(bf16[128,1024]{1,0:T(8,128)(2,1)} %param.13) | copy-start | bytes 786436
  0.6 26.2 %copy-start.7 = (s32[64]{0:T(128)S(1)}, s32[64]{0:T(128)}, u32[]{:S(2)}) copy-start(s32[64]{0:T(128)} %param.17) | copy-start | bytes 772
  0.7 41.1 %copy-start.4 = (bf16[128,1024]{1,0:T(8,128)(2,1)S(1)}, bf16[128,1024]{1,0:T(8,128)(2,1)}, u32[]{:S(2)}) copy-start(bf16[128,1024]{1,0:T(8,128)(2,1)} %param.12) | copy-start | bytes 786436
  9.9 24.6 %all-to-all-start = ((bf16[64,2,256]{2,1,0:T(2,128)(2,1)}), bf16[64,2,256]{2,1,0:T(2,128)(2,1)S(1)}, u32[]{:S(2)}, u32[]{:S(2)}) async-start(bf16[64,2,256]{2,1,0:T(2,128)(2,1)} %reshape.159), calls=%async_computation | async-start | bytes 131072 | tf_op jit(solution)/shard_map/all_to_all | solution.py:72
  36.7 14.6 %all-to-all-start.1 = ((bf16[64,2,256]{2,1,0:T(2,128)(2,1)}), bf16[64,2,256]{2,1,0:T(2,128)(2,1)S(1)}, u32[]{:S(2)}, u32[]{:S(2)}) async-start(bf16[64,2,256]{2,1,0:T(2,128)(2,1)} %reshape.161), calls=%async_computation.1 | async-start | bytes 131072 | tf_op jit(solution)/shard_map/all_to_all | solution.py:74
  52.4 11.5 %copy-start.8 = (s32[1,4]{1,0:T(1,128)S(1)}, s32[1,4]{1,0:T(1,128)}, u32[]{:S(2)}) copy-start(s32[1,4]{1,0:T(1,128)} %param.15) | copy-start | bytes 52
  54.1 48.7 %all-to-all-start.2 = ((bf16[128,8,1024]{2,0,1:T(8,128)(2,1)}), bf16[128,8,1024]{2,0,1:T(8,128)(2,1)S(1)}, u32[]{:S(2)}, u32[]{:S(2)}) async-start(bf16[128,8,1024]{2,0,1:T(8,128)(2,1)} %pad_maximum_fusion), calls=%async_computation.2 | async-start | bytes 4194304 | tf_op jit(solution)/shard_map/all_to_all | solution.py:121
  105.1 4.6 %copy-start.3 = (bf16[1024,384]{1,0:T(8,128)(2,1)S(1)}, bf16[1024,384]{1,0:T(8,128)(2,1)}, u32[]{:S(2)}) copy-start(bf16[1024,384]{1,0:T(8,128)(2,1)} %get-tuple-element.345) | copy-start | bytes 2359300 | tf_op jit(solution)/shard_map/while
  107.1 1.9 copy-start.1
  109.7 3.5 %copy-start.2 = (f32[1024,1024]{0,1:T(8,128)S(1)}, f32[1024,1024]{0,1:T(8,128)}, u32[]{:S(2)}) copy-start(f32[1024,1024]{0,1:T(8,128)} %copy-done.1) | copy-start | bytes 12582916 | tf_op jit(solution)/shard_map/while
  109.7 3.5 %copy-start.5 = (bf16[1024,128]{1,0:T(8,128)(2,1)S(1)}, bf16[1024,128]{1,0:T(8,128)(2,1)}, u32[]{:S(2)}) copy-start(bf16[1024,128]{1,0:T(8,128)(2,1)} %get-tuple-element.346) | copy-start | bytes 786436 | tf_op jit(solution)/shard_map/while
  114.1 1.2 copy-start.6
  118.0 4.6 %copy-start.3 = (bf16[1024,384]{1,0:T(8,128)(2,1)S(1)}, bf16[1024,384]{1,0:T(8,128)(2,1)}, u32[]{:S(2)}) copy-start(bf16[1024,384]{1,0:T(8,128)(2,1)} %get-tuple-element.345) | copy-start | bytes 2359300 | tf_op jit(solution)/shard_map/while
  120.0 1.9 copy-start.1
  122.6 3.5 %copy-start.2 = (f32[1024,1024]{0,1:T(8,128)S(1)}, f32[1024,1024]{0,1:T(8,128)}, u32[]{:S(2)}) copy-start(f32[1024,1024]{0,1:T(8,128)} %copy-done.1) | copy-start | bytes 12582916 | tf_op jit(solution)/shard_map/while
  122.6 3.5 %copy-start.5 = (bf16[1024,128]{1,0:T(8,128)(2,1)S(1)}, bf16[1024,128]{1,0:T(8,128)(2,1)}, u32[]{:S(2)}) copy-start(bf16[1024,128]{1,0:T(8,128)(2,1)} %get-tuple-element.346) | copy-start | bytes 786436 | tf_op jit(solution)/shard_map/while
  127.0 1.2 copy-start.6
  130.9 4.6 %copy-start.3 = (bf16[1024,384]{1,0:T(8,128)(2,1)S(1)}, bf16[1024,384]{1,0:T(8,128)(2,1)}, u32[]{:S(2)}) copy-start(bf16[1024,384]{1,0:T(8,128)(2,1)} %get-tuple-element.345) | copy-start | bytes 2359300 | tf_op jit(solution)/shard_map/while
  132.9 1.9 copy-start.1
  135.4 3.5 %copy-start.2 = (f32[1024,1024]{0,1:T(8,128)S(1)}, f32[1024,1024]{0,1:T(8,128)}, u32[]{:S(2)}) copy-start(f32[1024,1024]{0,1:T(8,128)} %copy-done.1) | copy-start | bytes 12582916 | tf_op jit(solution)/shard_map/while
  135.5 3.5 %copy-start.5 = (bf16[1024,128]{1,0:T(8,128)(2,1)S(1)}, bf16[1024,128]{1,0:T(8,128)(2,1)}, u32[]{:S(2)}) copy-start(bf16[1024,128]{1,0:T(8,128)(2,1)} %get-tuple-element.346) | copy-start | bytes 786436 | tf_op jit(solution)/shard_map/while
  139.9 1.2 copy-start.6
  145.0 21.2 %all-to-all-start.3 = ((bf16[8,128,640]{2,1,0:T(8,128)(2,1)}), bf16[8,128,640]{2,1,0:T(8,128)(2,1)S(1)}, u32[]{:S(2)}, u32[]{:S(2)}) async-start(bf16[8,128,640]{2,1,0:T(8,128)(2,1)} %bitcast.18), calls=%async_computation.3 | async-start | bytes 2621440 | tf_op jit(solution)/shard_map/all_to_all | solution.py:137
  169.2 46.1 %all-to-all-start.4 = ((bf16[64,2,256]{2,1,0:T(2,128)(2,1)}), bf16[64,2,256]{2,1,0:T(2,128)(2,1)S(1)}, u32[]{:S(2)}, u32[]{:S(2)}) async-start(bf16[64,2,256]{2,1,0:T(2,128)(2,1)} %reshape.163), calls=%async_computation.4 | async-start | bytes 131072 | tf_op jit(solution)/shard_map/all_to_all | solution.py:72
  217.4 14.6 %all-to-all-start.5 = ((bf16[64,2,256]{2,1,0:T(2,128)(2,1)}), bf16[64,2,256]{2,1,0:T(2,128)(2,1)S(1)}, u32[]{:S(2)}, u32[]{:S(2)}) async-start(bf16[64,2,256]{2,1,0:T(2,128)(2,1)} %reshape.165), calls=%async_computation.5 | async-start | bytes 131072 | tf_op jit(solution)/shard_map/all_to_all | solution.py:74

commit v4 on v3

--- a/solution.py
+++ b/solution.py
@@ -3,6 +3,8 @@
 import jax
 import jax.numpy as jnp
 from jax import lax
+from jax.experimental import pallas as pl
+from jax.experimental.pallas import tpu as pltpu
 from jax.sharding import PartitionSpec as P
 
 KEY_VALUE_HEADS = 8
@@ -64,6 +66,92 @@
         jnp.zeros((length, value_side.shape[1]), jnp.float32),
     )
     return lax.fori_loop(0, heads_of_query, one_head, initial)
+
+
+BLOCK_ROWS = 256
+
+
+def attend_kernel(seg_row_ref, seg_col_ref, q_ref, g_ref, k_ref, v_ref, dq_ref, dk_ref, dv_ref):
+    scaling = 1.0 / math.sqrt(HEAD_WIDTH)
+    length = q_ref.shape[0]
+
+    @pl.when(pl.program_id(0) == 0)
+    def _():
+        dk_ref[...] = jnp.zeros_like(dk_ref)
+        dv_ref[...] = jnp.zeros_like(dv_ref)
+
+    for block in range(length // BLOCK_ROWS):
+        rows = pl.ds(block * BLOCK_ROWS, BLOCK_ROWS)
+        span = (block + 1) * BLOCK_ROWS
+        keys = k_ref[0:span, :]
+        vals = v_ref[0:span, :]
+        q_rows = q_ref[rows, :]
+        g_rows = g_ref[rows, :]
+        scores = lax.dot_general(
+            q_rows, keys, (((1,), (1,)), ((), ())), preferred_element_type=jnp.float32
+        ) * scaling
+        row_pos = block * BLOCK_ROWS + lax.broadcasted_iota(jnp.int32, (BLOCK_ROWS, span), 0)
+        col_pos = lax.broadcasted_iota(jnp.int32, (BLOCK_ROWS, span), 1)
+        same = seg_row_ref[rows, :] == seg_col_ref[:, 0:span]
+        visible = jnp.logical_and(row_pos >= col_pos, same)
+        scores = jnp.where(visible, scores, masked_score)
+        row_max = jnp.max(scores, axis=1, keepdims=True)
+        weights = jnp.exp(scores - row_max)
+        probs = weights / jnp.sum(weights, axis=1, keepdims=True)
+        probs_low = probs.astype(jnp.bfloat16)
+        dv_ref[0:span, :] += lax.dot_general(
+            probs_low, g_rows, (((0,), (0,)), ((), ())), preferred_element_type=jnp.float32
+        )
+        prob_grads = lax.dot_general(
+            g_rows, vals, (((1,), (1,)), ((), ())), preferred_element_type=jnp.float32
+        )
+        row_delta = jnp.sum(probs * prob_grads, axis=1, keepdims=True)
+        score_grads = (probs * (prob_grads - row_delta) * scaling).astype(jnp.bfloat16)
+        dq_ref[rows, :] = jnp.dot(
+            score_grads, keys, preferred_element_type=jnp.float32
+        ).astype(dq_ref.dtype)
+        dk_ref[0:span, :] += lax.dot_general(
+            score_grads, q_rows, (((0,), (0,)), ((), ())), preferred_element_type=jnp.float32
+        )
+
+
+def attend_back_kernel(gathered, segment, heads_of_query, q_block, g_block, k_block, v_block):
+    length = gathered.shape[0]
+    seg_row = segment.reshape(length, 1)
+    seg_col = segment.reshape(1, length)
+    full = lambda h: (0, 0)
+    col = lambda b: pl.BlockSpec((length, HEAD_WIDTH), lambda h: (0, b))
+    flops = 5 * 2 * length * length * HEAD_WIDTH * heads_of_query * 10 // 16
+    return pl.pallas_call(
+        attend_kernel,
+        grid=(heads_of_query,),
+        in_specs=[
+            pl.BlockSpec((length, 1), full),
+            pl.BlockSpec((1, length), full),
+            pl.BlockSpec((length, HEAD_WIDTH), lambda h: (0, q_block + h)),
+            pl.BlockSpec((length, HEAD_WIDTH), lambda h: (0, g_block + h)),
+            col(k_block),
+            col(v_block),
+        ],
+        out_specs=[
+            pl.BlockSpec((length, HEAD_WIDTH), lambda h: (0, h)),
+            pl.BlockSpec((length, HEAD_WIDTH), full),
+            pl.BlockSpec((length, HEAD_WIDTH), full),
+        ],
+        out_shape=[
+            jax.ShapeDtypeStruct((length, heads_of_query * HEAD_WIDTH), jnp.bfloat16),
+            jax.ShapeDtypeStruct((length, HEAD_WIDTH), jnp.float32),
+            jax.ShapeDtypeStruct((length, HEAD_WIDTH), jnp.float32),
+        ],
+        compiler_params=pltpu.CompilerParams(
+            dimension_semantics=("arbitrary",), vmem_limit_bytes=48 * 1024 * 1024
+        ),
+        cost_estimate=pl.CostEstimate(
+            flops=flops,
+            transcendentals=length * length * heads_of_query * 10 // 16,
+            bytes_accessed=length * HEAD_WIDTH * (2 * 2 * heads_of_query + 2 * 2 + 2 * heads_of_query + 8),
+        ),
+    )(seg_row, seg_col, gathered, gathered, gathered, gathered)
 
 
 def route(payload, order):
@@ -96,7 +184,6 @@
     my_knock = knocked[prompt_index]
     their_knock = knocked[consumer[prompt_index]]
     head_ids = jnp.arange(KEY_VALUE_HEADS, dtype=jnp.int32)[None, :, None]
-    visible = document_mask(seg_lengths[0], length)
 
     outgoing = pick_heads(keys, their_knock)
     fetched = route(outgoing, source)
@@ -123,12 +210,13 @@
     offsets = [0]
     for w in widths:
         offsets.append(offsets[-1] + w)
-    query_side, grad_side, key_side, value_side = (
-        gathered[:, offsets[i] : offsets[i + 1]] for i in range(4)
-    )
-
-    query_grads, key_grads, value_gradient = attend_back(
-        query_side, key_side, value_side, grad_side, visible
+
+    doc_ends = jnp.cumsum(seg_lengths[0])
+    position = jnp.arange(length, dtype=jnp.int32)
+    segment = jnp.sum((position[:, None] >= doc_ends[None, :]).astype(jnp.int32), axis=1)
+    heads_here = widths[0] // HEAD_WIDTH
+    query_grads, key_grads, value_gradient = attend_back_kernel(
+        gathered, segment, heads_here, 0, heads_here, 2 * heads_here, 2 * heads_here + 1
     )
 
     low = jnp.concatenate(

time: 235 us -> 206 us (0.88)
  matrix products: 26.3 us -> 0 us
  Pallas kernels: 0 us -> 13.5 us
  local copies, waits for them, and re-layouts: 23.3 us -> 15.1 us
  other arithmetic: 17.3 us -> 10.3 us
    dot_general x15 -> x0, matrix products: 26.3 us -> none  [the longest x3 9.6 us: one_head(): jnp.einsum('ij,id->jd', probs_low, grad_rows, preferred_element_type=jnp....]
    pallas_call x0 -> x1, Pallas kernels: none -> 13.5 us  [attend_back_kernel(): pl.pallas_call(attend_kernel, grid=(heads_of_query,), in_specs=[pl.BlockS...]
    while x30 -> x0, local copies, waits for them, and re-layouts: 6.54 us -> none
    convert_element_type x3 -> x0, other arithmetic: 3.61 us -> none  [one_head(): (attn_probs * (prob_grads - row_delta) * scaling).astype(jnp.bfloat16)]
  transfers between devices with their start and end apart: 6 -> 6, of which waited for: 6 -> 6; matrix products, arithmetic and copies ran while one was open for 3% -> 4% of each run, Pallas kernels for 0% -> 0%
where the time goes in v4:
time: 206 us
  waiting for transfers between devices  86.2 us (42%)
  starting transfers between devices  74.8 us (36%)
  local copies, waits for them, and re-layouts  15.1 us (7%)
  Pallas kernels  13.5 us (7%)
  other arithmetic  10.3 us (5%)
  between operations  5.57 us (3%)
    all_to_all x2, starting transfers between devices, route(): spread = lax.all_to_all(flat, 'dp', 0, 0, tiled=True)  50.6 us
    all_to_all x1, waiting for transfers between devices, per_device(): lax.all_to_all(packed, 'seq', split_axis=1, concat_axis=0, tiled=True)  38.5 us
    all_to_all x2, waiting for transfers between devices, route(): spread = lax.all_to_all(flat, 'dp', 0, 0, tiled=True)  17.8 us
    all_to_all x2, waiting for transfers between devices, route(): back = lax.all_to_all(routed, 'dp', 0, 0, tiled=True)  15.4 us
    all_to_all x1, waiting for transfers between devices, per_device(): lax.all_to_all(low, 'seq', split_axis=0, concat_axis=1, tiled=True)  14.4 us
    pallas_call x1, Pallas kernels, attend_back_kernel(): pl.pallas_call(attend_kernel, grid=(heads_of_query,), in_specs=[pl.BlockS...  13.5 us
    all_to_all x1, starting transfers between devices, per_device(): lax.all_to_all(packed, 'seq', split_axis=1, concat_axis=0, tiled=True)  9.9 us
    all_to_all x2, starting transfers between devices, route(): back = lax.all_to_all(routed, 'dp', 0, 0, tiled=True)  8.89 us
  transfers between devices with their start and end apart: 6, of which 6 were waited for; matrix products, arithmetic and copies ran while one was open for 4% of the time, Pallas kernels for 0%

profile of v4, /device:TPU:1, one launch (start us, length us, event | category | flops | bytes accessed | tf_op | source)
XLA Modules:
  0.0 205.5 jit_solution(16364563338416691721)
XLA Ops:
  0.7 0.8 select_reduce_fusion
  1.5 0.6 dynamic_slice.22
  4.0 0.8 constant_dynamic-slice_fusion.2
  4.9 0.6 fusion.3
  6.7 0.8 dynamic-slice_bitcast_fusion.1
  7.6 0.5 broadcast.39
  8.1 0.9 reduce.2
  9.0 0.6 reshape.162
  9.7 14.6 %all-to-all-start = ((bf16[64,2,256]{2,1,0:T(2,128)(2,1)}), bf16[64,2,256]{2,1,0:T(2,128)(2,1)S(1)}, u32[]{:S(2)}, u32[]{:S(2)}) async-start(bf16[64,2,256]{2,1,0:T(2,128)(2,1)} %reshape.162), calls=%async_computation | async-start | bytes 131072 | tf_op jit(solution)/shard_map/all_to_all | solution.py:160
  24.3 0.7 compare_and_fusion
  25.0 1.4 copy_bitcast_fusion
  26.4 7.8 %all-to-all-done = bf16[64,2,256]{2,1,0:T(2,128)(2,1)S(1)} async-done(((bf16[64,2,256]{2,1,0:T(2,128)(2,1)}), bf16[64,2,256]{2,1,0:T(2,128)(2,1)S(1)}, u32[]{:S(2)}, u32[]{:S(2)}) %all-to-all-start) | async-done | bytes 65568 | tf_op jit(solution)/shard_map/all_to_all | solution.py:160
  34.4 0.7 gather_fusion
  35.1 0.6 reduce.3
  35.7 0.6 reshape.164
  36.4 4.4 %all-to-all-start.1 = ((bf16[64,2,256]{2,1,0:T(2,128)(2,1)}), bf16[64,2,256]{2,1,0:T(2,128)(2,1)S(1)}, u32[]{:S(2)}, u32[]{:S(2)}) async-start(bf16[64,2,256]{2,1,0:T(2,128)(2,1)} %reshape.164), calls=%async_computation.1 | async-start | bytes 131072 | tf_op jit(solution)/shard_map/all_to_all | solution.py:162
  40.8 0.7 iota_compare_fusion.4
  41.5 0.2 copy.84
  41.7 0.6 iota_compare_fusion.5
  42.3 8.7 %all-to-all-done.1 = bf16[64,2,256]{2,1,0:T(2,128)(2,1)S(1)} async-done(((bf16[64,2,256]{2,1,0:T(2,128)(2,1)}), bf16[64,2,256]{2,1,0:T(2,128)(2,1)S(1)}, u32[]{:S(2)}, u32[]{:S(2)}) %all-to-all-start.1) | async-done | bytes 65568 | tf_op jit(solution)/shard_map/all_to_all | solution.py:162
  51.0 0.4 reduce
  51.9 0.2 copy.87
  52.1 1.7 pad_maximum_fusion
  53.7 9.9 %all-to-all-start.2 = ((bf16[128,8,1024]{2,0,1:T(8,128)(2,1)}), bf16[128,8,1024]{2,0,1:T(8,128)(2,1)S(1)}, u32[]{:S(2)}, u32[]{:S(2)}) async-start(bf16[128,8,1024]{2,0,1:T(8,128)(2,1)} %pad_maximum_fusion), calls=%async_computation.2 | async-start | bytes 4194304 | tf_op jit(solution)/shard_map/all_to_all | solution.py:208
  63.6 0.2 reduce-window.8
  63.9 0.2 copy.89.seg_row_ref
  64.1 38.5 %all-to-all-done.2 = bf16[128,8,1024]{2,0,1:T(8,128)(2,1)S(1)} async-done(((bf16[128,8,1024]{2,0,1:T(8,128)(2,1)}), bf16[128,8,1024]{2,0,1:T(8,128)(2,1)S(1)}, u32[]{:S(2)}, u32[]{:S(2)}) %all-to-all-start.2) | async-done | bytes 2097184 | tf_op jit(solution)/shard_map/all_to_all | solution.py:208
  102.6 13.5 %shard_map.94 = (bf16[1024,384]{1,0:T(8,128)(2,1)S(1)}, f32[1024,128]{1,0:T(8,128)S(1)}, f32[1024,128]{1,0:T(8,128)S(1)}) custom-call(s32[1024,1]{1,0:T(8,128)S(1)} %copy.89.seg_row_ref, s32[1,1024]{1,0:T(1,128)S(1)} %bitcast.57, bf16[1024,1024]{1,0:T(8,128)(2,1)S(1)} %bitcast.52, bf16[1024,1024]{1,0:T(8,128)(2,1)S(1)} %bitcast.53, ...), custom_call_target="tpu_custom_call" | custom-call | flops 2516582400 | bytes 3932160 | tf_op jit(solution)/shard_map/pallas_call | solution.py:125
  116.1 0.1 pad_maximum_fusion.1
  116.3 1.5 copy.90
  117.8 5.5 %all-to-all-start.3 = ((bf16[8,128,640]{1,2,0:T(8,128)(2,1)}), bf16[8,128,640]{1,2,0:T(8,128)(2,1)S(1)}, u32[]{:S(2)}, u32[]{:S(2)}) async-start(bf16[8,128,640]{1,2,0:T(8,128)(2,1)} %copy.90), calls=%async_computation.3 | async-start | bytes 2621440 | tf_op jit(solution)/shard_map/all_to_all | solution.py:225
  124.5 14.4 %all-to-all-done.3 = bf16[8,128,640]{1,2,0:T(8,128)(2,1)S(1)} async-done(((bf16[8,128,640]{1,2,0:T(8,128)(2,1)}), bf16[8,128,640]{1,2,0:T(8,128)(2,1)S(1)}, u32[]{:S(2)}, u32[]{:S(2)}) %all-to-all-start.3) | async-done | bytes 1310752 | tf_op jit(solution)/shard_map/all_to_all | solution.py:225
  139.4 0.9 reduce.4
  140.3 0.6 reshape.166
  141.0 36.0 %all-to-all-start.4 = ((bf16[64,2,256]{2,1,0:T(2,128)(2,1)}), bf16[64,2,256]{2,1,0:T(2,128)(2,1)S(1)}, u32[]{:S(2)}, u32[]{:S(2)}) async-start(bf16[64,2,256]{2,1,0:T(2,128)(2,1)} %reshape.166), calls=%async_computation.4 | async-start | bytes 131072 | tf_op jit(solution)/shard_map/all_to_all | solution.py:160
  177.0 10.0 %all-to-all-done.4 = bf16[64,2,256]{2,1,0:T(2,128)(2,1)S(1)} async-done(((bf16[64,2,256]{2,1,0:T(2,128)(2,1)}), bf16[64,2,256]{2,1,0:T(2,128)(2,1)S(1)}, u32[]{:S(2)}, u32[]{:S(2)}) %all-to-all-start.4) | async-done | bytes 65568 | tf_op jit(solution)/shard_map/all_to_all | solution.py:160
  187.1 0.7 gather_fusion.1
  187.9 0.6 reduce.5
  188.4 0.6 reshape.168
  189.1 4.4 %all-to-all-start.5 = ((bf16[64,2,256]{2,1,0:T(2,128)(2,1)}), bf16[64,2,256]{2,1,0:T(2,128)(2,1)S(1)}, u32[]{:S(2)}, u32[]{:S(2)}) async-start(bf16[64,2,256]{2,1,0:T(2,128)(2,1)} %reshape.168), calls=%async_computation.5 | async-start | bytes 131072 | tf_op jit(solution)/shard_map/all_to_all | solution.py:162
  193.5 0.7 iota_compare_fusion.2
  194.2 0.6 iota_compare_fusion.3
  194.9 1.2 copy.98
  196.0 0.8 copy.100
  196.9 6.8 %all-to-all-done.5 = bf16[64,2,256]{2,1,0:T(2,128)(2,1)S(1)} async-done(((bf16[64,2,256]{2,1,0:T(2,128)(2,1)}), bf16[64,2,256]{2,1,0:T(2,128)(2,1)S(1)}, u32[]{:S(2)}, u32[]{:S(2)}) %all-to-all-start.5) | async-done | bytes 65568 | tf_op jit(solution)/shard_map/all_to_all | solution.py:162
  203.7 0.4 reduce.1
  204.5 0.2 add_convert_fusion
  204.7 0.9 copy.99
  (46 shorter events, 2.0 us)
Async XLA Ops:
  0.6 24.3 %copy-start = (bf16[128,1024]{1,0:T(8,128)(2,1)S(1)}, bf16[128,1024]{1,0:T(8,128)(2,1)}, u32[]{:S(2)}) copy-start(bf16[128,1024]{1,0:T(8,128)(2,1)} %param.11) | copy-start | bytes 786436
  0.6 24.3 %copy-start.1 = (bf16[128,3072]{1,0:T(8,128)(2,1)S(1)}, bf16[128,3072]{1,0:T(8,128)(2,1)}, u32[]{:S(2)}) copy-start(bf16[128,3072]{1,0:T(8,128)(2,1)} %param.12) | copy-start | bytes 2359300
  7.6 18.8 %copy-start.3 = (s32[64]{0:T(128)S(1)}, s32[64]{0:T(128)}, u32[]{:S(2)}) copy-start(s32[64]{0:T(128)} %param.15) | copy-start | bytes 772
  9.7 24.6 %all-to-all-start = ((bf16[64,2,256]{2,1,0:T(2,128)(2,1)}), bf16[64,2,256]{2,1,0:T(2,128)(2,1)S(1)}, u32[]{:S(2)}, u32[]{:S(2)}) async-start(bf16[64,2,256]{2,1,0:T(2,128)(2,1)} %reshape.162), calls=%async_computation | async-start | bytes 131072 | tf_op jit(solution)/shard_map/all_to_all | solution.py:160
  25.0 16.5 %copy-start.2 = (bf16[128,1024]{1,0:T(8,128)(2,1)S(1)}, bf16[128,1024]{1,0:T(8,128)(2,1)}, u32[]{:S(2)}) copy-start(bf16[128,1024]{1,0:T(8,128)(2,1)} %param.10) | copy-start | bytes 786436
  36.4 14.6 %all-to-all-start.1 = ((bf16[64,2,256]{2,1,0:T(2,128)(2,1)}), bf16[64,2,256]{2,1,0:T(2,128)(2,1)S(1)}, u32[]{:S(2)}, u32[]{:S(2)}) async-start(bf16[64,2,256]{2,1,0:T(2,128)(2,1)} %reshape.164), calls=%async_computation.1 | async-start | bytes 131072 | tf_op jit(solution)/shard_map/all_to_all | solution.py:162
  53.7 9.9 %copy-start.4 = (s32[1,4]{1,0:T(1,128)S(1)}, s32[1,4]{1,0:T(1,128)}, u32[]{:S(2)}) copy-start(s32[1,4]{1,0:T(1,128)} %param.13) | copy-start | bytes 52
  53.7 48.9 %all-to-all-start.2 = ((bf16[128,8,1024]{2,0,1:T(8,128)(2,1)}), bf16[128,8,1024]{2,0,1:T(8,128)(2,1)S(1)}, u32[]{:S(2)}, u32[]{:S(2)}) async-start(bf16[128,8,1024]{2,0,1:T(8,128)(2,1)} %pad_maximum_fusion), calls=%async_computation.2 | async-start | bytes 4194304 | tf_op jit(solution)/shard_map/all_to_all | solution.py:208
  117.8 21.2 %all-to-all-start.3 = ((bf16[8,128,640]{1,2,0:T(8,128)(2,1)}), bf16[8,128,640]{1,2,0:T(8,128)(2,1)S(1)}, u32[]{:S(2)}, u32[]{:S(2)}) async-start(bf16[8,128,640]{1,2,0:T(8,128)(2,1)} %copy.90), calls=%async_computation.3 | async-start | bytes 2621440 | tf_op jit(solution)/shard_map/all_to_all | solution.py:225
  141.0 46.0 %all-to-all-start.4 = ((bf16[64,2,256]{2,1,0:T(2,128)(2,1)}), bf16[64,2,256]{2,1,0:T(2,128)(2,1)S(1)}, u32[]{:S(2)}, u32[]{:S(2)}) async-start(bf16[64,2,256]{2,1,0:T(2,128)(2,1)} %reshape.166), calls=%async_computation.4 | async-start | bytes 131072 | tf_op jit(solution)/shard_map/all_to_all | solution.py:160
  189.1 14.6 %all-to-all-start.5 = ((bf16[64,2,256]{2,1,0:T(2,128)(2,1)}), bf16[64,2,256]{2,1,0:T(2,128)(2,1)S(1)}, u32[]{:S(2)}, u32[]{:S(2)}) async-start(bf16[64,2,256]{2,1,0:T(2,128)(2,1)} %reshape.168), calls=%async_computation.5 | async-start | bytes 131072 | tf_op jit(solution)/shard_map/all_to_all | solution.py:162

commit v5 on v4

--- a/solution.py
+++ b/solution.py
@@ -154,21 +154,15 @@
     )(seg_row, seg_col, gathered, gathered, gathered, gathered)
 
 
-def route(payload, order):
+def route(block, order, heads):
     prompt_count = lax.axis_size("dp")
-    flat = payload.reshape(prompt_count, -1)
+    rows = block.shape[0]
+    flat = block.reshape(prompt_count, rows // prompt_count, KEY_VALUE_HEADS, HEAD_WIDTH)
     spread = lax.all_to_all(flat, "dp", 0, 0, tiled=True)
     routed = jnp.take(spread, order, axis=0)
+    routed = jnp.take_along_axis(routed, heads[:, None, :, None], axis=2)
     back = lax.all_to_all(routed, "dp", 0, 0, tiled=True)
-    return back.reshape(payload.shape)
-
-
-def pick_heads(block, heads):
-    parts = [
-        lax.dynamic_slice_in_dim(block, heads[k] * HEAD_WIDTH, HEAD_WIDTH, 1)
-        for k in range(KNOCKOUT_COUNT)
-    ]
-    return jnp.stack(parts, axis=1)
+    return back.reshape(rows, KNOCKOUT_COUNT, HEAD_WIDTH)
 
 
 def per_device(queries, keys, values, output_gradient, seg_lengths, knocked, source):
@@ -185,8 +179,7 @@
     their_knock = knocked[consumer[prompt_index]]
     head_ids = jnp.arange(KEY_VALUE_HEADS, dtype=jnp.int32)[None, :, None]
 
-    outgoing = pick_heads(keys, their_knock)
-    fetched = route(outgoing, source)
+    fetched = route(keys, source, knocked)
     keys3 = keys.reshape(tok_rows, KEY_VALUE_HEADS, HEAD_WIDTH)
     used3 = keys3
     for k in range(KNOCKOUT_COUNT - 1, -1, -1):
@@ -229,8 +222,7 @@
     value_out = low_back[:, :, widths[0] : v_end].reshape(tok_rows, -1)
     key_back = low_back[:, :, v_end:].reshape(tok_rows, -1)
 
-    returning = pick_heads(key_back, my_knock)
-    returned = route(returning, consumer)
+    returned = route(key_back, consumer, knocked[consumer])
     key3 = key_back.reshape(tok_rows, KEY_VALUE_HEADS, HEAD_WIDTH)
     own = key3
     for k in range(KNOCKOUT_COUNT):

time: 206 us -> 208 us (level)
  starting transfers between devices: 74.8 us -> 79.1 us
  between operations: 5.57 us -> 2.87 us
  waiting for transfers between devices: 86.2 us -> 83.8 us
  other arithmetic: 10.3 us -> 12.6 us
    all_to_all x2, starting transfers between devices: 8.89 us -> 13.2 us  [route(): back = lax.all_to_all(routed, 'dp', 0, 0, tiled=True)]
    all_to_all x8 -> x0, other arithmetic: 3.83 us -> none  [the longest x6 2.01 us: route(): back = lax.all_to_all(routed, 'dp', 0, 0, tiled=True)]
    gather x0 -> x8, local copies, waits for them, and re-layouts: none -> 2.9 us  [the longest x6 2.23 us: route(): routed = jnp.take_along_axis(routed, heads[:, None, :, None], axis=2)]
    all_to_all x2, waiting for transfers between devices: 17.8 us -> 15.2 us  [route(): spread = lax.all_to_all(flat, 'dp', 0, 0, tiled=True)]
    unnamed x24 -> x13, local copies, waits for them, and re-layouts: 5.89 us -> 4.43 us
  transfers between devices with their start and end apart: 6 -> 6, of which waited for: 6 -> 6; matrix products, arithmetic and copies ran while one was open for 4% -> 6% of each run, Pallas kernels for 0% -> 0%
where the time goes in v5:
time: 208 us; the launch traced here: 207 us
  waiting for transfers between devices  83.8 us (40%)
  starting transfers between devices  79.1 us (38%)
  local copies, waits for them, and re-layouts  15 us (7%)
  Pallas kernels  13.5 us (6%)
  other arithmetic  12.6 us (6%)
  between operations  2.87 us (1%)
    all_to_all x2, starting transfers between devices, route(): spread = lax.all_to_all(flat, 'dp', 0, 0, tiled=True)  50.6 us
    all_to_all x1, waiting for transfers between devices, per_device(): lax.all_to_all(packed, 'seq', split_axis=1, concat_axis=0, tiled=True)  38.5 us
    all_to_all x2, waiting for transfers between devices, route(): back = lax.all_to_all(routed, 'dp', 0, 0, tiled=True)  15.7 us
    all_to_all x2, waiting for transfers between devices, route(): spread = lax.all_to_all(flat, 'dp', 0, 0, tiled=True)  15.2 us
    all_to_all x1, waiting for transfers between devices, per_device(): lax.all_to_all(low, 'seq', split_axis=0, concat_axis=1, tiled=True)  14.5 us
    pallas_call x1, Pallas kernels, attend_back_kernel(): pl.pallas_call(attend_kernel, grid=(heads_of_query,), in_specs=[pl.BlockS...  13.5 us
    all_to_all x2, starting transfers between devices, route(): back = lax.all_to_all(routed, 'dp', 0, 0, tiled=True)  13.2 us
    all_to_all x1, starting transfers between devices, per_device(): lax.all_to_all(packed, 'seq', split_axis=1, concat_axis=0, tiled=True)  9.9 us
  transfers between devices with their start and end apart: 6, of which 6 were waited for; matrix products, arithmetic and copies ran while one was open for 6% of the time, Pallas kernels for 0%

profile of v5, /device:TPU:1, one launch (start us, length us, event | category | flops | bytes accessed | tf_op | source)
XLA Modules:
  0.0 207.0 jit_solution(9045860235547852611)
XLA Ops:
  0.7 1.8 copy.122
  2.4 14.6 %all-to-all-start = ((bf16[64,2,8,128]{3,2,1,0:T(8,128)(2,1)}), bf16[64,2,8,128]{3,2,1,0:T(8,128)(2,1)S(1)}, u32[]{:S(2)}, u32[]{:S(2)}) async-start(bf16[64,2,8,128]{3,2,1,0:T(8,128)(2,1)} %bitcast.43), calls=%async_computation | async-start | bytes 524288 | tf_op jit(solution)/shard_map/all_to_all | solution.py:161
  17.0 0.8 select_reduce_fusion
  17.8 0.6 dynamic_slice.10
  19.7 0.7 compare_select_fusion.3
  20.4 0.7 bitcast_or_fusion.1
  21.0 0.7 and_bitcast_fusion.1
  22.4 0.8 constant_dynamic-slice_fusion
  23.6 0.6 fusion.5
  24.2 0.7 compare_and_fusion.1
  24.9 1.4 copy_bitcast_fusion.1
  26.3 3.0 %all-to-all-done = bf16[64,2,8,128]{3,2,1,0:T(8,128)(2,1)S(1)} async-done(((bf16[64,2,8,128]{3,2,1,0:T(8,128)(2,1)}), bf16[64,2,8,128]{3,2,1,0:T(8,128)(2,1)S(1)}, u32[]{:S(2)}, u32[]{:S(2)}) %all-to-all-start) | async-done | bytes 262176 | tf_op jit(solution)/shard_map/all_to_all | solution.py:161
  29.3 0.6 gather_fusion.1
  30.0 0.2 copy.105
  30.3 0.9 gather_fusion.2
  31.1 0.8 fusion.1
  32.0 7.7 %all-to-all-start.1 = ((bf16[64,2,2,128]{3,1,2,0:T(2,128)(2,1)}), bf16[64,2,2,128]{3,1,2,0:T(2,128)(2,1)S(1)}, u32[]{:S(2)}, u32[]{:S(2)}) async-start(bf16[64,2,2,128]{3,1,2,0:T(2,128)(2,1)} %fusion.1), calls=%async_computation.1 | async-start | bytes 131072 | tf_op jit(solution)/shard_map/all_to_all | solution.py:164
  39.7 0.6 iota_compare_fusion.4
  40.3 0.6 iota_compare_fusion.5
  41.0 8.8 %all-to-all-done.1 = bf16[64,2,2,128]{3,1,2,0:T(2,128)(2,1)S(1)} async-done(((bf16[64,2,2,128]{3,1,2,0:T(2,128)(2,1)}), bf16[64,2,2,128]{3,1,2,0:T(2,128)(2,1)S(1)}, u32[]{:S(2)}, u32[]{:S(2)}) %all-to-all-start.1) | async-done | bytes 65568 | tf_op jit(solution)/shard_map/all_to_all | solution.py:164
  49.8 1.1 fusion
  50.9 1.7 pad_maximum_fusion
  52.6 9.9 %all-to-all-start.2 = ((bf16[128,8,1024]{2,0,1:T(8,128)(2,1)}), bf16[128,8,1024]{2,0,1:T(8,128)(2,1)S(1)}, u32[]{:S(2)}, u32[]{:S(2)}) async-start(bf16[128,8,1024]{2,0,1:T(8,128)(2,1)} %pad_maximum_fusion), calls=%async_computation.2 | async-start | bytes 4194304 | tf_op jit(solution)/shard_map/all_to_all | solution.py:201
  62.5 0.2 reduce-window.8
  62.7 0.2 copy.111.seg_row_ref
  63.0 38.5 %all-to-all-done.2 = bf16[128,8,1024]{2,0,1:T(8,128)(2,1)S(1)} async-done(((bf16[128,8,1024]{2,0,1:T(8,128)(2,1)}), bf16[128,8,1024]{2,0,1:T(8,128)(2,1)S(1)}, u32[]{:S(2)}, u32[]{:S(2)}) %all-to-all-start.2) | async-done | bytes 2097184 | tf_op jit(solution)/shard_map/all_to_all | solution.py:201
  101.4 13.5 %shard_map.94 = (bf16[1024,384]{1,0:T(8,128)(2,1)S(1)}, f32[1024,128]{1,0:T(8,128)S(1)}, f32[1024,128]{1,0:T(8,128)S(1)}) custom-call(s32[1024,1]{1,0:T(8,128)S(1)} %copy.111.seg_row_ref, s32[1,1024]{1,0:T(1,128)S(1)} %bitcast.97, bf16[1024,1024]{1,0:T(8,128)(2,1)S(1)} %bitcast.92, bf16[1024,1024]{1,0:T(8,128)(2,1)S(1)} %bitcast.93, ...), custom_call_target="tpu_custom_call" | custom-call | flops 2516582400 | bytes 3932160 | tf_op jit(solution)/shard_map/pallas_call | solution.py:125
  115.0 1.2 pad_maximum_fusion.1
  116.2 5.5 %all-to-all-start.3 = ((bf16[8,128,640]{2,1,0:T(8,128)(2,1)}), bf16[8,128,640]{2,1,0:T(8,128)(2,1)S(1)}, u32[]{:S(2)}, u32[]{:S(2)}) async-start(bf16[8,128,640]{2,1,0:T(8,128)(2,1)} %bitcast.17), calls=%async_computation.3 | async-start | bytes 2621440 | tf_op jit(solution)/shard_map/all_to_all | solution.py:218
  121.8 0.6 gather_fusion
  122.6 0.1 reshape.214
  122.8 14.5 %all-to-all-done.3 = bf16[8,128,640]{2,1,0:T(8,128)(2,1)S(1)} async-done(((bf16[8,128,640]{2,1,0:T(8,128)(2,1)}), bf16[8,128,640]{2,1,0:T(8,128)(2,1)S(1)}, u32[]{:S(2)}, u32[]{:S(2)}) %all-to-all-start.3) | async-done | bytes 1310752 | tf_op jit(solution)/shard_map/all_to_all | solution.py:218
  137.4 0.7 copy.133
  138.2 0.9 copy.116
  139.1 36.0 %all-to-all-start.4 = ((bf16[64,2,8,128]{3,1,2,0:T(2,128)(2,1)}), bf16[64,2,8,128]{3,1,2,0:T(2,128)(2,1)S(1)}, u32[]{:S(2)}, u32[]{:S(2)}) async-start(bf16[64,2,8,128]{3,1,2,0:T(2,128)(2,1)} %copy.116), calls=%async_computation.4 | async-start | bytes 524288 | tf_op jit(solution)/shard_map/all_to_all | solution.py:161
  175.1 12.2 %all-to-all-done.4 = bf16[64,2,8,128]{3,1,2,0:T(2,128)(2,1)S(1)} async-done(((bf16[64,2,8,128]{3,1,2,0:T(2,128)(2,1)}), bf16[64,2,8,128]{3,1,2,0:T(2,128)(2,1)S(1)}, u32[]{:S(2)}, u32[]{:S(2)}) %all-to-all-start.4) | async-done | bytes 262176 | tf_op jit(solution)/shard_map/all_to_all | solution.py:161
  187.3 1.1 gather_fusion.3
  188.4 0.3 broadcast_select_fusion
  188.8 0.9 gather_fusion.4
  189.6 0.8 fusion.2
  190.5 5.5 %all-to-all-start.5 = ((bf16[64,2,2,128]{3,1,2,0:T(2,128)(2,1)}), bf16[64,2,2,128]{3,1,2,0:T(2,128)(2,1)S(1)}, u32[]{:S(2)}, u32[]{:S(2)}) async-start(bf16[64,2,2,128]{3,1,2,0:T(2,128)(2,1)} %fusion.2), calls=%async_computation.5 | async-start | bytes 131072 | tf_op jit(solution)/shard_map/all_to_all | solution.py:164
  195.9 0.6 iota_compare_fusion.2
  196.6 0.7 iota_compare_fusion.3
  197.3 1.0 copy.124
  198.3 0.8 copy.134
  199.1 6.9 %all-to-all-done.5 = bf16[64,2,2,128]{3,1,2,0:T(2,128)(2,1)S(1)} async-done(((bf16[64,2,2,128]{3,1,2,0:T(2,128)(2,1)}), bf16[64,2,2,128]{3,1,2,0:T(2,128)(2,1)S(1)}, u32[]{:S(2)}, u32[]{:S(2)}) %all-to-all-start.5) | async-done | bytes 65568 | tf_op jit(solution)/shard_map/all_to_all | solution.py:164
  206.0 0.2 add_convert_fusion
  206.2 0.8 copy.135
  (35 shorter events, 1.4 us)
Async XLA Ops:
  0.6 22.9 %copy-start = (bf16[128,1024]{1,0:T(8,128)(2,1)S(1)}, bf16[128,1024]{1,0:T(8,128)(2,1)}, u32[]{:S(2)}) copy-start(bf16[128,1024]{1,0:T(8,128)(2,1)} %param.13) | copy-start | bytes 786436
  0.6 24.2 %copy-start.1 = (bf16[128,3072]{1,0:T(8,128)(2,1)S(1)}, bf16[128,3072]{1,0:T(8,128)(2,1)}, u32[]{:S(2)}) copy-start(bf16[128,3072]{1,0:T(8,128)(2,1)} %param.14) | copy-start | bytes 2359300
  2.4 26.8 %all-to-all-start = ((bf16[64,2,8,128]{3,2,1,0:T(8,128)(2,1)}), bf16[64,2,8,128]{3,2,1,0:T(8,128)(2,1)S(1)}, u32[]{:S(2)}, u32[]{:S(2)}) async-start(bf16[64,2,8,128]{3,2,1,0:T(8,128)(2,1)} %bitcast.43), calls=%async_computation | async-start | bytes 524288 | tf_op jit(solution)/shard_map/all_to_all | solution.py:161
  32.0 17.8 %all-to-all-start.1 = ((bf16[64,2,2,128]{3,1,2,0:T(2,128)(2,1)}), bf16[64,2,2,128]{3,1,2,0:T(2,128)(2,1)S(1)}, u32[]{:S(2)}, u32[]{:S(2)}) async-start(bf16[64,2,2,128]{3,1,2,0:T(2,128)(2,1)} %fusion.1), calls=%async_computation.1 | async-start | bytes 131072 | tf_op jit(solution)/shard_map/all_to_all | solution.py:164
  52.6 9.9 %copy-start.3 = (s32[1,4]{1,0:T(1,128)S(1)}, s32[1,4]{1,0:T(1,128)}, u32[]{:S(2)}) copy-start(s32[1,4]{1,0:T(1,128)} %param.15) | copy-start | bytes 52
  52.6 48.9 %all-to-all-start.2 = ((bf16[128,8,1024]{2,0,1:T(8,128)(2,1)}), bf16[128,8,1024]{2,0,1:T(8,128)(2,1)S(1)}, u32[]{:S(2)}, u32[]{:S(2)}) async-start(bf16[128,8,1024]{2,0,1:T(8,128)(2,1)} %pad_maximum_fusion), calls=%async_computation.2 | async-start | bytes 4194304 | tf_op jit(solution)/shard_map/all_to_all | solution.py:201
  115.0 6.7 %copy-start.2 = (s32[64,2]{0,1:T(2,128)S(1)}, s32[64,2]{0,1:T(2,128)}, u32[]{:S(2)}) copy-start(s32[64,2]{0,1:T(2,128)} %param.16) | copy-start | bytes 1540
  116.2 21.2 %all-to-all-start.3 = ((bf16[8,128,640]{2,1,0:T(8,128)(2,1)}), bf16[8,128,640]{2,1,0:T(8,128)(2,1)S(1)}, u32[]{:S(2)}, u32[]{:S(2)}) async-start(bf16[8,128,640]{2,1,0:T(8,128)(2,1)} %bitcast.17), calls=%async_computation.3 | async-start | bytes 2621440 | tf_op jit(solution)/shard_map/all_to_all | solution.py:218
  139.1 48.3 %all-to-all-start.4 = ((bf16[64,2,8,128]{3,1,2,0:T(2,128)(2,1)}), bf16[64,2,8,128]{3,1,2,0:T(2,128)(2,1)S(1)}, u32[]{:S(2)}, u32[]{:S(2)}) async-start(bf16[64,2,8,128]{3,1,2,0:T(2,128)(2,1)} %copy.116), calls=%async_computation.4 | async-start | bytes 524288 | tf_op jit(solution)/shard_map/all_to_all | solution.py:161
  190.5 15.5 %all-to-all-start.5 = ((bf16[64,2,2,128]{3,1,2,0:T(2,128)(2,1)}), bf16[64,2,2,128]{3,1,2,0:T(2,128)(2,1)S(1)}, u32[]{:S(2)}, u32[]{:S(2)}) async-start(bf16[64,2,2,128]{3,1,2,0:T(2,128)(2,1)} %fusion.2), calls=%async_computation.5 | async-start | bytes 131072 | tf_op jit(solution)/shard_map/all_to_all | solution.py:164

commit v6 on v4

--- a/solution.py
+++ b/solution.py
@@ -68,7 +68,7 @@
     return lax.fori_loop(0, heads_of_query, one_head, initial)
 
 
-BLOCK_ROWS = 256
+BLOCK_ROWS = 128
 
 
 def attend_kernel(seg_row_ref, seg_col_ref, q_ref, g_ref, k_ref, v_ref, dq_ref, dk_ref, dv_ref):
@@ -97,7 +97,7 @@
         scores = jnp.where(visible, scores, masked_score)
         row_max = jnp.max(scores, axis=1, keepdims=True)
         weights = jnp.exp(scores - row_max)
-        probs = weights / jnp.sum(weights, axis=1, keepdims=True)
+        probs = weights * (1.0 / jnp.sum(weights, axis=1, keepdims=True))
         probs_low = probs.astype(jnp.bfloat16)
         dv_ref[0:span, :] += lax.dot_general(
             probs_low, g_rows, (((0,), (0,)), ((), ())), preferred_element_type=jnp.float32
@@ -121,7 +121,7 @@
     seg_col = segment.reshape(1, length)
     full = lambda h: (0, 0)
     col = lambda b: pl.BlockSpec((length, HEAD_WIDTH), lambda h: (0, b))
-    flops = 5 * 2 * length * length * HEAD_WIDTH * heads_of_query * 10 // 16
+    flops = 5 * 2 * length * length * HEAD_WIDTH * heads_of_query * 9 // 16
     return pl.pallas_call(
         attend_kernel,
         grid=(heads_of_query,),
@@ -148,7 +148,7 @@
         ),
         cost_estimate=pl.CostEstimate(
             flops=flops,
-            transcendentals=length * length * heads_of_query * 10 // 16,
+            transcendentals=length * length * heads_of_query * 9 // 16,
             bytes_accessed=length * HEAD_WIDTH * (2 * 2 * heads_of_query + 2 * 2 + 2 * heads_of_query + 8),
         ),
     )(seg_row, seg_col, gathered, gathered, gathered, gathered)

time: 206 us -> 209 us (1.015)
  Pallas kernels: 13.5 us -> 16 us
    pallas_call x1, Pallas kernels: 13.5 us -> 16 us  [attend_back_kernel(): pl.pallas_call(attend_kernel, grid=(heads_of_query,), in_specs=[pl.BlockS...]
where the time goes in v6:
time: 209 us; the launch traced here: 208 us
  waiting for transfers between devices  86.2 us (41%)
  starting transfers between devices  74.8 us (36%)
  Pallas kernels  16 us (8%)
  local copies, waits for them, and re-layouts  15.1 us (7%)
  other arithmetic  10.3 us (5%)
  between operations  5.57 us (3%)
    all_to_all x2, starting transfers between devices, route(): spread = lax.all_to_all(flat, 'dp', 0, 0, tiled=True)  50.6 us
    all_to_all x1, waiting for transfers between devices, per_device(): lax.all_to_all(packed, 'seq', split_axis=1, concat_axis=0, tiled=True)  38.5 us
    all_to_all x2, waiting for transfers between devices, route(): spread = lax.all_to_all(flat, 'dp', 0, 0, tiled=True)  17.8 us
    pallas_call x1, Pallas kernels, attend_back_kernel(): pl.pallas_call(attend_kernel, grid=(heads_of_query,), in_specs=[pl.BlockS...  16 us
    all_to_all x2, waiting for transfers between devices, route(): back = lax.all_to_all(routed, 'dp', 0, 0, tiled=True)  15.4 us
    all_to_all x1, waiting for transfers between devices, per_device(): lax.all_to_all(low, 'seq', split_axis=0, concat_axis=1, tiled=True)  14.4 us
    all_to_all x1, starting transfers between devices, per_device(): lax.all_to_all(packed, 'seq', split_axis=1, concat_axis=0, tiled=True)  9.9 us
    all_to_all x2, starting transfers between devices, route(): back = lax.all_to_all(routed, 'dp', 0, 0, tiled=True)  8.89 us
  transfers between devices with their start and end apart: 6, of which 6 were waited for; matrix products, arithmetic and copies ran while one was open for 4% of the time, Pallas kernels for 0%

profile of v6, /device:TPU:1, one launch (start us, length us, event | category | flops | bytes accessed | tf_op | source)
XLA Modules:
  0.0 208.1 jit_solution(14472910835158749587)
XLA Ops:
  0.7 0.8 select_reduce_fusion
  1.5 0.6 dynamic_slice.22
  4.0 0.8 constant_dynamic-slice_fusion.2
  4.9 0.6 fusion.3
  6.7 0.8 dynamic-slice_bitcast_fusion.1
  7.6 0.5 broadcast.39
  8.1 0.9 reduce.2
  9.0 0.6 reshape.162
  9.7 14.6 %all-to-all-start = ((bf16[64,2,256]{2,1,0:T(2,128)(2,1)}), bf16[64,2,256]{2,1,0:T(2,128)(2,1)S(1)}, u32[]{:S(2)}, u32[]{:S(2)}) async-start(bf16[64,2,256]{2,1,0:T(2,128)(2,1)} %reshape.162), calls=%async_computation | async-start | bytes 131072 | tf_op jit(solution)/shard_map/all_to_all | solution.py:160
  24.3 0.7 compare_and_fusion
  25.0 1.4 copy_bitcast_fusion
  26.4 7.8 %all-to-all-done = bf16[64,2,256]{2,1,0:T(2,128)(2,1)S(1)} async-done(((bf16[64,2,256]{2,1,0:T(2,128)(2,1)}), bf16[64,2,256]{2,1,0:T(2,128)(2,1)S(1)}, u32[]{:S(2)}, u32[]{:S(2)}) %all-to-all-start) | async-done | bytes 65568 | tf_op jit(solution)/shard_map/all_to_all | solution.py:160
  34.4 0.7 gather_fusion
  35.1 0.6 reduce.3
  35.7 0.6 reshape.164
  36.4 4.4 %all-to-all-start.1 = ((bf16[64,2,256]{2,1,0:T(2,128)(2,1)}), bf16[64,2,256]{2,1,0:T(2,128)(2,1)S(1)}, u32[]{:S(2)}, u32[]{:S(2)}) async-start(bf16[64,2,256]{2,1,0:T(2,128)(2,1)} %reshape.164), calls=%async_computation.1 | async-start | bytes 131072 | tf_op jit(solution)/shard_map/all_to_all | solution.py:162
  40.8 0.7 iota_compare_fusion.4
  41.5 0.2 copy.84
  41.7 0.6 iota_compare_fusion.5
  42.3 8.7 %all-to-all-done.1 = bf16[64,2,256]{2,1,0:T(2,128)(2,1)S(1)} async-done(((bf16[64,2,256]{2,1,0:T(2,128)(2,1)}), bf16[64,2,256]{2,1,0:T(2,128)(2,1)S(1)}, u32[]{:S(2)}, u32[]{:S(2)}) %all-to-all-start.1) | async-done | bytes 65568 | tf_op jit(solution)/shard_map/all_to_all | solution.py:162
  51.0 0.4 reduce
  51.9 0.2 copy.87
  52.1 1.7 pad_maximum_fusion
  53.7 9.9 %all-to-all-start.2 = ((bf16[128,8,1024]{2,0,1:T(8,128)(2,1)}), bf16[128,8,1024]{2,0,1:T(8,128)(2,1)S(1)}, u32[]{:S(2)}, u32[]{:S(2)}) async-start(bf16[128,8,1024]{2,0,1:T(8,128)(2,1)} %pad_maximum_fusion), calls=%async_computation.2 | async-start | bytes 4194304 | tf_op jit(solution)/shard_map/all_to_all | solution.py:208
  63.6 0.2 reduce-window.8
  63.9 0.2 copy.89.seg_row_ref
  64.1 38.5 %all-to-all-done.2 = bf16[128,8,1024]{2,0,1:T(8,128)(2,1)S(1)} async-done(((bf16[128,8,1024]{2,0,1:T(8,128)(2,1)}), bf16[128,8,1024]{2,0,1:T(8,128)(2,1)S(1)}, u32[]{:S(2)}, u32[]{:S(2)}) %all-to-all-start.2) | async-done | bytes 2097184 | tf_op jit(solution)/shard_map/all_to_all | solution.py:208
  102.6 16.0 %shard_map.94 = (bf16[1024,384]{1,0:T(8,128)(2,1)S(1)}, f32[1024,128]{1,0:T(8,128)S(1)}, f32[1024,128]{1,0:T(8,128)S(1)}) custom-call(s32[1024,1]{1,0:T(8,128)S(1)} %copy.89.seg_row_ref, s32[1,1024]{1,0:T(1,128)S(1)} %bitcast.57, bf16[1024,1024]{1,0:T(8,128)(2,1)S(1)} %bitcast.52, bf16[1024,1024]{1,0:T(8,128)(2,1)S(1)} %bitcast.53, ...), custom_call_target="tpu_custom_call" | custom-call | flops 2264924160 | bytes 3932160 | tf_op jit(solution)/shard_map/pallas_call | solution.py:125
  118.7 0.1 pad_maximum_fusion.1
  118.8 1.5 copy.90
  120.3 5.5 %all-to-all-start.3 = ((bf16[8,128,640]{1,2,0:T(8,128)(2,1)}), bf16[8,128,640]{1,2,0:T(8,128)(2,1)S(1)}, u32[]{:S(2)}, u32[]{:S(2)}) async-start(bf16[8,128,640]{1,2,0:T(8,128)(2,1)} %copy.90), calls=%async_computation.3 | async-start | bytes 2621440 | tf_op jit(solution)/shard_map/all_to_all | solution.py:225
  127.1 14.4 %all-to-all-done.3 = bf16[8,128,640]{1,2,0:T(8,128)(2,1)S(1)} async-done(((bf16[8,128,640]{1,2,0:T(8,128)(2,1)}), bf16[8,128,640]{1,2,0:T(8,128)(2,1)S(1)}, u32[]{:S(2)}, u32[]{:S(2)}) %all-to-all-start.3) | async-done | bytes 1310752 | tf_op jit(solution)/shard_map/all_to_all | solution.py:225
  141.9 0.9 reduce.4
  142.8 0.6 reshape.166
  143.5 36.0 %all-to-all-start.4 = ((bf16[64,2,256]{2,1,0:T(2,128)(2,1)}), bf16[64,2,256]{2,1,0:T(2,128)(2,1)S(1)}, u32[]{:S(2)}, u32[]{:S(2)}) async-start(bf16[64,2,256]{2,1,0:T(2,128)(2,1)} %reshape.166), calls=%async_computation.4 | async-start | bytes 131072 | tf_op jit(solution)/shard_map/all_to_all | solution.py:160
  179.5 10.0 %all-to-all-done.4 = bf16[64,2,256]{2,1,0:T(2,128)(2,1)S(1)} async-done(((bf16[64,2,256]{2,1,0:T(2,128)(2,1)}), bf16[64,2,256]{2,1,0:T(2,128)(2,1)S(1)}, u32[]{:S(2)}, u32[]{:S(2)}) %all-to-all-start.4) | async-done | bytes 65568 | tf_op jit(solution)/shard_map/all_to_all | solution.py:160
  189.6 0.7 gather_fusion.1
  190.4 0.6 reduce.5
  191.0 0.6 reshape.168
  191.6 4.4 %all-to-all-start.5 = ((bf16[64,2,256]{2,1,0:T(2,128)(2,1)}), bf16[64,2,256]{2,1,0:T(2,128)(2,1)S(1)}, u32[]{:S(2)}, u32[]{:S(2)}) async-start(bf16[64,2,256]{2,1,0:T(2,128)(2,1)} %reshape.168), calls=%async_computation.5 | async-start | bytes 131072 | tf_op jit(solution)/shard_map/all_to_all | solution.py:162
  196.1 0.7 iota_compare_fusion.2
  196.7 0.6 iota_compare_fusion.3
  197.4 1.2 copy.98
  198.6 0.8 copy.100
  199.4 6.8 %all-to-all-done.5 = bf16[64,2,256]{2,1,0:T(2,128)(2,1)S(1)} async-done(((bf16[64,2,256]{2,1,0:T(2,128)(2,1)}), bf16[64,2,256]{2,1,0:T(2,128)(2,1)S(1)}, u32[]{:S(2)}, u32[]{:S(2)}) %all-to-all-start.5) | async-done | bytes 65568 | tf_op jit(solution)/shard_map/all_to_all | solution.py:162
  206.3 0.4 reduce.1
  207.0 0.2 add_convert_fusion
  207.2 0.9 copy.99
  (46 shorter events, 2.0 us)
Async XLA Ops:
  0.6 24.3 %copy-start = (bf16[128,1024]{1,0:T(8,128)(2,1)S(1)}, bf16[128,1024]{1,0:T(8,128)(2,1)}, u32[]{:S(2)}) copy-start(bf16[128,1024]{1,0:T(8,128)(2,1)} %param.11) | copy-start | bytes 786436
  0.6 24.3 %copy-start.1 = (bf16[128,3072]{1,0:T(8,128)(2,1)S(1)}, bf16[128,3072]{1,0:T(8,128)(2,1)}, u32[]{:S(2)}) copy-start(bf16[128,3072]{1,0:T(8,128)(2,1)} %param.12) | copy-start | bytes 2359300
  7.6 18.8 %copy-start.3 = (s32[64]{0:T(128)S(1)}, s32[64]{0:T(128)}, u32[]{:S(2)}) copy-start(s32[64]{0:T(128)} %param.15) | copy-start | bytes 772
  9.7 24.6 %all-to-all-start = ((bf16[64,2,256]{2,1,0:T(2,128)(2,1)}), bf16[64,2,256]{2,1,0:T(2,128)(2,1)S(1)}, u32[]{:S(2)}, u32[]{:S(2)}) async-start(bf16[64,2,256]{2,1,0:T(2,128)(2,1)} %reshape.162), calls=%async_computation | async-start | bytes 131072 | tf_op jit(solution)/shard_map/all_to_all | solution.py:160
  25.0 16.5 %copy-start.2 = (bf16[128,1024]{1,0:T(8,128)(2,1)S(1)}, bf16[128,1024]{1,0:T(8,128)(2,1)}, u32[]{:S(2)}) copy-start(bf16[128,1024]{1,0:T(8,128)(2,1)} %param.10) | copy-start | bytes 786436
  36.4 14.6 %all-to-all-start.1 = ((bf16[64,2,256]{2,1,0:T(2,128)(2,1)}), bf16[64,2,256]{2,1,0:T(2,128)(2,1)S(1)}, u32[]{:S(2)}, u32[]{:S(2)}) async-start(bf16[64,2,256]{2,1,0:T(2,128)(2,1)} %reshape.164), calls=%async_computation.1 | async-start | bytes 131072 | tf_op jit(solution)/shard_map/all_to_all | solution.py:162
  53.7 9.9 %copy-start.4 = (s32[1,4]{1,0:T(1,128)S(1)}, s32[1,4]{1,0:T(1,128)}, u32[]{:S(2)}) copy-start(s32[1,4]{1,0:T(1,128)} %param.13) | copy-start | bytes 52
  53.7 48.9 %all-to-all-start.2 = ((bf16[128,8,1024]{2,0,1:T(8,128)(2,1)}), bf16[128,8,1024]{2,0,1:T(8,128)(2,1)S(1)}, u32[]{:S(2)}, u32[]{:S(2)}) async-start(bf16[128,8,1024]{2,0,1:T(8,128)(2,1)} %pad_maximum_fusion), calls=%async_computation.2 | async-start | bytes 4194304 | tf_op jit(solution)/shard_map/all_to_all | solution.py:208
  120.3 21.2 %all-to-all-start.3 = ((bf16[8,128,640]{1,2,0:T(8,128)(2,1)}), bf16[8,128,640]{1,2,0:T(8,128)(2,1)S(1)}, u32[]{:S(2)}, u32[]{:S(2)}) async-start(bf16[8,128,640]{1,2,0:T(8,128)(2,1)} %copy.90), calls=%async_computation.3 | async-start | bytes 2621440 | tf_op jit(solution)/shard_map/all_to_all | solution.py:225
  143.5 46.1 %all-to-all-start.4 = ((bf16[64,2,256]{2,1,0:T(2,128)(2,1)}), bf16[64,2,256]{2,1,0:T(2,128)(2,1)S(1)}, u32[]{:S(2)}, u32[]{:S(2)}) async-start(bf16[64,2,256]{2,1,0:T(2,128)(2,1)} %reshape.166), calls=%async_computation.4 | async-start | bytes 131072 | tf_op jit(solution)/shard_map/all_to_all | solution.py:160
  191.6 14.6 %all-to-all-start.5 = ((bf16[64,2,256]{2,1,0:T(2,128)(2,1)}), bf16[64,2,256]{2,1,0:T(2,128)(2,1)S(1)}, u32[]{:S(2)}, u32[]{:S(2)}) async-start(bf16[64,2,256]{2,1,0:T(2,128)(2,1)} %reshape.168), calls=%async_computation.5 | async-start | bytes 131072 | tf_op jit(solution)/shard_map/all_to_all | solution.py:162

commit v7 on v4

--- a/solution.py
+++ b/solution.py
@@ -88,31 +88,27 @@
         q_rows = q_ref[rows, :]
         g_rows = g_ref[rows, :]
         scores = lax.dot_general(
-            q_rows, keys, (((1,), (1,)), ((), ())), preferred_element_type=jnp.float32
+            keys, q_rows, (((1,), (1,)), ((), ())), preferred_element_type=jnp.float32
         ) * scaling
-        row_pos = block * BLOCK_ROWS + lax.broadcasted_iota(jnp.int32, (BLOCK_ROWS, span), 0)
-        col_pos = lax.broadcasted_iota(jnp.int32, (BLOCK_ROWS, span), 1)
-        same = seg_row_ref[rows, :] == seg_col_ref[:, 0:span]
-        visible = jnp.logical_and(row_pos >= col_pos, same)
+        key_pos = lax.broadcasted_iota(jnp.int32, (span, BLOCK_ROWS), 0)
+        query_pos = block * BLOCK_ROWS + lax.broadcasted_iota(jnp.int32, (span, BLOCK_ROWS), 1)
+        same = seg_row_ref[0:span, :] == seg_col_ref[:, rows]
+        visible = jnp.logical_and(query_pos >= key_pos, same)
         scores = jnp.where(visible, scores, masked_score)
-        row_max = jnp.max(scores, axis=1, keepdims=True)
-        weights = jnp.exp(scores - row_max)
-        probs = weights / jnp.sum(weights, axis=1, keepdims=True)
+        col_max = jnp.max(scores, axis=0, keepdims=True)
+        weights = jnp.exp(scores - col_max)
+        probs = weights / jnp.sum(weights, axis=0, keepdims=True)
         probs_low = probs.astype(jnp.bfloat16)
-        dv_ref[0:span, :] += lax.dot_general(
-            probs_low, g_rows, (((0,), (0,)), ((), ())), preferred_element_type=jnp.float32
-        )
+        dv_ref[0:span, :] += jnp.dot(probs_low, g_rows, preferred_element_type=jnp.float32)
         prob_grads = lax.dot_general(
-            g_rows, vals, (((1,), (1,)), ((), ())), preferred_element_type=jnp.float32
-        )
-        row_delta = jnp.sum(probs * prob_grads, axis=1, keepdims=True)
-        score_grads = (probs * (prob_grads - row_delta) * scaling).astype(jnp.bfloat16)
-        dq_ref[rows, :] = jnp.dot(
-            score_grads, keys, preferred_element_type=jnp.float32
+            vals, g_rows, (((1,), (1,)), ((), ())), preferred_element_type=jnp.float32
+        )
+        col_delta = jnp.sum(probs * prob_grads, axis=0, keepdims=True)
+        score_grads = (probs * (prob_grads - col_delta) * scaling).astype(jnp.bfloat16)
+        dq_ref[rows, :] = lax.dot_general(
+            score_grads, keys, (((0,), (0,)), ((), ())), preferred_element_type=jnp.float32
         ).astype(dq_ref.dtype)
-        dk_ref[0:span, :] += lax.dot_general(
-            score_grads, q_rows, (((0,), (0,)), ((), ())), preferred_element_type=jnp.float32
-        )
+        dk_ref[0:span, :] += jnp.dot(score_grads, q_rows, preferred_element_type=jnp.float32)
 
 
 def attend_back_kernel(gathered, segment, heads_of_query, q_block, g_block, k_block, v_block):

time: 206 us -> 206 us (level)
  no operation moved by 1% of the time
where the time goes in v7:
time: 206 us; the launch traced here: 205 us
  waiting for transfers between devices  86.2 us (42%)
  starting transfers between devices  74.8 us (36%)
  local copies, waits for them, and re-layouts  15.1 us (7%)
  Pallas kernels  13.4 us (7%)
  other arithmetic  10.3 us (5%)
  between operations  5.58 us (3%)
    all_to_all x2, starting transfers between devices, route(): spread = lax.all_to_all(flat, 'dp', 0, 0, tiled=True)  50.6 us
    all_to_all x1, waiting for transfers between devices, per_device(): lax.all_to_all(packed, 'seq', split_axis=1, concat_axis=0, tiled=True)  38.5 us
    all_to_all x2, waiting for transfers between devices, route(): spread = lax.all_to_all(flat, 'dp', 0, 0, tiled=True)  17.8 us
    all_to_all x2, waiting for transfers between devices, route(): back = lax.all_to_all(routed, 'dp', 0, 0, tiled=True)  15.4 us
    all_to_all x1, waiting for transfers between devices, per_device(): lax.all_to_all(low, 'seq', split_axis=0, concat_axis=1, tiled=True)  14.4 us
    pallas_call x1, Pallas kernels, attend_back_kernel(): pl.pallas_call(attend_kernel, grid=(heads_of_query,), in_specs=[pl.BlockS...  13.4 us
    all_to_all x1, starting transfers between devices, per_device(): lax.all_to_all(packed, 'seq', split_axis=1, concat_axis=0, tiled=True)  9.9 us
    all_to_all x2, starting transfers between devices, route(): back = lax.all_to_all(routed, 'dp', 0, 0, tiled=True)  8.89 us
  transfers between devices with their start and end apart: 6, of which 6 were waited for; matrix products, arithmetic and copies ran while one was open for 4% of the time, Pallas kernels for 0%

profile of v7, /device:TPU:1, one launch (start us, length us, event | category | flops | bytes accessed | tf_op | source)
XLA Modules:
  0.0 205.4 jit_solution(6594343365175608519)
XLA Ops:
  0.7 0.8 select_reduce_fusion
  1.5 0.6 dynamic_slice.22
  4.0 0.8 constant_dynamic-slice_fusion.2
  4.9 0.6 fusion.3
  6.7 0.8 dynamic-slice_bitcast_fusion.1
  7.6 0.5 broadcast.39
  8.1 0.9 reduce.2
  9.0 0.6 reshape.162
  9.7 14.6 %all-to-all-start = ((bf16[64,2,256]{2,1,0:T(2,128)(2,1)}), bf16[64,2,256]{2,1,0:T(2,128)(2,1)S(1)}, u32[]{:S(2)}, u32[]{:S(2)}) async-start(bf16[64,2,256]{2,1,0:T(2,128)(2,1)} %reshape.162), calls=%async_computation | async-start | bytes 131072 | tf_op jit(solution)/shard_map/all_to_all | solution.py:156
  24.3 0.7 compare_and_fusion
  25.0 1.4 copy_bitcast_fusion
  26.4 7.8 %all-to-all-done = bf16[64,2,256]{2,1,0:T(2,128)(2,1)S(1)} async-done(((bf16[64,2,256]{2,1,0:T(2,128)(2,1)}), bf16[64,2,256]{2,1,0:T(2,128)(2,1)S(1)}, u32[]{:S(2)}, u32[]{:S(2)}) %all-to-all-start) | async-done | bytes 65568 | tf_op jit(solution)/shard_map/all_to_all | solution.py:156
  34.4 0.7 gather_fusion
  35.1 0.6 reduce.3
  35.7 0.6 reshape.164
  36.4 4.4 %all-to-all-start.1 = ((bf16[64,2,256]{2,1,0:T(2,128)(2,1)}), bf16[64,2,256]{2,1,0:T(2,128)(2,1)S(1)}, u32[]{:S(2)}, u32[]{:S(2)}) async-start(bf16[64,2,256]{2,1,0:T(2,128)(2,1)} %reshape.164), calls=%async_computation.1 | async-start | bytes 131072 | tf_op jit(solution)/shard_map/all_to_all | solution.py:158
  40.8 0.7 iota_compare_fusion.4
  41.5 0.2 copy.84
  41.7 0.6 iota_compare_fusion.5
  42.3 8.7 %all-to-all-done.1 = bf16[64,2,256]{2,1,0:T(2,128)(2,1)S(1)} async-done(((bf16[64,2,256]{2,1,0:T(2,128)(2,1)}), bf16[64,2,256]{2,1,0:T(2,128)(2,1)S(1)}, u32[]{:S(2)}, u32[]{:S(2)}) %all-to-all-start.1) | async-done | bytes 65568 | tf_op jit(solution)/shard_map/all_to_all | solution.py:158
  51.0 0.4 reduce
  51.9 0.2 copy.87
  52.1 1.7 pad_maximum_fusion
  53.7 9.9 %all-to-all-start.2 = ((bf16[128,8,1024]{2,0,1:T(8,128)(2,1)}), bf16[128,8,1024]{2,0,1:T(8,128)(2,1)S(1)}, u32[]{:S(2)}, u32[]{:S(2)}) async-start(bf16[128,8,1024]{2,0,1:T(8,128)(2,1)} %pad_maximum_fusion), calls=%async_computation.2 | async-start | bytes 4194304 | tf_op jit(solution)/shard_map/all_to_all | solution.py:204
  63.6 0.2 reduce-window.8
  63.9 0.2 copy.89.seg_row_ref
  64.1 38.5 %all-to-all-done.2 = bf16[128,8,1024]{2,0,1:T(8,128)(2,1)S(1)} async-done(((bf16[128,8,1024]{2,0,1:T(8,128)(2,1)}), bf16[128,8,1024]{2,0,1:T(8,128)(2,1)S(1)}, u32[]{:S(2)}, u32[]{:S(2)}) %all-to-all-start.2) | async-done | bytes 2097184 | tf_op jit(solution)/shard_map/all_to_all | solution.py:204
  102.6 13.4 %shard_map.94 = (bf16[1024,384]{1,0:T(8,128)(2,1)S(1)}, f32[1024,128]{1,0:T(8,128)S(1)}, f32[1024,128]{1,0:T(8,128)S(1)}) custom-call(s32[1024,1]{1,0:T(8,128)S(1)} %copy.89.seg_row_ref, s32[1,1024]{1,0:T(1,128)S(1)} %bitcast.57, bf16[1024,1024]{1,0:T(8,128)(2,1)S(1)} %bitcast.52, bf16[1024,1024]{1,0:T(8,128)(2,1)S(1)} %bitcast.53, ...), custom_call_target="tpu_custom_call" | custom-call | flops 2516582400 | bytes 3932160 | tf_op jit(solution)/shard_map/pallas_call | solution.py:121
  116.1 0.1 pad_maximum_fusion.1
  116.2 1.5 copy.90
  117.7 5.5 %all-to-all-start.3 = ((bf16[8,128,640]{1,2,0:T(8,128)(2,1)}), bf16[8,128,640]{1,2,0:T(8,128)(2,1)S(1)}, u32[]{:S(2)}, u32[]{:S(2)}) async-start(bf16[8,128,640]{1,2,0:T(8,128)(2,1)} %copy.90), calls=%async_computation.3 | async-start | bytes 2621440 | tf_op jit(solution)/shard_map/all_to_all | solution.py:221
  124.4 14.4 %all-to-all-done.3 = bf16[8,128,640]{1,2,0:T(8,128)(2,1)S(1)} async-done(((bf16[8,128,640]{1,2,0:T(8,128)(2,1)}), bf16[8,128,640]{1,2,0:T(8,128)(2,1)S(1)}, u32[]{:S(2)}, u32[]{:S(2)}) %all-to-all-start.3) | async-done | bytes 1310752 | tf_op jit(solution)/shard_map/all_to_all | solution.py:221
  139.3 0.9 reduce.4
  140.2 0.6 reshape.166
  140.9 36.0 %all-to-all-start.4 = ((bf16[64,2,256]{2,1,0:T(2,128)(2,1)}), bf16[64,2,256]{2,1,0:T(2,128)(2,1)S(1)}, u32[]{:S(2)}, u32[]{:S(2)}) async-start(bf16[64,2,256]{2,1,0:T(2,128)(2,1)} %reshape.166), calls=%async_computation.4 | async-start | bytes 131072 | tf_op jit(solution)/shard_map/all_to_all | solution.py:156
  176.9 10.0 %all-to-all-done.4 = bf16[64,2,256]{2,1,0:T(2,128)(2,1)S(1)} async-done(((bf16[64,2,256]{2,1,0:T(2,128)(2,1)}), bf16[64,2,256]{2,1,0:T(2,128)(2,1)S(1)}, u32[]{:S(2)}, u32[]{:S(2)}) %all-to-all-start.4) | async-done | bytes 65568 | tf_op jit(solution)/shard_map/all_to_all | solution.py:156
  187.0 0.7 gather_fusion.1
  187.8 0.6 reduce.5
  188.4 0.6 reshape.168
  189.0 4.4 %all-to-all-start.5 = ((bf16[64,2,256]{2,1,0:T(2,128)(2,1)}), bf16[64,2,256]{2,1,0:T(2,128)(2,1)S(1)}, u32[]{:S(2)}, u32[]{:S(2)}) async-start(bf16[64,2,256]{2,1,0:T(2,128)(2,1)} %reshape.168), calls=%async_computation.5 | async-start | bytes 131072 | tf_op jit(solution)/shard_map/all_to_all | solution.py:158
  193.5 0.7 iota_compare_fusion.2
  194.1 0.6 iota_compare_fusion.3
  194.8 1.2 copy.98
  196.0 0.8 copy.100
  196.8 6.8 %all-to-all-done.5 = bf16[64,2,256]{2,1,0:T(2,128)(2,1)S(1)} async-done(((bf16[64,2,256]{2,1,0:T(2,128)(2,1)}), bf16[64,2,256]{2,1,0:T(2,128)(2,1)S(1)}, u32[]{:S(2)}, u32[]{:S(2)}) %all-to-all-start.5) | async-done | bytes 65568 | tf_op jit(solution)/shard_map/all_to_all | solution.py:158
  203.7 0.4 reduce.1
  204.4 0.2 add_convert_fusion
  204.6 0.9 copy.99
  (46 shorter events, 2.0 us)
Async XLA Ops:
  0.6 24.3 %copy-start = (bf16[128,1024]{1,0:T(8,128)(2,1)S(1)}, bf16[128,1024]{1,0:T(8,128)(2,1)}, u32[]{:S(2)}) copy-start(bf16[128,1024]{1,0:T(8,128)(2,1)} %param.11) | copy-start | bytes 786436
  0.6 24.3 %copy-start.1 = (bf16[128,3072]{1,0:T(8,128)(2,1)S(1)}, bf16[128,3072]{1,0:T(8,128)(2,1)}, u32[]{:S(2)}) copy-start(bf16[128,3072]{1,0:T(8,128)(2,1)} %param.12) | copy-start | bytes 2359300
  7.6 18.8 %copy-start.3 = (s32[64]{0:T(128)S(1)}, s32[64]{0:T(128)}, u32[]{:S(2)}) copy-start(s32[64]{0:T(128)} %param.15) | copy-start | bytes 772
  9.7 24.6 %all-to-all-start = ((bf16[64,2,256]{2,1,0:T(2,128)(2,1)}), bf16[64,2,256]{2,1,0:T(2,128)(2,1)S(1)}, u32[]{:S(2)}, u32[]{:S(2)}) async-start(bf16[64,2,256]{2,1,0:T(2,128)(2,1)} %reshape.162), calls=%async_computation | async-start | bytes 131072 | tf_op jit(solution)/shard_map/all_to_all | solution.py:156
  25.0 16.5 %copy-start.2 = (bf16[128,1024]{1,0:T(8,128)(2,1)S(1)}, bf16[128,1024]{1,0:T(8,128)(2,1)}, u32[]{:S(2)}) copy-start(bf16[128,1024]{1,0:T(8,128)(2,1)} %param.10) | copy-start | bytes 786436
  36.4 14.6 %all-to-all-start.1 = ((bf16[64,2,256]{2,1,0:T(2,128)(2,1)}), bf16[64,2,256]{2,1,0:T(2,128)(2,1)S(1)}, u32[]{:S(2)}, u32[]{:S(2)}) async-start(bf16[64,2,256]{2,1,0:T(2,128)(2,1)} %reshape.164), calls=%async_computation.1 | async-start | bytes 131072 | tf_op jit(solution)/shard_map/all_to_all | solution.py:158
  53.7 9.9 %copy-start.4 = (s32[1,4]{1,0:T(1,128)S(1)}, s32[1,4]{1,0:T(1,128)}, u32[]{:S(2)}) copy-start(s32[1,4]{1,0:T(1,128)} %param.13) | copy-start | bytes 52
  53.7 48.9 %all-to-all-start.2 = ((bf16[128,8,1024]{2,0,1:T(8,128)(2,1)}), bf16[128,8,1024]{2,0,1:T(8,128)(2,1)S(1)}, u32[]{:S(2)}, u32[]{:S(2)}) async-start(bf16[128,8,1024]{2,0,1:T(8,128)(2,1)} %pad_maximum_fusion), calls=%async_computation.2 | async-start | bytes 4194304 | tf_op jit(solution)/shard_map/all_to_all | solution.py:204
  117.7 21.2 %all-to-all-start.3 = ((bf16[8,128,640]{1,2,0:T(8,128)(2,1)}), bf16[8,128,640]{1,2,0:T(8,128)(2,1)S(1)}, u32[]{:S(2)}, u32[]{:S(2)}) async-start(bf16[8,128,640]{1,2,0:T(8,128)(2,1)} %copy.90), calls=%async_computation.3 | async-start | bytes 2621440 | tf_op jit(solution)/shard_map/all_to_all | solution.py:221
  140.9 46.1 %all-to-all-start.4 = ((bf16[64,2,256]{2,1,0:T(2,128)(2,1)}), bf16[64,2,256]{2,1,0:T(2,128)(2,1)S(1)}, u32[]{:S(2)}, u32[]{:S(2)}) async-start(bf16[64,2,256]{2,1,0:T(2,128)(2,1)} %reshape.166), calls=%async_computation.4 | async-start | bytes 131072 | tf_op jit(solution)/shard_map/all_to_all | solution.py:156
  189.0 14.6 %all-to-all-start.5 = ((bf16[64,2,256]{2,1,0:T(2,128)(2,1)}), bf16[64,2,256]{2,1,0:T(2,128)(2,1)S(1)}, u32[]{:S(2)}, u32[]{:S(2)}) async-start(bf16[64,2,256]{2,1,0:T(2,128)(2,1)} %reshape.168), calls=%async_computation.5 | async-start | bytes 131072 | tf_op jit(solution)/shard_map/all_to_all | solution.py:158

commit v8 on v4

--- a/solution.py
+++ b/solution.py
@@ -154,6 +154,17 @@
     )(seg_row, seg_col, gathered, gathered, gathered, gathered)
 
 
+def route_block(block, order, heads):
+    prompt_count = lax.axis_size("dp")
+    rows = block.shape[0]
+    flat = block.reshape(prompt_count, rows // prompt_count, KEY_VALUE_HEADS, HEAD_WIDTH)
+    spread = lax.all_to_all(flat, "dp", 0, 0, tiled=True)
+    routed = jnp.take(spread, order, axis=0)
+    routed = jnp.take_along_axis(routed, heads[:, None, :, None], axis=2)
+    back = lax.all_to_all(routed, "dp", 0, 0, tiled=True)
+    return back.reshape(rows, KNOCKOUT_COUNT, HEAD_WIDTH)
+
+
 def route(payload, order):
     prompt_count = lax.axis_size("dp")
     flat = payload.reshape(prompt_count, -1)
@@ -178,15 +189,12 @@
     length = tok_rows * sequence_count
     prompt_index = lax.axis_index("dp")
     prompt_ids = jnp.arange(prompt_count, dtype=jnp.int32)
-    consumer = jnp.sum(
-        jnp.where(source[None, :] == prompt_ids[:, None], prompt_ids[None, :], 0), axis=1
-    )
+    consumer = jnp.zeros((prompt_count,), jnp.int32).at[source].set(prompt_ids)
     my_knock = knocked[prompt_index]
     their_knock = knocked[consumer[prompt_index]]
     head_ids = jnp.arange(KEY_VALUE_HEADS, dtype=jnp.int32)[None, :, None]
 
-    outgoing = pick_heads(keys, their_knock)
-    fetched = route(outgoing, source)
+    fetched = route_block(keys, source, knocked)
     keys3 = keys.reshape(tok_rows, KEY_VALUE_HEADS, HEAD_WIDTH)
     used3 = keys3
     for k in range(KNOCKOUT_COUNT - 1, -1, -1):

time: 206 us -> 205 us (level)
  waiting for transfers between devices: 86.2 us -> 81 us
  starting transfers between devices: 74.8 us -> 78.2 us
    all_to_all x0 -> x2, starting transfers between devices: none -> 22.4 us  [the longest x1 14.6 us: route_block(): spread = lax.all_to_all(flat, 'dp', 0, 0, tiled=True)]
    all_to_all x2 -> x1, starting transfers between devices: 50.6 us -> 36 us  [route(): spread = lax.all_to_all(flat, 'dp', 0, 0, tiled=True)]
    all_to_all x0 -> x2, waiting for transfers between devices: none -> 11.5 us  [the longest x1 8.53 us: route_block(): back = lax.all_to_all(routed, 'dp', 0, 0, tiled=True)]
    all_to_all x2 -> x1, waiting for transfers between devices: 15.4 us -> 6.72 us  [route(): back = lax.all_to_all(routed, 'dp', 0, 0, tiled=True)]
    all_to_all x2 -> x1, waiting for transfers between devices: 17.8 us -> 10 us  [route(): spread = lax.all_to_all(flat, 'dp', 0, 0, tiled=True)]
    all_to_all x2 -> x1, starting transfers between devices: 8.89 us -> 4.44 us  [route(): back = lax.all_to_all(routed, 'dp', 0, 0, tiled=True)]
    unnamed x24 -> x18, local copies, waits for them, and re-layouts: 5.89 us -> 6.26 us
  transfers between devices with their start and end apart: 6 -> 6, of which waited for: 6 -> 6; matrix products, arithmetic and copies ran while one was open for 4% -> 6% of each run, Pallas kernels for 0% -> 0%
where the time goes in v8:
time: 205 us
  waiting for transfers between devices  81 us (40%)
  starting transfers between devices  78.2 us (38%)
  local copies, waits for them, and re-layouts  16.7 us (8%)
  Pallas kernels  13.5 us (7%)
  other arithmetic  10.9 us (5%)
  between operations  4.27 us (2%)
    all_to_all x1, waiting for transfers between devices, per_device(): lax.all_to_all(packed, 'seq', split_axis=1, concat_axis=0, tiled=True)  38.5 us
    all_to_all x1, starting transfers between devices, route(): spread = lax.all_to_all(flat, 'dp', 0, 0, tiled=True)  36 us
    all_to_all x1, starting transfers between devices, route_block(): spread = lax.all_to_all(flat, 'dp', 0, 0, tiled=True)  14.6 us
    all_to_all x1, waiting for transfers between devices, per_device(): lax.all_to_all(low, 'seq', split_axis=0, concat_axis=1, tiled=True)  14.4 us
    pallas_call x1, Pallas kernels, attend_back_kernel(): pl.pallas_call(attend_kernel, grid=(heads_of_query,), in_specs=[pl.BlockS...  13.5 us
    all_to_all x1, waiting for transfers between devices, route(): spread = lax.all_to_all(flat, 'dp', 0, 0, tiled=True)  10 us
    all_to_all x1, starting transfers between devices, per_device(): lax.all_to_all(packed, 'seq', split_axis=1, concat_axis=0, tiled=True)  9.9 us
    all_to_all x1, waiting for transfers between devices, route_block(): back = lax.all_to_all(routed, 'dp', 0, 0, tiled=True)  8.53 us
  transfers between devices with their start and end apart: 6, of which 6 were waited for; matrix products, arithmetic and copies ran while one was open for 6% of the time, Pallas kernels for 0%

profile of v8, /device:TPU:1, one launch (start us, length us, event | category | flops | bytes accessed | tf_op | source)
XLA Modules:
  0.0 204.6 jit_solution(6234053952479523786)
XLA Ops:
  0.7 1.8 copy.134
  2.4 14.6 %all-to-all-start = ((bf16[64,2,8,128]{3,2,1,0:T(8,128)(2,1)}), bf16[64,2,8,128]{3,2,1,0:T(8,128)(2,1)S(1)}, u32[]{:S(2)}, u32[]{:S(2)}) async-start(bf16[64,2,8,128]{3,2,1,0:T(8,128)(2,1)} %bitcast.41), calls=%async_computation | async-start | bytes 524288 | tf_op jit(solution)/shard_map/all_to_all | solution.py:161
  17.0 0.7 compare_select_fusion.2
  17.7 0.8 scatter_custom_fusion
  18.5 0.6 dynamic_slice.16
  20.4 0.7 bitcast_or_fusion
  21.1 0.7 compare_and_fusion.2
  22.4 0.8 constant_dynamic-slice_fusion.2
  23.7 0.6 fusion.5
  24.2 0.7 compare_and_fusion.1
  24.9 1.4 copy_bitcast_fusion
  26.3 2.9 %all-to-all-done = bf16[64,2,8,128]{3,2,1,0:T(8,128)(2,1)S(1)} async-done(((bf16[64,2,8,128]{3,2,1,0:T(8,128)(2,1)}), bf16[64,2,8,128]{3,2,1,0:T(8,128)(2,1)S(1)}, u32[]{:S(2)}, u32[]{:S(2)}) %all-to-all-start) | async-done | bytes 262176 | tf_op jit(solution)/shard_map/all_to_all | solution.py:161
  29.3 0.6 gather_fusion
  30.0 0.2 copy.107
  30.3 0.9 gather_fusion.2
  31.1 0.8 fusion
  32.0 7.8 %all-to-all-start.1 = ((bf16[64,2,2,128]{3,1,2,0:T(2,128)(2,1)}), bf16[64,2,2,128]{3,1,2,0:T(2,128)(2,1)S(1)}, u32[]{:S(2)}, u32[]{:S(2)}) async-start(bf16[64,2,2,128]{3,1,2,0:T(2,128)(2,1)} %fusion), calls=%async_computation.1 | async-start | bytes 131072 | tf_op jit(solution)/shard_map/all_to_all | solution.py:164
  39.8 0.7 iota_compare_fusion.3
  40.4 0.2 copy.111
  40.6 0.6 iota_compare_fusion.4
  41.3 8.5 %all-to-all-done.1 = bf16[64,2,2,128]{3,1,2,0:T(2,128)(2,1)S(1)} async-done(((bf16[64,2,2,128]{3,1,2,0:T(2,128)(2,1)}), bf16[64,2,2,128]{3,1,2,0:T(2,128)(2,1)S(1)}, u32[]{:S(2)}, u32[]{:S(2)}) %all-to-all-start.1) | async-done | bytes 65568 | tf_op jit(solution)/shard_map/all_to_all | solution.py:164
  50.2 0.2 copy.114
  50.4 1.7 pad_maximum_fusion
  52.1 9.9 %all-to-all-start.2 = ((bf16[128,8,1024]{2,0,1:T(8,128)(2,1)}), bf16[128,8,1024]{2,0,1:T(8,128)(2,1)S(1)}, u32[]{:S(2)}, u32[]{:S(2)}) async-start(bf16[128,8,1024]{2,0,1:T(8,128)(2,1)} %pad_maximum_fusion), calls=%async_computation.2 | async-start | bytes 4194304 | tf_op jit(solution)/shard_map/all_to_all | solution.py:216
  62.0 0.2 reduce-window.8
  62.3 0.2 copy.116.seg_row_ref
  62.5 38.5 %all-to-all-done.2 = bf16[128,8,1024]{2,0,1:T(8,128)(2,1)S(1)} async-done(((bf16[128,8,1024]{2,0,1:T(8,128)(2,1)}), bf16[128,8,1024]{2,0,1:T(8,128)(2,1)S(1)}, u32[]{:S(2)}, u32[]{:S(2)}) %all-to-all-start.2) | async-done | bytes 2097184 | tf_op jit(solution)/shard_map/all_to_all | solution.py:216
  101.0 13.5 %shard_map.94 = (bf16[1024,384]{1,0:T(8,128)(2,1)S(1)}, f32[1024,128]{1,0:T(8,128)S(1)}, f32[1024,128]{1,0:T(8,128)S(1)}) custom-call(s32[1024,1]{1,0:T(8,128)S(1)} %copy.116.seg_row_ref, s32[1,1024]{1,0:T(1,128)S(1)} %bitcast.61, bf16[1024,1024]{1,0:T(8,128)(2,1)S(1)} %bitcast.56, bf16[1024,1024]{1,0:T(8,128)(2,1)S(1)} %bitcast.57, ...), custom_call_target="tpu_custom_call" | custom-call | flops 2516582400 | bytes 3932160 | tf_op jit(solution)/shard_map/pallas_call | solution.py:125
  114.6 1.5 copy.117
  116.1 5.5 %all-to-all-start.3 = ((bf16[8,128,640]{1,2,0:T(8,128)(2,1)}), bf16[8,128,640]{1,2,0:T(8,128)(2,1)S(1)}, u32[]{:S(2)}, u32[]{:S(2)}) async-start(bf16[8,128,640]{1,2,0:T(8,128)(2,1)} %copy.117), calls=%async_computation.3 | async-start | bytes 2621440 | tf_op jit(solution)/shard_map/all_to_all | solution.py:233
  122.9 14.4 %all-to-all-done.3 = bf16[8,128,640]{1,2,0:T(8,128)(2,1)S(1)} async-done(((bf16[8,128,640]{1,2,0:T(8,128)(2,1)}), bf16[8,128,640]{1,2,0:T(8,128)(2,1)S(1)}, u32[]{:S(2)}, u32[]{:S(2)}) %all-to-all-start.3) | async-done | bytes 1310752 | tf_op jit(solution)/shard_map/all_to_all | solution.py:233
  137.7 0.5 broadcast.99
  138.2 1.0 reduce.1
  139.3 0.6 reshape.225
  139.9 36.0 %all-to-all-start.4 = ((bf16[64,2,256]{2,1,0:T(2,128)(2,1)}), bf16[64,2,256]{2,1,0:T(2,128)(2,1)S(1)}, u32[]{:S(2)}, u32[]{:S(2)}) async-start(bf16[64,2,256]{2,1,0:T(2,128)(2,1)} %reshape.225), calls=%async_computation.4 | async-start | bytes 131072 | tf_op jit(solution)/shard_map/all_to_all | solution.py:171
  176.0 10.0 %all-to-all-done.4 = bf16[64,2,256]{2,1,0:T(2,128)(2,1)S(1)} async-done(((bf16[64,2,256]{2,1,0:T(2,128)(2,1)}), bf16[64,2,256]{2,1,0:T(2,128)(2,1)S(1)}, u32[]{:S(2)}, u32[]{:S(2)}) %all-to-all-start.4) | async-done | bytes 65568 | tf_op jit(solution)/shard_map/all_to_all | solution.py:171
  186.0 0.7 gather_fusion.1
  186.8 0.7 reduce.2
  187.5 0.6 reshape.227
  188.1 4.4 %all-to-all-start.5 = ((bf16[64,2,256]{2,1,0:T(2,128)(2,1)}), bf16[64,2,256]{2,1,0:T(2,128)(2,1)S(1)}, u32[]{:S(2)}, u32[]{:S(2)}) async-start(bf16[64,2,256]{2,1,0:T(2,128)(2,1)} %reshape.227), calls=%async_computation.5 | async-start | bytes 131072 | tf_op jit(solution)/shard_map/all_to_all | solution.py:173
  192.6 0.7 iota_compare_fusion.1
  193.3 0.7 iota_compare_fusion.2
  194.0 1.2 copy.125
  195.2 0.8 copy.127
  196.0 6.7 %all-to-all-done.5 = bf16[64,2,256]{2,1,0:T(2,128)(2,1)S(1)} async-done(((bf16[64,2,256]{2,1,0:T(2,128)(2,1)}), bf16[64,2,256]{2,1,0:T(2,128)(2,1)S(1)}, u32[]{:S(2)}, u32[]{:S(2)}) %all-to-all-start.5) | async-done | bytes 65568 | tf_op jit(solution)/shard_map/all_to_all | solution.py:173
  202.8 0.4 reduce
  203.5 0.2 add_convert_fusion
  203.7 0.9 copy.126
  (43 shorter events, 2.3 us)
Async XLA Ops:
  0.6 23.0 %copy-start = (bf16[128,1024]{1,0:T(8,128)(2,1)S(1)}, bf16[128,1024]{1,0:T(8,128)(2,1)}, u32[]{:S(2)}) copy-start(bf16[128,1024]{1,0:T(8,128)(2,1)} %param.9) | copy-start | bytes 786436
  0.6 24.3 %copy-start.2 = (bf16[128,3072]{1,0:T(8,128)(2,1)S(1)}, bf16[128,3072]{1,0:T(8,128)(2,1)}, u32[]{:S(2)}) copy-start(bf16[128,3072]{1,0:T(8,128)(2,1)} %param.10) | copy-start | bytes 2359300
  2.4 26.8 %all-to-all-start = ((bf16[64,2,8,128]{3,2,1,0:T(8,128)(2,1)}), bf16[64,2,8,128]{3,2,1,0:T(8,128)(2,1)S(1)}, u32[]{:S(2)}, u32[]{:S(2)}) async-start(bf16[64,2,8,128]{3,2,1,0:T(8,128)(2,1)} %bitcast.41), calls=%async_computation | async-start | bytes 524288 | tf_op jit(solution)/shard_map/all_to_all | solution.py:161
  24.9 15.5 %copy-start.1 = (bf16[128,1024]{1,0:T(8,128)(2,1)S(1)}, bf16[128,1024]{1,0:T(8,128)(2,1)}, u32[]{:S(2)}) copy-start(bf16[128,1024]{1,0:T(8,128)(2,1)} %param.8) | copy-start | bytes 786436
  32.0 17.8 %all-to-all-start.1 = ((bf16[64,2,2,128]{3,1,2,0:T(2,128)(2,1)}), bf16[64,2,2,128]{3,1,2,0:T(2,128)(2,1)S(1)}, u32[]{:S(2)}, u32[]{:S(2)}) async-start(bf16[64,2,2,128]{3,1,2,0:T(2,128)(2,1)} %fusion), calls=%async_computation.1 | async-start | bytes 131072 | tf_op jit(solution)/shard_map/all_to_all | solution.py:164
  52.1 9.9 %copy-start.3 = (s32[1,4]{1,0:T(1,128)S(1)}, s32[1,4]{1,0:T(1,128)}, u32[]{:S(2)}) copy-start(s32[1,4]{1,0:T(1,128)} %param.11) | copy-start | bytes 52
  52.1 48.9 %all-to-all-start.2 = ((bf16[128,8,1024]{2,0,1:T(8,128)(2,1)}), bf16[128,8,1024]{2,0,1:T(8,128)(2,1)S(1)}, u32[]{:S(2)}, u32[]{:S(2)}) async-start(bf16[128,8,1024]{2,0,1:T(8,128)(2,1)} %pad_maximum_fusion), calls=%async_computation.2 | async-start | bytes 4194304 | tf_op jit(solution)/shard_map/all_to_all | solution.py:216
  116.1 21.2 %all-to-all-start.3 = ((bf16[8,128,640]{1,2,0:T(8,128)(2,1)}), bf16[8,128,640]{1,2,0:T(8,128)(2,1)S(1)}, u32[]{:S(2)}, u32[]{:S(2)}) async-start(bf16[8,128,640]{1,2,0:T(8,128)(2,1)} %copy.117), calls=%async_computation.3 | async-start | bytes 2621440 | tf_op jit(solution)/shard_map/all_to_all | solution.py:233
  139.9 46.0 %all-to-all-start.4 = ((bf16[64,2,256]{2,1,0:T(2,128)(2,1)}), bf16[64,2,256]{2,1,0:T(2,128)(2,1)S(1)}, u32[]{:S(2)}, u32[]{:S(2)}) async-start(bf16[64,2,256]{2,1,0:T(2,128)(2,1)} %reshape.225), calls=%async_computation.4 | async-start | bytes 131072 | tf_op jit(solution)/shard_map/all_to_all | solution.py:171
  188.1 14.6 %all-to-all-start.5 = ((bf16[64,2,256]{2,1,0:T(2,128)(2,1)}), bf16[64,2,256]{2,1,0:T(2,128)(2,1)S(1)}, u32[]{:S(2)}, u32[]{:S(2)}) async-start(bf16[64,2,256]{2,1,0:T(2,128)(2,1)} %reshape.227), calls=%async_computation.5 | async-start | bytes 131072 | tf_op jit(solution)/shard_map/all_to_all | solution.py:173

commit v9 on v8

--- a/solution.py
+++ b/solution.py
@@ -71,15 +71,18 @@
 BLOCK_ROWS = 256
 
 
-def attend_kernel(seg_row_ref, seg_col_ref, q_ref, g_ref, k_ref, v_ref, dq_ref, dk_ref, dv_ref):
+def attend_kernel(seg_row_ref, seg_col_ref, q_ref, g_ref, k_ref, v_ref, out_ref, dk_acc, dv_acc):
     scaling = 1.0 / math.sqrt(HEAD_WIDTH)
     length = q_ref.shape[0]
-
-    @pl.when(pl.program_id(0) == 0)
+    head = pl.program_id(0)
+    heads = pl.num_programs(0)
+
+    @pl.when(head == 0)
     def _():
-        dk_ref[...] = jnp.zeros_like(dk_ref)
-        dv_ref[...] = jnp.zeros_like(dv_ref)
-
+        dk_acc[...] = jnp.zeros_like(dk_acc)
+        dv_acc[...] = jnp.zeros_like(dv_acc)
+
+    dq_cols = pl.ds(pl.multiple_of(head * HEAD_WIDTH, HEAD_WIDTH), HEAD_WIDTH)
     for block in range(length // BLOCK_ROWS):
         rows = pl.ds(block * BLOCK_ROWS, BLOCK_ROWS)
         span = (block + 1) * BLOCK_ROWS
@@ -99,7 +102,7 @@
         weights = jnp.exp(scores - row_max)
         probs = weights / jnp.sum(weights, axis=1, keepdims=True)
         probs_low = probs.astype(jnp.bfloat16)
-        dv_ref[0:span, :] += lax.dot_general(
+        dv_acc[0:span, :] += lax.dot_general(
             probs_low, g_rows, (((0,), (0,)), ((), ())), preferred_element_type=jnp.float32
         )
         prob_grads = lax.dot_general(
@@ -107,12 +110,18 @@
         )
         row_delta = jnp.sum(probs * prob_grads, axis=1, keepdims=True)
         score_grads = (probs * (prob_grads - row_delta) * scaling).astype(jnp.bfloat16)
-        dq_ref[rows, :] = jnp.dot(
+        out_ref[rows, dq_cols] = jnp.dot(
             score_grads, keys, preferred_element_type=jnp.float32
-        ).astype(dq_ref.dtype)
-        dk_ref[0:span, :] += lax.dot_general(
+        ).astype(out_ref.dtype)
+        dk_acc[0:span, :] += lax.dot_general(
             score_grads, q_rows, (((0,), (0,)), ((), ())), preferred_element_type=jnp.float32
         )
+
+    @pl.when(head == heads - 1)
+    def _():
+        base = out_ref.shape[1] - 2 * HEAD_WIDTH
+        out_ref[:, base : base + HEAD_WIDTH] = dv_acc[...].astype(out_ref.dtype)
+        out_ref[:, base + HEAD_WIDTH :] = dk_acc[...].astype(out_ref.dtype)
 
 
 def attend_back_kernel(gathered, segment, heads_of_query, q_block, g_block, k_block, v_block):
@@ -121,6 +130,7 @@
     seg_col = segment.reshape(1, length)
     full = lambda h: (0, 0)
     col = lambda b: pl.BlockSpec((length, HEAD_WIDTH), lambda h: (0, b))
+    width = (heads_of_query + 2) * HEAD_WIDTH
     flops = 5 * 2 * length * length * HEAD_WIDTH * heads_of_query * 10 // 16
     return pl.pallas_call(
         attend_kernel,
@@ -133,15 +143,11 @@
             col(k_block),
             col(v_block),
         ],
-        out_specs=[
-            pl.BlockSpec((length, HEAD_WIDTH), lambda h: (0, h)),
-            pl.BlockSpec((length, HEAD_WIDTH), full),
-            pl.BlockSpec((length, HEAD_WIDTH), full),
-        ],
-        out_shape=[
-            jax.ShapeDtypeStruct((length, heads_of_query * HEAD_WIDTH), jnp.bfloat16),
-            jax.ShapeDtypeStruct((length, HEAD_WIDTH), jnp.float32),
-            jax.ShapeDtypeStruct((length, HEAD_WIDTH), jnp.float32),
+        out_specs=pl.BlockSpec((length, width), full),
+        out_shape=jax.ShapeDtypeStruct((length, width), jnp.bfloat16),
+        scratch_shapes=[
+            pltpu.VMEM((length, HEAD_WIDTH), jnp.float32),
+            pltpu.VMEM((length, HEAD_WIDTH), jnp.float32),
         ],
         compiler_params=pltpu.CompilerParams(
             dimension_semantics=("arbitrary",), vmem_limit_bytes=48 * 1024 * 1024
@@ -149,10 +155,9 @@
         cost_estimate=pl.CostEstimate(
             flops=flops,
             transcendentals=length * length * heads_of_query * 10 // 16,
-            bytes_accessed=length * HEAD_WIDTH * (2 * 2 * heads_of_query + 2 * 2 + 2 * heads_of_query + 8),
+            bytes_accessed=length * HEAD_WIDTH * (2 * 2 * heads_of_query + 2 * 2 + 2 * width // HEAD_WIDTH),
         ),
     )(seg_row, seg_col, gathered, gathered, gathered, gathered)
-
 
 def route_block(block, order, heads):
     prompt_count = lax.axis_size("dp")
@@ -204,9 +209,12 @@
     def cols(x):
         return x.reshape(tok_rows, sequence_count, -1)
 
-    packed = jnp.concatenate(
-        [cols(queries), cols(output_gradient), cols(used_keys), cols(values)], axis=2
-    )
+    pre = jnp.concatenate(
+        [cols(queries), cols(output_gradient), jnp.zeros_like(cols(keys)), cols(values)], axis=2
+    )
+    pre = lax.optimization_barrier(pre)
+    key_at = (queries.shape[1] + output_gradient.shape[1]) // sequence_count
+    packed = lax.dynamic_update_slice(pre, cols(used_keys), (0, 0, key_at))
     widths = (
         queries.shape[1] // sequence_count,
         output_gradient.shape[1] // sequence_count,
@@ -223,13 +231,10 @@
     position = jnp.arange(length, dtype=jnp.int32)
     segment = jnp.sum((position[:, None] >= doc_ends[None, :]).astype(jnp.int32), axis=1)
     heads_here = widths[0] // HEAD_WIDTH
-    query_grads, key_grads, value_gradient = attend_back_kernel(
+    low = attend_back_kernel(
         gathered, segment, heads_here, 0, heads_here, 2 * heads_here, 2 * heads_here + 1
     )
 
-    low = jnp.concatenate(
-        [query_grads, value_gradient.astype(jnp.bfloat16), key_grads.astype(jnp.bfloat16)], axis=1
-    )
     low_back = lax.all_to_all(low, "seq", split_axis=0, concat_axis=1, tiled=True)
     low_back = low_back.reshape(tok_rows, sequence_count, -1)
     v_end = widths[0] + widths[3]

time: 205 us -> 208 us (1.015)
  local copies, waits for them, and re-layouts: 16.7 us -> 19.6 us
  waiting for transfers between devices: 81 us -> 78.9 us
  transfers between devices with their start and end apart: 6 -> 6, of which waited for: 6 -> 6; matrix products, arithmetic and copies ran while one was open for 6% -> 7% of each run, Pallas kernels for 0% -> 0%
where the time goes in v9:
time: 208 us; the launch traced here: 207 us
  starting transfers between devices  80.2 us (39%)
  waiting for transfers between devices  78.9 us (38%)
  local copies, waits for them, and re-layouts  19.6 us (9%)
  Pallas kernels  13.4 us (6%)
  other arithmetic  10.9 us (5%)
  between operations  4.31 us (2%)
    all_to_all x1, waiting for transfers between devices, per_device(): lax.all_to_all(packed, 'seq', split_axis=1, concat_axis=0, tiled=True)  38.5 us
    all_to_all x1, starting transfers between devices, route(): spread = lax.all_to_all(flat, 'dp', 0, 0, tiled=True)  36 us
    all_to_all x1, starting transfers between devices, route_block(): spread = lax.all_to_all(flat, 'dp', 0, 0, tiled=True)  14.6 us
    all_to_all x1, waiting for transfers between devices, per_device(): lax.all_to_all(low, 'seq', split_axis=0, concat_axis=1, tiled=True)  14.4 us
    pallas_call x1, Pallas kernels, attend_back_kernel(): pl.pallas_call(attend_kernel, grid=(heads_of_query,), in_specs=[pl.BlockS...  13.4 us
    all_to_all x1, waiting for transfers between devices, route(): spread = lax.all_to_all(flat, 'dp', 0, 0, tiled=True)  10 us
    all_to_all x1, starting transfers between devices, per_device(): lax.all_to_all(packed, 'seq', split_axis=1, concat_axis=0, tiled=True)  9.9 us
    all_to_all x1, starting transfers between devices, route_block(): back = lax.all_to_all(routed, 'dp', 0, 0, tiled=True)  9.82 us
  transfers between devices with their start and end apart: 6, of which 6 were waited for; matrix products, arithmetic and copies ran while one was open for 7% of the time, Pallas kernels for 0%

profile of v9, /device:TPU:1, one launch (start us, length us, event | category | flops | bytes accessed | tf_op | source)
XLA Modules:
  0.0 207.4 jit_solution(6738428578075466526)
XLA Ops:
  0.6 1.7 copy.139
  2.4 14.6 %all-to-all-start = ((bf16[64,2,8,128]{3,2,1,0:T(8,128)(2,1)}), bf16[64,2,8,128]{3,2,1,0:T(8,128)(2,1)S(1)}, u32[]{:S(2)}, u32[]{:S(2)}) async-start(bf16[64,2,8,128]{3,2,1,0:T(8,128)(2,1)} %bitcast.41), calls=%async_computation | async-start | bytes 524288 | tf_op jit(solution)/shard_map/all_to_all | solution.py:166
  17.0 0.7 compare_select_fusion.2
  17.6 0.8 scatter_custom_fusion
  18.4 0.6 dynamic_slice.16
  20.3 0.7 compare_and_fusion.1
  21.0 0.7 bitcast_or_fusion
  21.7 0.7 compare_and_fusion.2
  23.0 0.8 constant_dynamic-slice_fusion.2
  23.8 0.6 fusion.5
  24.4 1.6 copy_bitcast_fusion
  26.5 1.8 pad_maximum_fusion
  28.3 0.9 all-to-all-done
  29.2 0.6 gather_fusion
  30.0 0.2 copy.115
  30.2 0.9 gather_fusion.2
  31.1 0.8 fusion
  31.9 9.8 %all-to-all-start.1 = ((bf16[64,2,2,128]{3,1,2,0:T(2,128)(2,1)}), bf16[64,2,2,128]{3,1,2,0:T(2,128)(2,1)S(1)}, u32[]{:S(2)}, u32[]{:S(2)}) async-start(bf16[64,2,2,128]{3,1,2,0:T(2,128)(2,1)} %fusion), calls=%async_computation.1 | async-start | bytes 131072 | tf_op jit(solution)/shard_map/all_to_all | solution.py:169
  41.7 0.7 iota_compare_fusion.3
  42.6 0.7 iota_compare_fusion.4
  43.3 8.5 %all-to-all-done.1 = bf16[64,2,2,128]{3,1,2,0:T(2,128)(2,1)S(1)} async-done(((bf16[64,2,2,128]{3,1,2,0:T(2,128)(2,1)}), bf16[64,2,2,128]{3,1,2,0:T(2,128)(2,1)S(1)}, u32[]{:S(2)}, u32[]{:S(2)}) %all-to-all-start.1) | async-done | bytes 65568 | tf_op jit(solution)/shard_map/all_to_all | solution.py:169
  52.4 0.7 constant_dynamic-update-slice_fusion
  53.1 9.9 %all-to-all-start.2 = ((bf16[128,8,1024]{2,0,1:T(8,128)(2,1)}), bf16[128,8,1024]{2,0,1:T(8,128)(2,1)S(1)}, u32[]{:S(2)}, u32[]{:S(2)}) async-start(bf16[128,8,1024]{2,0,1:T(8,128)(2,1)} %constant_dynamic-update-slice_fusion), calls=%async_computation.2 | async-start | bytes 4194304 | tf_op jit(solution)/shard_map/all_to_all | solution.py:224
  63.0 0.2 reduce-window.8
  63.3 0.2 copy.121.seg_row_ref
  63.5 38.5 %all-to-all-done.2 = bf16[128,8,1024]{2,0,1:T(8,128)(2,1)S(1)} async-done(((bf16[128,8,1024]{2,0,1:T(8,128)(2,1)}), bf16[128,8,1024]{2,0,1:T(8,128)(2,1)S(1)}, u32[]{:S(2)}, u32[]{:S(2)}) %all-to-all-start.2) | async-done | bytes 2097184 | tf_op jit(solution)/shard_map/all_to_all | solution.py:224
  102.0 13.4 %shard_map.94 = bf16[1024,640]{1,0:T(8,128)(2,1)S(1)} custom-call(s32[1024,1]{1,0:T(8,128)S(1)} %copy.121.seg_row_ref, s32[1,1024]{1,0:T(1,128)S(1)} %bitcast.62, bf16[1024,1024]{1,0:T(8,128)(2,1)S(1)} %bitcast.56, bf16[1024,1024]{1,0:T(8,128)(2,1)S(1)} %bitcast.57, bf16[1024,1024]{1,0:T(8,128)(2,1)S(1)} %bitcast.58, bf16[1024,1024]{1,0:T(8,128)(2,1)S(1)} %bitcast.59), custom_call_target="tpu_custom_call" | custom-call | flops 2516582400 | bytes 3407872 | tf_op jit(solution)/shard_map/pallas_call | solution.py:135
  115.5 1.1 copy-done.1
  116.5 2.4 %copy.122 = bf16[8,128,640]{1,2,0:T(8,128)(2,1)} copy(bf16[8,128,640]{2,1,0:T(8,128)(2,1)} %bitcast.60) | data formatting | bytes 2621440 | tf_op jit(solution)/shard_map/all_to_all | solution.py:238
  118.9 5.5 %all-to-all-start.3 = ((bf16[8,128,640]{1,2,0:T(8,128)(2,1)}), bf16[8,128,640]{1,2,0:T(8,128)(2,1)S(1)}, u32[]{:S(2)}, u32[]{:S(2)}) async-start(bf16[8,128,640]{1,2,0:T(8,128)(2,1)} %copy.122), calls=%async_computation.3 | async-start | bytes 2621440 | tf_op jit(solution)/shard_map/all_to_all | solution.py:238
  125.8 14.4 %all-to-all-done.3 = bf16[8,128,640]{1,2,0:T(8,128)(2,1)S(1)} async-done(((bf16[8,128,640]{1,2,0:T(8,128)(2,1)}), bf16[8,128,640]{1,2,0:T(8,128)(2,1)S(1)}, u32[]{:S(2)}, u32[]{:S(2)}) %all-to-all-start.3) | async-done | bytes 1310752 | tf_op jit(solution)/shard_map/all_to_all | solution.py:238
  140.6 0.5 broadcast.101
  141.1 1.0 reduce.1
  142.1 0.6 reshape.225
  142.7 36.0 %all-to-all-start.4 = ((bf16[64,2,256]{2,1,0:T(2,128)(2,1)}), bf16[64,2,256]{2,1,0:T(2,128)(2,1)S(1)}, u32[]{:S(2)}, u32[]{:S(2)}) async-start(bf16[64,2,256]{2,1,0:T(2,128)(2,1)} %reshape.225), calls=%async_computation.4 | async-start | bytes 131072 | tf_op jit(solution)/shard_map/all_to_all | solution.py:176
  178.8 10.0 %all-to-all-done.4 = bf16[64,2,256]{2,1,0:T(2,128)(2,1)S(1)} async-done(((bf16[64,2,256]{2,1,0:T(2,128)(2,1)}), bf16[64,2,256]{2,1,0:T(2,128)(2,1)S(1)}, u32[]{:S(2)}, u32[]{:S(2)}) %all-to-all-start.4) | async-done | bytes 65568 | tf_op jit(solution)/shard_map/all_to_all | solution.py:176
  188.9 0.7 gather_fusion.1
  189.6 0.7 reduce.2
  190.3 0.6 reshape.227
  191.0 4.4 %all-to-all-start.5 = ((bf16[64,2,256]{2,1,0:T(2,128)(2,1)}), bf16[64,2,256]{2,1,0:T(2,128)(2,1)S(1)}, u32[]{:S(2)}, u32[]{:S(2)}) async-start(bf16[64,2,256]{2,1,0:T(2,128)(2,1)} %reshape.227), calls=%async_computation.5 | async-start | bytes 131072 | tf_op jit(solution)/shard_map/all_to_all | solution.py:178
  195.4 0.7 iota_compare_fusion.1
  196.1 0.7 iota_compare_fusion.2
  196.8 1.2 copy.130
  198.0 0.8 copy.132
  198.9 6.7 %all-to-all-done.5 = bf16[64,2,256]{2,1,0:T(2,128)(2,1)S(1)} async-done(((bf16[64,2,256]{2,1,0:T(2,128)(2,1)}), bf16[64,2,256]{2,1,0:T(2,128)(2,1)S(1)}, u32[]{:S(2)}, u32[]{:S(2)}) %all-to-all-start.5) | async-done | bytes 65568 | tf_op jit(solution)/shard_map/all_to_all | solution.py:178
  205.6 0.4 reduce
  206.4 0.2 add_convert_fusion
  206.6 0.9 copy.131
  (43 shorter events, 2.4 us)
Async XLA Ops:
  0.6 25.8 %copy-start = (bf16[128,1024]{1,0:T(8,128)(2,1)S(1)}, bf16[128,1024]{1,0:T(8,128)(2,1)}, u32[]{:S(2)}) copy-start(bf16[128,1024]{1,0:T(8,128)(2,1)} %param.9) | copy-start | bytes 786436
  2.4 26.8 %all-to-all-start = ((bf16[64,2,8,128]{3,2,1,0:T(8,128)(2,1)}), bf16[64,2,8,128]{3,2,1,0:T(8,128)(2,1)S(1)}, u32[]{:S(2)}, u32[]{:S(2)}) async-start(bf16[64,2,8,128]{3,2,1,0:T(8,128)(2,1)} %bitcast.41), calls=%async_computation | async-start | bytes 524288 | tf_op jit(solution)/shard_map/all_to_all | solution.py:166
  26.5 15.9 %copy-start.2 = (bf16[128,1024]{1,0:T(8,128)(2,1)S(1)}, bf16[128,1024]{1,0:T(8,128)(2,1)}, u32[]{:S(2)}) copy-start(bf16[128,1024]{1,0:T(8,128)(2,1)} %param.8) | copy-start | bytes 786436
  31.9 19.9 %all-to-all-start.1 = ((bf16[64,2,2,128]{3,1,2,0:T(2,128)(2,1)}), bf16[64,2,2,128]{3,1,2,0:T(2,128)(2,1)S(1)}, u32[]{:S(2)}, u32[]{:S(2)}) async-start(bf16[64,2,2,128]{3,1,2,0:T(2,128)(2,1)} %fusion), calls=%async_computation.1 | async-start | bytes 131072 | tf_op jit(solution)/shard_map/all_to_all | solution.py:169
  53.1 9.9 %copy-start.3 = (s32[1,4]{1,0:T(1,128)S(1)}, s32[1,4]{1,0:T(1,128)}, u32[]{:S(2)}) copy-start(s32[1,4]{1,0:T(1,128)} %param.11) | copy-start | bytes 52
  53.1 48.9 %all-to-all-start.2 = ((bf16[128,8,1024]{2,0,1:T(8,128)(2,1)}), bf16[128,8,1024]{2,0,1:T(8,128)(2,1)S(1)}, u32[]{:S(2)}, u32[]{:S(2)}) async-start(bf16[128,8,1024]{2,0,1:T(8,128)(2,1)} %constant_dynamic-update-slice_fusion), calls=%async_computation.2 | async-start | bytes 4194304 | tf_op jit(solution)/shard_map/all_to_all | solution.py:224
  115.4 1.1 copy-start.1
  118.9 21.2 %all-to-all-start.3 = ((bf16[8,128,640]{1,2,0:T(8,128)(2,1)}), bf16[8,128,640]{1,2,0:T(8,128)(2,1)S(1)}, u32[]{:S(2)}, u32[]{:S(2)}) async-start(bf16[8,128,640]{1,2,0:T(8,128)(2,1)} %copy.122), calls=%async_computation.3 | async-start | bytes 2621440 | tf_op jit(solution)/shard_map/all_to_all | solution.py:238
  142.7 46.0 %all-to-all-start.4 = ((bf16[64,2,256]{2,1,0:T(2,128)(2,1)}), bf16[64,2,256]{2,1,0:T(2,128)(2,1)S(1)}, u32[]{:S(2)}, u32[]{:S(2)}) async-start(bf16[64,2,256]{2,1,0:T(2,128)(2,1)} %reshape.225), calls=%async_computation.4 | async-start | bytes 131072 | tf_op jit(solution)/shard_map/all_to_all | solution.py:176
  191.0 14.6 %all-to-all-start.5 = ((bf16[64,2,256]{2,1,0:T(2,128)(2,1)}), bf16[64,2,256]{2,1,0:T(2,128)(2,1)S(1)}, u32[]{:S(2)}, u32[]{:S(2)}) async-start(bf16[64,2,256]{2,1,0:T(2,128)(2,1)} %reshape.227), calls=%async_computation.5 | async-start | bytes 131072 | tf_op jit(solution)/shard_map/all_to_all | solution.py:178

commit v10 on v9

--- a/solution.py
+++ b/solution.py
@@ -209,12 +209,9 @@
     def cols(x):
         return x.reshape(tok_rows, sequence_count, -1)
 
-    pre = jnp.concatenate(
-        [cols(queries), cols(output_gradient), jnp.zeros_like(cols(keys)), cols(values)], axis=2
-    )
-    pre = lax.optimization_barrier(pre)
-    key_at = (queries.shape[1] + output_gradient.shape[1]) // sequence_count
-    packed = lax.dynamic_update_slice(pre, cols(used_keys), (0, 0, key_at))
+    packed = jnp.concatenate(
+        [cols(queries), cols(output_gradient), cols(used_keys), cols(values)], axis=2
+    )
     widths = (
         queries.shape[1] // sequence_count,
         output_gradient.shape[1] // sequence_count,

time: 208 us -> 207 us (level)
  waiting for transfers between devices: 78.9 us -> 81.2 us
    unnamed x18 -> x20, local copies, waits for them, and re-layouts: 7.28 us -> 7.32 us
  transfers between devices with their start and end apart: 6 -> 6, of which waited for: 6 -> 6; matrix products, arithmetic and copies ran while one was open for 7% -> 6% of each run, Pallas kernels for 0% -> 0%
where the time goes in v10:
time: 207 us; the launch traced here: 206 us
  waiting for transfers between devices  81.2 us (39%)
  starting transfers between devices  78.2 us (38%)
  local copies, waits for them, and re-layouts  18.7 us (9%)
  Pallas kernels  13.5 us (7%)
  other arithmetic  10.6 us (5%)
  between operations  4.2 us (2%)
    all_to_all x1, waiting for transfers between devices, per_device(): lax.all_to_all(packed, 'seq', split_axis=1, concat_axis=0, tiled=True)  38.5 us
    all_to_all x1, starting transfers between devices, route(): spread = lax.all_to_all(flat, 'dp', 0, 0, tiled=True)  36 us
    all_to_all x1, starting transfers between devices, route_block(): spread = lax.all_to_all(flat, 'dp', 0, 0, tiled=True)  14.6 us
    all_to_all x1, waiting for transfers between devices, per_device(): lax.all_to_all(low, 'seq', split_axis=0, concat_axis=1, tiled=True)  14.5 us
    pallas_call x1, Pallas kernels, attend_back_kernel(): pl.pallas_call(attend_kernel, grid=(heads_of_query,), in_specs=[pl.BlockS...  13.5 us
    all_to_all x1, waiting for transfers between devices, route(): spread = lax.all_to_all(flat, 'dp', 0, 0, tiled=True)  10 us
    all_to_all x1, starting transfers between devices, per_device(): lax.all_to_all(packed, 'seq', split_axis=1, concat_axis=0, tiled=True)  9.9 us
    all_to_all x1, waiting for transfers between devices, route_block(): back = lax.all_to_all(routed, 'dp', 0, 0, tiled=True)  8.59 us
  transfers between devices with their start and end apart: 6, of which 6 were waited for; matrix products, arithmetic and copies ran while one was open for 6% of the time, Pallas kernels for 0%

profile of v10, /device:TPU:1, one launch (start us, length us, event | category | flops | bytes accessed | tf_op | source)
XLA Modules:
  0.0 206.4 jit_solution(10304728366986657622)
XLA Ops:
  0.7 1.8 copy.134
  2.4 14.6 %all-to-all-start = ((bf16[64,2,8,128]{3,2,1,0:T(8,128)(2,1)}), bf16[64,2,8,128]{3,2,1,0:T(8,128)(2,1)S(1)}, u32[]{:S(2)}, u32[]{:S(2)}) async-start(bf16[64,2,8,128]{3,2,1,0:T(8,128)(2,1)} %bitcast.41), calls=%async_computation | async-start | bytes 524288 | tf_op jit(solution)/shard_map/all_to_all | solution.py:166
  17.0 0.7 compare_select_fusion.2
  17.7 0.8 scatter_custom_fusion
  18.5 0.6 dynamic_slice.16
  20.4 0.7 bitcast_or_fusion
  21.1 0.7 compare_and_fusion.2
  22.4 0.8 constant_dynamic-slice_fusion.2
  23.7 0.6 fusion.5
  24.2 0.7 compare_and_fusion.1
  24.9 1.4 copy_bitcast_fusion
  26.3 2.9 %all-to-all-done = bf16[64,2,8,128]{3,2,1,0:T(8,128)(2,1)S(1)} async-done(((bf16[64,2,8,128]{3,2,1,0:T(8,128)(2,1)}), bf16[64,2,8,128]{3,2,1,0:T(8,128)(2,1)S(1)}, u32[]{:S(2)}, u32[]{:S(2)}) %all-to-all-start) | async-done | bytes 262176 | tf_op jit(solution)/shard_map/all_to_all | solution.py:166
  29.3 0.6 gather_fusion
  30.0 0.2 copy.107
  30.3 0.9 gather_fusion.2
  31.1 0.8 fusion
  32.0 7.8 %all-to-all-start.1 = ((bf16[64,2,2,128]{3,1,2,0:T(2,128)(2,1)}), bf16[64,2,2,128]{3,1,2,0:T(2,128)(2,1)S(1)}, u32[]{:S(2)}, u32[]{:S(2)}) async-start(bf16[64,2,2,128]{3,1,2,0:T(2,128)(2,1)} %fusion), calls=%async_computation.1 | async-start | bytes 131072 | tf_op jit(solution)/shard_map/all_to_all | solution.py:169
  39.8 0.7 iota_compare_fusion.3
  40.6 0.6 iota_compare_fusion.4
  41.2 8.6 %all-to-all-done.1 = bf16[64,2,2,128]{3,1,2,0:T(2,128)(2,1)S(1)} async-done(((bf16[64,2,2,128]{3,1,2,0:T(2,128)(2,1)}), bf16[64,2,2,128]{3,1,2,0:T(2,128)(2,1)S(1)}, u32[]{:S(2)}, u32[]{:S(2)}) %all-to-all-start.1) | async-done | bytes 65568 | tf_op jit(solution)/shard_map/all_to_all | solution.py:169
  50.2 0.2 copy.114
  50.4 1.7 pad_maximum_fusion
  52.1 9.9 %all-to-all-start.2 = ((bf16[128,8,1024]{2,0,1:T(8,128)(2,1)}), bf16[128,8,1024]{2,0,1:T(8,128)(2,1)S(1)}, u32[]{:S(2)}, u32[]{:S(2)}) async-start(bf16[128,8,1024]{2,0,1:T(8,128)(2,1)} %pad_maximum_fusion), calls=%async_computation.2 | async-start | bytes 4194304 | tf_op jit(solution)/shard_map/all_to_all | solution.py:221
  62.0 0.2 reduce-window.8
  62.2 0.2 copy.116.seg_row_ref
  62.5 38.5 %all-to-all-done.2 = bf16[128,8,1024]{2,0,1:T(8,128)(2,1)S(1)} async-done(((bf16[128,8,1024]{2,0,1:T(8,128)(2,1)}), bf16[128,8,1024]{2,0,1:T(8,128)(2,1)S(1)}, u32[]{:S(2)}, u32[]{:S(2)}) %all-to-all-start.2) | async-done | bytes 2097184 | tf_op jit(solution)/shard_map/all_to_all | solution.py:221
  100.9 13.5 %shard_map.94 = bf16[1024,640]{1,0:T(8,128)(2,1)S(1)} custom-call(s32[1024,1]{1,0:T(8,128)S(1)} %copy.116.seg_row_ref, s32[1,1024]{1,0:T(1,128)S(1)} %bitcast.62, bf16[1024,1024]{1,0:T(8,128)(2,1)S(1)} %bitcast.56, bf16[1024,1024]{1,0:T(8,128)(2,1)S(1)} %bitcast.57, bf16[1024,1024]{1,0:T(8,128)(2,1)S(1)} %bitcast.58, bf16[1024,1024]{1,0:T(8,128)(2,1)S(1)} %bitcast.59), custom_call_target="tpu_custom_call" | custom-call | flops 2516582400 | bytes 3407872 | tf_op jit(solution)/shard_map/pallas_call | solution.py:135
  114.4 1.1 copy-done.1
  115.5 2.4 %copy.117 = bf16[8,128,640]{1,2,0:T(8,128)(2,1)} copy(bf16[8,128,640]{2,1,0:T(8,128)(2,1)} %bitcast.60) | data formatting | bytes 2621440 | tf_op jit(solution)/shard_map/all_to_all | solution.py:235
  117.9 5.5 %all-to-all-start.3 = ((bf16[8,128,640]{1,2,0:T(8,128)(2,1)}), bf16[8,128,640]{1,2,0:T(8,128)(2,1)S(1)}, u32[]{:S(2)}, u32[]{:S(2)}) async-start(bf16[8,128,640]{1,2,0:T(8,128)(2,1)} %copy.117), calls=%async_computation.3 | async-start | bytes 2621440 | tf_op jit(solution)/shard_map/all_to_all | solution.py:235
  124.6 14.5 %all-to-all-done.3 = bf16[8,128,640]{1,2,0:T(8,128)(2,1)S(1)} async-done(((bf16[8,128,640]{1,2,0:T(8,128)(2,1)}), bf16[8,128,640]{1,2,0:T(8,128)(2,1)S(1)}, u32[]{:S(2)}, u32[]{:S(2)}) %all-to-all-start.3) | async-done | bytes 1310752 | tf_op jit(solution)/shard_map/all_to_all | solution.py:235
  139.5 0.5 broadcast.99
  140.0 1.0 reduce.1
  141.1 0.6 reshape.225
  141.7 36.0 %all-to-all-start.4 = ((bf16[64,2,256]{2,1,0:T(2,128)(2,1)}), bf16[64,2,256]{2,1,0:T(2,128)(2,1)S(1)}, u32[]{:S(2)}, u32[]{:S(2)}) async-start(bf16[64,2,256]{2,1,0:T(2,128)(2,1)} %reshape.225), calls=%async_computation.4 | async-start | bytes 131072 | tf_op jit(solution)/shard_map/all_to_all | solution.py:176
  177.8 10.0 %all-to-all-done.4 = bf16[64,2,256]{2,1,0:T(2,128)(2,1)S(1)} async-done(((bf16[64,2,256]{2,1,0:T(2,128)(2,1)}), bf16[64,2,256]{2,1,0:T(2,128)(2,1)S(1)}, u32[]{:S(2)}, u32[]{:S(2)}) %all-to-all-start.4) | async-done | bytes 65568 | tf_op jit(solution)/shard_map/all_to_all | solution.py:176
  187.8 0.7 gather_fusion.1
  188.6 0.7 reduce.2
  189.3 0.6 reshape.227
  189.9 4.4 %all-to-all-start.5 = ((bf16[64,2,256]{2,1,0:T(2,128)(2,1)}), bf16[64,2,256]{2,1,0:T(2,128)(2,1)S(1)}, u32[]{:S(2)}, u32[]{:S(2)}) async-start(bf16[64,2,256]{2,1,0:T(2,128)(2,1)} %reshape.227), calls=%async_computation.5 | async-start | bytes 131072 | tf_op jit(solution)/shard_map/all_to_all | solution.py:178
  194.4 0.7 iota_compare_fusion.1
  195.1 0.7 iota_compare_fusion.2
  195.8 1.2 copy.125
  197.0 0.8 copy.127
  197.8 6.7 %all-to-all-done.5 = bf16[64,2,256]{2,1,0:T(2,128)(2,1)S(1)} async-done(((bf16[64,2,256]{2,1,0:T(2,128)(2,1)}), bf16[64,2,256]{2,1,0:T(2,128)(2,1)S(1)}, u32[]{:S(2)}, u32[]{:S(2)}) %all-to-all-start.5) | async-done | bytes 65568 | tf_op jit(solution)/shard_map/all_to_all | solution.py:178
  204.6 0.4 reduce
  205.3 0.2 add_convert_fusion
  205.5 0.9 copy.126
  (42 shorter events, 2.2 us)
Async XLA Ops:
  0.6 23.0 %copy-start = (bf16[128,1024]{1,0:T(8,128)(2,1)S(1)}, bf16[128,1024]{1,0:T(8,128)(2,1)}, u32[]{:S(2)}) copy-start(bf16[128,1024]{1,0:T(8,128)(2,1)} %param.9) | copy-start | bytes 786436
  0.6 24.3 %copy-start.3 = (bf16[128,3072]{1,0:T(8,128)(2,1)S(1)}, bf16[128,3072]{1,0:T(8,128)(2,1)}, u32[]{:S(2)}) copy-start(bf16[128,3072]{1,0:T(8,128)(2,1)} %param.10) | copy-start | bytes 2359300
  2.4 26.8 %all-to-all-start = ((bf16[64,2,8,128]{3,2,1,0:T(8,128)(2,1)}), bf16[64,2,8,128]{3,2,1,0:T(8,128)(2,1)S(1)}, u32[]{:S(2)}, u32[]{:S(2)}) async-start(bf16[64,2,8,128]{3,2,1,0:T(8,128)(2,1)} %bitcast.41), calls=%async_computation | async-start | bytes 524288 | tf_op jit(solution)/shard_map/all_to_all | solution.py:166
  24.9 15.5 %copy-start.2 = (bf16[128,1024]{1,0:T(8,128)(2,1)S(1)}, bf16[128,1024]{1,0:T(8,128)(2,1)}, u32[]{:S(2)}) copy-start(bf16[128,1024]{1,0:T(8,128)(2,1)} %param.8) | copy-start | bytes 786436
  32.0 17.8 %all-to-all-start.1 = ((bf16[64,2,2,128]{3,1,2,0:T(2,128)(2,1)}), bf16[64,2,2,128]{3,1,2,0:T(2,128)(2,1)S(1)}, u32[]{:S(2)}, u32[]{:S(2)}) async-start(bf16[64,2,2,128]{3,1,2,0:T(2,128)(2,1)} %fusion), calls=%async_computation.1 | async-start | bytes 131072 | tf_op jit(solution)/shard_map/all_to_all | solution.py:169
  52.1 9.9 %copy-start.4 = (s32[1,4]{1,0:T(1,128)S(1)}, s32[1,4]{1,0:T(1,128)}, u32[]{:S(2)}) copy-start(s32[1,4]{1,0:T(1,128)} %param.11) | copy-start | bytes 52
  52.1 48.9 %all-to-all-start.2 = ((bf16[128,8,1024]{2,0,1:T(8,128)(2,1)}), bf16[128,8,1024]{2,0,1:T(8,128)(2,1)S(1)}, u32[]{:S(2)}, u32[]{:S(2)}) async-start(bf16[128,8,1024]{2,0,1:T(8,128)(2,1)} %pad_maximum_fusion), calls=%async_computation.2 | async-start | bytes 4194304 | tf_op jit(solution)/shard_map/all_to_all | solution.py:221
  114.4 1.1 copy-start.1
  117.9 21.2 %all-to-all-start.3 = ((bf16[8,128,640]{1,2,0:T(8,128)(2,1)}), bf16[8,128,640]{1,2,0:T(8,128)(2,1)S(1)}, u32[]{:S(2)}, u32[]{:S(2)}) async-start(bf16[8,128,640]{1,2,0:T(8,128)(2,1)} %copy.117), calls=%async_computation.3 | async-start | bytes 2621440 | tf_op jit(solution)/shard_map/all_to_all | solution.py:235
  141.7 46.0 %all-to-all-start.4 = ((bf16[64,2,256]{2,1,0:T(2,128)(2,1)}), bf16[64,2,256]{2,1,0:T(2,128)(2,1)S(1)}, u32[]{:S(2)}, u32[]{:S(2)}) async-start(bf16[64,2,256]{2,1,0:T(2,128)(2,1)} %reshape.225), calls=%async_computation.4 | async-start | bytes 131072 | tf_op jit(solution)/shard_map/all_to_all | solution.py:176
  189.9 14.6 %all-to-all-start.5 = ((bf16[64,2,256]{2,1,0:T(2,128)(2,1)}), bf16[64,2,256]{2,1,0:T(2,128)(2,1)S(1)}, u32[]{:S(2)}, u32[]{:S(2)}) async-start(bf16[64,2,256]{2,1,0:T(2,128)(2,1)} %reshape.227), calls=%async_computation.5 | async-start | bytes 131072 | tf_op jit(solution)/shard_map/all_to_all | solution.py:178

commit v11 on v8

--- a/solution.py
+++ b/solution.py
@@ -68,7 +68,7 @@
     return lax.fori_loop(0, heads_of_query, one_head, initial)
 
 
-BLOCK_ROWS = 256
+BLOCK_ROWS = 512
 
 
 def attend_kernel(seg_row_ref, seg_col_ref, q_ref, g_ref, k_ref, v_ref, dq_ref, dk_ref, dv_ref):
@@ -121,7 +121,7 @@
     seg_col = segment.reshape(1, length)
     full = lambda h: (0, 0)
     col = lambda b: pl.BlockSpec((length, HEAD_WIDTH), lambda h: (0, b))
-    flops = 5 * 2 * length * length * HEAD_WIDTH * heads_of_query * 10 // 16
+    flops = 5 * 2 * length * length * HEAD_WIDTH * heads_of_query * 12 // 16
     return pl.pallas_call(
         attend_kernel,
         grid=(heads_of_query,),
@@ -148,7 +148,7 @@
         ),
         cost_estimate=pl.CostEstimate(
             flops=flops,
-            transcendentals=length * length * heads_of_query * 10 // 16,
+            transcendentals=length * length * heads_of_query * 12 // 16,
             bytes_accessed=length * HEAD_WIDTH * (2 * 2 * heads_of_query + 2 * 2 + 2 * heads_of_query + 8),
         ),
     )(seg_row, seg_col, gathered, gathered, gathered, gathered)

time: 205 us -> 203 us (level)
  Pallas kernels: 13.5 us -> 11 us
    pallas_call x1, Pallas kernels: 13.5 us -> 11 us  [attend_back_kernel(): pl.pallas_call(attend_kernel, grid=(heads_of_query,), in_specs=[pl.BlockS...]
where the time goes in v11:
time: 203 us; the launch traced here: 202 us
  waiting for transfers between devices  81 us (40%)
  starting transfers between devices  78.2 us (39%)
  local copies, waits for them, and re-layouts  16.7 us (8%)
  Pallas kernels  11 us (5%)
  other arithmetic  10.9 us (5%)
  between operations  4.27 us (2%)
    all_to_all x1, waiting for transfers between devices, per_device(): lax.all_to_all(packed, 'seq', split_axis=1, concat_axis=0, tiled=True)  38.5 us
    all_to_all x1, starting transfers between devices, route(): spread = lax.all_to_all(flat, 'dp', 0, 0, tiled=True)  36 us
    all_to_all x1, starting transfers between devices, route_block(): spread = lax.all_to_all(flat, 'dp', 0, 0, tiled=True)  14.6 us
    all_to_all x1, waiting for transfers between devices, per_device(): lax.all_to_all(low, 'seq', split_axis=0, concat_axis=1, tiled=True)  14.4 us
    pallas_call x1, Pallas kernels, attend_back_kernel(): pl.pallas_call(attend_kernel, grid=(heads_of_query,), in_specs=[pl.BlockS...  11 us
    all_to_all x1, waiting for transfers between devices, route(): spread = lax.all_to_all(flat, 'dp', 0, 0, tiled=True)  10 us
    all_to_all x1, starting transfers between devices, per_device(): lax.all_to_all(packed, 'seq', split_axis=1, concat_axis=0, tiled=True)  9.9 us
    all_to_all x1, waiting for transfers between devices, route_block(): back = lax.all_to_all(routed, 'dp', 0, 0, tiled=True)  8.53 us
  transfers between devices with their start and end apart: 6, of which 6 were waited for; matrix products, arithmetic and copies ran while one was open for 6% of the time, Pallas kernels for 0%

profile of v11, /device:TPU:1, one launch (start us, length us, event | category | flops | bytes accessed | tf_op | source)
XLA Modules:
  0.0 202.2 jit_solution(14082661916138836267)
XLA Ops:
  0.7 1.8 copy.134
  2.4 14.6 %all-to-all-start = ((bf16[64,2,8,128]{3,2,1,0:T(8,128)(2,1)}), bf16[64,2,8,128]{3,2,1,0:T(8,128)(2,1)S(1)}, u32[]{:S(2)}, u32[]{:S(2)}) async-start(bf16[64,2,8,128]{3,2,1,0:T(8,128)(2,1)} %bitcast.41), calls=%async_computation | async-start | bytes 524288 | tf_op jit(solution)/shard_map/all_to_all | solution.py:161
  17.0 0.7 compare_select_fusion.2
  17.7 0.8 scatter_custom_fusion
  18.5 0.6 dynamic_slice.16
  20.4 0.7 bitcast_or_fusion
  21.1 0.7 compare_and_fusion.2
  22.4 0.8 constant_dynamic-slice_fusion.2
  23.7 0.6 fusion.5
  24.2 0.7 compare_and_fusion.1
  24.9 1.4 copy_bitcast_fusion
  26.3 2.9 %all-to-all-done = bf16[64,2,8,128]{3,2,1,0:T(8,128)(2,1)S(1)} async-done(((bf16[64,2,8,128]{3,2,1,0:T(8,128)(2,1)}), bf16[64,2,8,128]{3,2,1,0:T(8,128)(2,1)S(1)}, u32[]{:S(2)}, u32[]{:S(2)}) %all-to-all-start) | async-done | bytes 262176 | tf_op jit(solution)/shard_map/all_to_all | solution.py:161
  29.3 0.6 gather_fusion
  30.0 0.2 copy.107
  30.3 0.9 gather_fusion.2
  31.1 0.8 fusion
  32.0 7.8 %all-to-all-start.1 = ((bf16[64,2,2,128]{3,1,2,0:T(2,128)(2,1)}), bf16[64,2,2,128]{3,1,2,0:T(2,128)(2,1)S(1)}, u32[]{:S(2)}, u32[]{:S(2)}) async-start(bf16[64,2,2,128]{3,1,2,0:T(2,128)(2,1)} %fusion), calls=%async_computation.1 | async-start | bytes 131072 | tf_op jit(solution)/shard_map/all_to_all | solution.py:164
  39.8 0.7 iota_compare_fusion.3
  40.4 0.2 copy.111
  40.6 0.6 iota_compare_fusion.4
  41.3 8.5 %all-to-all-done.1 = bf16[64,2,2,128]{3,1,2,0:T(2,128)(2,1)S(1)} async-done(((bf16[64,2,2,128]{3,1,2,0:T(2,128)(2,1)}), bf16[64,2,2,128]{3,1,2,0:T(2,128)(2,1)S(1)}, u32[]{:S(2)}, u32[]{:S(2)}) %all-to-all-start.1) | async-done | bytes 65568 | tf_op jit(solution)/shard_map/all_to_all | solution.py:164
  50.2 0.2 copy.114
  50.4 1.7 pad_maximum_fusion
  52.1 9.9 %all-to-all-start.2 = ((bf16[128,8,1024]{2,0,1:T(8,128)(2,1)}), bf16[128,8,1024]{2,0,1:T(8,128)(2,1)S(1)}, u32[]{:S(2)}, u32[]{:S(2)}) async-start(bf16[128,8,1024]{2,0,1:T(8,128)(2,1)} %pad_maximum_fusion), calls=%async_computation.2 | async-start | bytes 4194304 | tf_op jit(solution)/shard_map/all_to_all | solution.py:216
  62.0 0.2 reduce-window.8
  62.3 0.2 copy.116.seg_row_ref
  62.5 38.5 %all-to-all-done.2 = bf16[128,8,1024]{2,0,1:T(8,128)(2,1)S(1)} async-done(((bf16[128,8,1024]{2,0,1:T(8,128)(2,1)}), bf16[128,8,1024]{2,0,1:T(8,128)(2,1)S(1)}, u32[]{:S(2)}, u32[]{:S(2)}) %all-to-all-start.2) | async-done | bytes 2097184 | tf_op jit(solution)/shard_map/all_to_all | solution.py:216
  101.0 11.0 %shard_map.94 = (bf16[1024,384]{1,0:T(8,128)(2,1)S(1)}, f32[1024,128]{1,0:T(8,128)S(1)}, f32[1024,128]{1,0:T(8,128)S(1)}) custom-call(s32[1024,1]{1,0:T(8,128)S(1)} %copy.116.seg_row_ref, s32[1,1024]{1,0:T(1,128)S(1)} %bitcast.61, bf16[1024,1024]{1,0:T(8,128)(2,1)S(1)} %bitcast.56, bf16[1024,1024]{1,0:T(8,128)(2,1)S(1)} %bitcast.57, ...), custom_call_target="tpu_custom_call" | custom-call | flops 3019898880 | bytes 3932160 | tf_op jit(solution)/shard_map/pallas_call | solution.py:125
  112.2 1.5 copy.117
  113.7 5.5 %all-to-all-start.3 = ((bf16[8,128,640]{1,2,0:T(8,128)(2,1)}), bf16[8,128,640]{1,2,0:T(8,128)(2,1)S(1)}, u32[]{:S(2)}, u32[]{:S(2)}) async-start(bf16[8,128,640]{1,2,0:T(8,128)(2,1)} %copy.117), calls=%async_computation.3 | async-start | bytes 2621440 | tf_op jit(solution)/shard_map/all_to_all | solution.py:233
  120.5 14.4 %all-to-all-done.3 = bf16[8,128,640]{1,2,0:T(8,128)(2,1)S(1)} async-done(((bf16[8,128,640]{1,2,0:T(8,128)(2,1)}), bf16[8,128,640]{1,2,0:T(8,128)(2,1)S(1)}, u32[]{:S(2)}, u32[]{:S(2)}) %all-to-all-start.3) | async-done | bytes 1310752 | tf_op jit(solution)/shard_map/all_to_all | solution.py:233
  135.3 0.5 broadcast.99
  135.8 1.0 reduce.1
  136.8 0.6 reshape.225
  137.5 36.0 %all-to-all-start.4 = ((bf16[64,2,256]{2,1,0:T(2,128)(2,1)}), bf16[64,2,256]{2,1,0:T(2,128)(2,1)S(1)}, u32[]{:S(2)}, u32[]{:S(2)}) async-start(bf16[64,2,256]{2,1,0:T(2,128)(2,1)} %reshape.225), calls=%async_computation.4 | async-start | bytes 131072 | tf_op jit(solution)/shard_map/all_to_all | solution.py:171
  173.5 10.0 %all-to-all-done.4 = bf16[64,2,256]{2,1,0:T(2,128)(2,1)S(1)} async-done(((bf16[64,2,256]{2,1,0:T(2,128)(2,1)}), bf16[64,2,256]{2,1,0:T(2,128)(2,1)S(1)}, u32[]{:S(2)}, u32[]{:S(2)}) %all-to-all-start.4) | async-done | bytes 65568 | tf_op jit(solution)/shard_map/all_to_all | solution.py:171
  183.6 0.7 gather_fusion.1
  184.4 0.7 reduce.2
  185.1 0.6 reshape.227
  185.7 4.4 %all-to-all-start.5 = ((bf16[64,2,256]{2,1,0:T(2,128)(2,1)}), bf16[64,2,256]{2,1,0:T(2,128)(2,1)S(1)}, u32[]{:S(2)}, u32[]{:S(2)}) async-start(bf16[64,2,256]{2,1,0:T(2,128)(2,1)} %reshape.227), calls=%async_computation.5 | async-start | bytes 131072 | tf_op jit(solution)/shard_map/all_to_all | solution.py:173
  190.2 0.7 iota_compare_fusion.1
  190.9 0.7 iota_compare_fusion.2
  191.6 1.2 copy.125
  192.7 0.8 copy.127
  193.6 6.7 %all-to-all-done.5 = bf16[64,2,256]{2,1,0:T(2,128)(2,1)S(1)} async-done(((bf16[64,2,256]{2,1,0:T(2,128)(2,1)}), bf16[64,2,256]{2,1,0:T(2,128)(2,1)S(1)}, u32[]{:S(2)}, u32[]{:S(2)}) %all-to-all-start.5) | async-done | bytes 65568 | tf_op jit(solution)/shard_map/all_to_all | solution.py:173
  200.4 0.4 reduce
  201.1 0.2 add_convert_fusion
  201.3 0.9 copy.126
  (43 shorter events, 2.3 us)
Async XLA Ops:
  0.6 23.0 %copy-start = (bf16[128,1024]{1,0:T(8,128)(2,1)S(1)}, bf16[128,1024]{1,0:T(8,128)(2,1)}, u32[]{:S(2)}) copy-start(bf16[128,1024]{1,0:T(8,128)(2,1)} %param.9) | copy-start | bytes 786436
  0.6 24.3 %copy-start.2 = (bf16[128,3072]{1,0:T(8,128)(2,1)S(1)}, bf16[128,3072]{1,0:T(8,128)(2,1)}, u32[]{:S(2)}) copy-start(bf16[128,3072]{1,0:T(8,128)(2,1)} %param.10) | copy-start | bytes 2359300
  2.4 26.8 %all-to-all-start = ((bf16[64,2,8,128]{3,2,1,0:T(8,128)(2,1)}), bf16[64,2,8,128]{3,2,1,0:T(8,128)(2,1)S(1)}, u32[]{:S(2)}, u32[]{:S(2)}) async-start(bf16[64,2,8,128]{3,2,1,0:T(8,128)(2,1)} %bitcast.41), calls=%async_computation | async-start | bytes 524288 | tf_op jit(solution)/shard_map/all_to_all | solution.py:161
  24.9 15.5 %copy-start.1 = (bf16[128,1024]{1,0:T(8,128)(2,1)S(1)}, bf16[128,1024]{1,0:T(8,128)(2,1)}, u32[]{:S(2)}) copy-start(bf16[128,1024]{1,0:T(8,128)(2,1)} %param.8) | copy-start | bytes 786436
  32.0 17.8 %all-to-all-start.1 = ((bf16[64,2,2,128]{3,1,2,0:T(2,128)(2,1)}), bf16[64,2,2,128]{3,1,2,0:T(2,128)(2,1)S(1)}, u32[]{:S(2)}, u32[]{:S(2)}) async-start(bf16[64,2,2,128]{3,1,2,0:T(2,128)(2,1)} %fusion), calls=%async_computation.1 | async-start | bytes 131072 | tf_op jit(solution)/shard_map/all_to_all | solution.py:164
  52.1 9.9 %copy-start.3 = (s32[1,4]{1,0:T(1,128)S(1)}, s32[1,4]{1,0:T(1,128)}, u32[]{:S(2)}) copy-start(s32[1,4]{1,0:T(1,128)} %param.11) | copy-start | bytes 52
  52.1 48.9 %all-to-all-start.2 = ((bf16[128,8,1024]{2,0,1:T(8,128)(2,1)}), bf16[128,8,1024]{2,0,1:T(8,128)(2,1)S(1)}, u32[]{:S(2)}, u32[]{:S(2)}) async-start(bf16[128,8,1024]{2,0,1:T(8,128)(2,1)} %pad_maximum_fusion), calls=%async_computation.2 | async-start | bytes 4194304 | tf_op jit(solution)/shard_map/all_to_all | solution.py:216
  113.7 21.2 %all-to-all-start.3 = ((bf16[8,128,640]{1,2,0:T(8,128)(2,1)}), bf16[8,128,640]{1,2,0:T(8,128)(2,1)S(1)}, u32[]{:S(2)}, u32[]{:S(2)}) async-start(bf16[8,128,640]{1,2,0:T(8,128)(2,1)} %copy.117), calls=%async_computation.3 | async-start | bytes 2621440 | tf_op jit(solution)/shard_map/all_to_all | solution.py:233
  137.5 46.0 %all-to-all-start.4 = ((bf16[64,2,256]{2,1,0:T(2,128)(2,1)}), bf16[64,2,256]{2,1,0:T(2,128)(2,1)S(1)}, u32[]{:S(2)}, u32[]{:S(2)}) async-start(bf16[64,2,256]{2,1,0:T(2,128)(2,1)} %reshape.225), calls=%async_computation.4 | async-start | bytes 131072 | tf_op jit(solution)/shard_map/all_to_all | solution.py:171
  185.7 14.6 %all-to-all-start.5 = ((bf16[64,2,256]{2,1,0:T(2,128)(2,1)}), bf16[64,2,256]{2,1,0:T(2,128)(2,1)S(1)}, u32[]{:S(2)}, u32[]{:S(2)}) async-start(bf16[64,2,256]{2,1,0:T(2,128)(2,1)} %reshape.227), calls=%async_computation.5 | async-start | bytes 131072 | tf_op jit(solution)/shard_map/all_to_all | solution.py:173

commit v12 on v11

--- a/solution.py
+++ b/solution.py
@@ -68,7 +68,7 @@
     return lax.fori_loop(0, heads_of_query, one_head, initial)
 
 
-BLOCK_ROWS = 512
+BLOCK_ROWS = 1024
 
 
 def attend_kernel(seg_row_ref, seg_col_ref, q_ref, g_ref, k_ref, v_ref, dq_ref, dk_ref, dv_ref):
@@ -121,7 +121,7 @@
     seg_col = segment.reshape(1, length)
     full = lambda h: (0, 0)
     col = lambda b: pl.BlockSpec((length, HEAD_WIDTH), lambda h: (0, b))
-    flops = 5 * 2 * length * length * HEAD_WIDTH * heads_of_query * 12 // 16
+    flops = 5 * 2 * length * length * HEAD_WIDTH * heads_of_query * 16 // 16
     return pl.pallas_call(
         attend_kernel,
         grid=(heads_of_query,),
@@ -148,7 +148,7 @@
         ),
         cost_estimate=pl.CostEstimate(
             flops=flops,
-            transcendentals=length * length * heads_of_query * 12 // 16,
+            transcendentals=length * length * heads_of_query * 16 // 16,
             bytes_accessed=length * HEAD_WIDTH * (2 * 2 * heads_of_query + 2 * 2 + 2 * heads_of_query + 8),
         ),
     )(seg_row, seg_col, gathered, gathered, gathered, gathered)

time: 203 us -> 204 us (level)
  no operation moved by 1% of the time
where the time goes in v12:
time: 204 us
  waiting for transfers between devices  81 us (40%)
  starting transfers between devices  78.2 us (38%)
  local copies, waits for them, and re-layouts  16.7 us (8%)
  Pallas kernels  12.5 us (6%)
  other arithmetic  10.9 us (5%)
  between operations  4.27 us (2%)
    all_to_all x1, waiting for transfers between devices, per_device(): lax.all_to_all(packed, 'seq', split_axis=1, concat_axis=0, tiled=True)  38.5 us
    all_to_all x1, starting transfers between devices, route(): spread = lax.all_to_all(flat, 'dp', 0, 0, tiled=True)  36 us
    all_to_all x1, starting transfers between devices, route_block(): spread = lax.all_to_all(flat, 'dp', 0, 0, tiled=True)  14.6 us
    all_to_all x1, waiting for transfers between devices, per_device(): lax.all_to_all(low, 'seq', split_axis=0, concat_axis=1, tiled=True)  14.4 us
    pallas_call x1, Pallas kernels, attend_back_kernel(): pl.pallas_call(attend_kernel, grid=(heads_of_query,), in_specs=[pl.BlockS...  12.5 us
    all_to_all x1, waiting for transfers between devices, route(): spread = lax.all_to_all(flat, 'dp', 0, 0, tiled=True)  10 us
    all_to_all x1, starting transfers between devices, per_device(): lax.all_to_all(packed, 'seq', split_axis=1, concat_axis=0, tiled=True)  9.9 us
    all_to_all x1, waiting for transfers between devices, route_block(): back = lax.all_to_all(routed, 'dp', 0, 0, tiled=True)  8.53 us
  transfers between devices with their start and end apart: 6, of which 6 were waited for; matrix products, arithmetic and copies ran while one was open for 6% of the time, Pallas kernels for 0%

profile of v12, /device:TPU:1, one launch (start us, length us, event | category | flops | bytes accessed | tf_op | source)
XLA Modules:
  0.0 203.7 jit_solution(1681918403204039281)
XLA Ops:
  0.7 1.8 copy.134
  2.4 14.6 %all-to-all-start = ((bf16[64,2,8,128]{3,2,1,0:T(8,128)(2,1)}), bf16[64,2,8,128]{3,2,1,0:T(8,128)(2,1)S(1)}, u32[]{:S(2)}, u32[]{:S(2)}) async-start(bf16[64,2,8,128]{3,2,1,0:T(8,128)(2,1)} %bitcast.41), calls=%async_computation | async-start | bytes 524288 | tf_op jit(solution)/shard_map/all_to_all | solution.py:161
  17.0 0.7 compare_select_fusion.2
  17.7 0.8 scatter_custom_fusion
  18.5 0.6 dynamic_slice.16
  20.4 0.7 bitcast_or_fusion
  21.1 0.7 compare_and_fusion.2
  22.4 0.8 constant_dynamic-slice_fusion.2
  23.7 0.6 fusion.5
  24.2 0.7 compare_and_fusion.1
  24.9 1.4 copy_bitcast_fusion
  26.3 2.9 %all-to-all-done = bf16[64,2,8,128]{3,2,1,0:T(8,128)(2,1)S(1)} async-done(((bf16[64,2,8,128]{3,2,1,0:T(8,128)(2,1)}), bf16[64,2,8,128]{3,2,1,0:T(8,128)(2,1)S(1)}, u32[]{:S(2)}, u32[]{:S(2)}) %all-to-all-start) | async-done | bytes 262176 | tf_op jit(solution)/shard_map/all_to_all | solution.py:161
  29.3 0.6 gather_fusion
  30.0 0.2 copy.107
  30.3 0.9 gather_fusion.2
  31.1 0.8 fusion
  32.0 7.8 %all-to-all-start.1 = ((bf16[64,2,2,128]{3,1,2,0:T(2,128)(2,1)}), bf16[64,2,2,128]{3,1,2,0:T(2,128)(2,1)S(1)}, u32[]{:S(2)}, u32[]{:S(2)}) async-start(bf16[64,2,2,128]{3,1,2,0:T(2,128)(2,1)} %fusion), calls=%async_computation.1 | async-start | bytes 131072 | tf_op jit(solution)/shard_map/all_to_all | solution.py:164
  39.8 0.7 iota_compare_fusion.3
  40.5 0.2 copy.111
  40.6 0.6 iota_compare_fusion.4
  41.3 8.5 %all-to-all-done.1 = bf16[64,2,2,128]{3,1,2,0:T(2,128)(2,1)S(1)} async-done(((bf16[64,2,2,128]{3,1,2,0:T(2,128)(2,1)}), bf16[64,2,2,128]{3,1,2,0:T(2,128)(2,1)S(1)}, u32[]{:S(2)}, u32[]{:S(2)}) %all-to-all-start.1) | async-done | bytes 65568 | tf_op jit(solution)/shard_map/all_to_all | solution.py:164
  50.2 0.2 copy.114
  50.4 1.7 pad_maximum_fusion
  52.1 9.9 %all-to-all-start.2 = ((bf16[128,8,1024]{2,0,1:T(8,128)(2,1)}), bf16[128,8,1024]{2,0,1:T(8,128)(2,1)S(1)}, u32[]{:S(2)}, u32[]{:S(2)}) async-start(bf16[128,8,1024]{2,0,1:T(8,128)(2,1)} %pad_maximum_fusion), calls=%async_computation.2 | async-start | bytes 4194304 | tf_op jit(solution)/shard_map/all_to_all | solution.py:216
  62.0 0.2 reduce-window.8
  62.3 0.2 copy.116.seg_row_ref
  62.5 38.5 %all-to-all-done.2 = bf16[128,8,1024]{2,0,1:T(8,128)(2,1)S(1)} async-done(((bf16[128,8,1024]{2,0,1:T(8,128)(2,1)}), bf16[128,8,1024]{2,0,1:T(8,128)(2,1)S(1)}, u32[]{:S(2)}, u32[]{:S(2)}) %all-to-all-start.2) | async-done | bytes 2097184 | tf_op jit(solution)/shard_map/all_to_all | solution.py:216
  101.0 12.5 %shard_map.94 = (bf16[1024,384]{1,0:T(8,128)(2,1)S(1)}, f32[1024,128]{1,0:T(8,128)S(1)}, f32[1024,128]{1,0:T(8,128)S(1)}) custom-call(s32[1024,1]{1,0:T(8,128)S(1)} %copy.116.seg_row_ref, s32[1,1024]{1,0:T(1,128)S(1)} %bitcast.61, bf16[1024,1024]{1,0:T(8,128)(2,1)S(1)} %bitcast.56, bf16[1024,1024]{1,0:T(8,128)(2,1)S(1)} %bitcast.57, ...), custom_call_target="tpu_custom_call" | custom-call | flops 4026531840 | bytes 3932160 | tf_op jit(solution)/shard_map/pallas_call | solution.py:125
  113.7 1.5 copy.117
  115.2 5.5 %all-to-all-start.3 = ((bf16[8,128,640]{1,2,0:T(8,128)(2,1)}), bf16[8,128,640]{1,2,0:T(8,128)(2,1)S(1)}, u32[]{:S(2)}, u32[]{:S(2)}) async-start(bf16[8,128,640]{1,2,0:T(8,128)(2,1)} %copy.117), calls=%async_computation.3 | async-start | bytes 2621440 | tf_op jit(solution)/shard_map/all_to_all | solution.py:233
  122.0 14.4 %all-to-all-done.3 = bf16[8,128,640]{1,2,0:T(8,128)(2,1)S(1)} async-done(((bf16[8,128,640]{1,2,0:T(8,128)(2,1)}), bf16[8,128,640]{1,2,0:T(8,128)(2,1)S(1)}, u32[]{:S(2)}, u32[]{:S(2)}) %all-to-all-start.3) | async-done | bytes 1310752 | tf_op jit(solution)/shard_map/all_to_all | solution.py:233
  136.8 0.5 broadcast.99
  137.3 1.0 reduce.1
  138.3 0.6 reshape.225
  139.0 36.0 %all-to-all-start.4 = ((bf16[64,2,256]{2,1,0:T(2,128)(2,1)}), bf16[64,2,256]{2,1,0:T(2,128)(2,1)S(1)}, u32[]{:S(2)}, u32[]{:S(2)}) async-start(bf16[64,2,256]{2,1,0:T(2,128)(2,1)} %reshape.225), calls=%async_computation.4 | async-start | bytes 131072 | tf_op jit(solution)/shard_map/all_to_all | solution.py:171
  175.0 10.0 %all-to-all-done.4 = bf16[64,2,256]{2,1,0:T(2,128)(2,1)S(1)} async-done(((bf16[64,2,256]{2,1,0:T(2,128)(2,1)}), bf16[64,2,256]{2,1,0:T(2,128)(2,1)S(1)}, u32[]{:S(2)}, u32[]{:S(2)}) %all-to-all-start.4) | async-done | bytes 65568 | tf_op jit(solution)/shard_map/all_to_all | solution.py:171
  185.1 0.7 gather_fusion.1
  185.9 0.7 reduce.2
  186.6 0.6 reshape.227
  187.2 4.4 %all-to-all-start.5 = ((bf16[64,2,256]{2,1,0:T(2,128)(2,1)}), bf16[64,2,256]{2,1,0:T(2,128)(2,1)S(1)}, u32[]{:S(2)}, u32[]{:S(2)}) async-start(bf16[64,2,256]{2,1,0:T(2,128)(2,1)} %reshape.227), calls=%async_computation.5 | async-start | bytes 131072 | tf_op jit(solution)/shard_map/all_to_all | solution.py:173
  191.7 0.7 iota_compare_fusion.1
  192.3 0.7 iota_compare_fusion.2
  193.1 1.2 copy.125
  194.2 0.8 copy.127
  195.1 6.7 %all-to-all-done.5 = bf16[64,2,256]{2,1,0:T(2,128)(2,1)S(1)} async-done(((bf16[64,2,256]{2,1,0:T(2,128)(2,1)}), bf16[64,2,256]{2,1,0:T(2,128)(2,1)S(1)}, u32[]{:S(2)}, u32[]{:S(2)}) %all-to-all-start.5) | async-done | bytes 65568 | tf_op jit(solution)/shard_map/all_to_all | solution.py:173
  201.9 0.4 reduce
  202.6 0.2 add_convert_fusion
  202.8 0.9 copy.126
  (43 shorter events, 2.3 us)
Async XLA Ops:
  0.6 23.0 %copy-start = (bf16[128,1024]{1,0:T(8,128)(2,1)S(1)}, bf16[128,1024]{1,0:T(8,128)(2,1)}, u32[]{:S(2)}) copy-start(bf16[128,1024]{1,0:T(8,128)(2,1)} %param.9) | copy-start | bytes 786436
  0.6 24.3 %copy-start.2 = (bf16[128,3072]{1,0:T(8,128)(2,1)S(1)}, bf16[128,3072]{1,0:T(8,128)(2,1)}, u32[]{:S(2)}) copy-start(bf16[128,3072]{1,0:T(8,128)(2,1)} %param.10) | copy-start | bytes 2359300
  2.4 26.8 %all-to-all-start = ((bf16[64,2,8,128]{3,2,1,0:T(8,128)(2,1)}), bf16[64,2,8,128]{3,2,1,0:T(8,128)(2,1)S(1)}, u32[]{:S(2)}, u32[]{:S(2)}) async-start(bf16[64,2,8,128]{3,2,1,0:T(8,128)(2,1)} %bitcast.41), calls=%async_computation | async-start | bytes 524288 | tf_op jit(solution)/shard_map/all_to_all | solution.py:161
  24.9 15.5 %copy-start.1 = (bf16[128,1024]{1,0:T(8,128)(2,1)S(1)}, bf16[128,1024]{1,0:T(8,128)(2,1)}, u32[]{:S(2)}) copy-start(bf16[128,1024]{1,0:T(8,128)(2,1)} %param.8) | copy-start | bytes 786436
  32.0 17.8 %all-to-all-start.1 = ((bf16[64,2,2,128]{3,1,2,0:T(2,128)(2,1)}), bf16[64,2,2,128]{3,1,2,0:T(2,128)(2,1)S(1)}, u32[]{:S(2)}, u32[]{:S(2)}) async-start(bf16[64,2,2,128]{3,1,2,0:T(2,128)(2,1)} %fusion), calls=%async_computation.1 | async-start | bytes 131072 | tf_op jit(solution)/shard_map/all_to_all | solution.py:164
  52.1 9.9 %copy-start.3 = (s32[1,4]{1,0:T(1,128)S(1)}, s32[1,4]{1,0:T(1,128)}, u32[]{:S(2)}) copy-start(s32[1,4]{1,0:T(1,128)} %param.11) | copy-start | bytes 52
  52.1 48.9 %all-to-all-start.2 = ((bf16[128,8,1024]{2,0,1:T(8,128)(2,1)}), bf16[128,8,1024]{2,0,1:T(8,128)(2,1)S(1)}, u32[]{:S(2)}, u32[]{:S(2)}) async-start(bf16[128,8,1024]{2,0,1:T(8,128)(2,1)} %pad_maximum_fusion), calls=%async_computation.2 | async-start | bytes 4194304 | tf_op jit(solution)/shard_map/all_to_all | solution.py:216
  115.2 21.2 %all-to-all-start.3 = ((bf16[8,128,640]{1,2,0:T(8,128)(2,1)}), bf16[8,128,640]{1,2,0:T(8,128)(2,1)S(1)}, u32[]{:S(2)}, u32[]{:S(2)}) async-start(bf16[8,128,640]{1,2,0:T(8,128)(2,1)} %copy.117), calls=%async_computation.3 | async-start | bytes 2621440 | tf_op jit(solution)/shard_map/all_to_all | solution.py:233
  139.0 46.1 %all-to-all-start.4 = ((bf16[64,2,256]{2,1,0:T(2,128)(2,1)}), bf16[64,2,256]{2,1,0:T(2,128)(2,1)S(1)}, u32[]{:S(2)}, u32[]{:S(2)}) async-start(bf16[64,2,256]{2,1,0:T(2,128)(2,1)} %reshape.225), calls=%async_computation.4 | async-start | bytes 131072 | tf_op jit(solution)/shard_map/all_to_all | solution.py:171
  187.2 14.6 %all-to-all-start.5 = ((bf16[64,2,256]{2,1,0:T(2,128)(2,1)}), bf16[64,2,256]{2,1,0:T(2,128)(2,1)S(1)}, u32[]{:S(2)}, u32[]{:S(2)}) async-start(bf16[64,2,256]{2,1,0:T(2,128)(2,1)} %reshape.227), calls=%async_computation.5 | async-start | bytes 131072 | tf_op jit(solution)/shard_map/all_to_all | solution.py:173

commit v13 on v11

--- a/solution.py
+++ b/solution.py
@@ -80,9 +80,11 @@
         dk_ref[...] = jnp.zeros_like(dk_ref)
         dv_ref[...] = jnp.zeros_like(dv_ref)
 
-    for block in range(length // BLOCK_ROWS):
-        rows = pl.ds(block * BLOCK_ROWS, BLOCK_ROWS)
-        span = (block + 1) * BLOCK_ROWS
+    bounds = [0, 3 * length // 8, 3 * length // 4, length]
+    for block in range(len(bounds) - 1):
+        first, size = bounds[block], bounds[block + 1] - bounds[block]
+        rows = pl.ds(first, size)
+        span = bounds[block + 1]
         keys = k_ref[0:span, :]
         vals = v_ref[0:span, :]
         q_rows = q_ref[rows, :]
@@ -90,8 +92,8 @@
         scores = lax.dot_general(
             q_rows, keys, (((1,), (1,)), ((), ())), preferred_element_type=jnp.float32
         ) * scaling
-        row_pos = block * BLOCK_ROWS + lax.broadcasted_iota(jnp.int32, (BLOCK_ROWS, span), 0)
-        col_pos = lax.broadcasted_iota(jnp.int32, (BLOCK_ROWS, span), 1)
+        row_pos = first + lax.broadcasted_iota(jnp.int32, (size, span), 0)
+        col_pos = lax.broadcasted_iota(jnp.int32, (size, span), 1)
         same = seg_row_ref[rows, :] == seg_col_ref[:, 0:span]
         visible = jnp.logical_and(row_pos >= col_pos, same)
         scores = jnp.where(visible, scores, masked_score)
@@ -121,7 +123,7 @@
     seg_col = segment.reshape(1, length)
     full = lambda h: (0, 0)
     col = lambda b: pl.BlockSpec((length, HEAD_WIDTH), lambda h: (0, b))
-    flops = 5 * 2 * length * length * HEAD_WIDTH * heads_of_query * 12 // 16
+    flops = 5 * 2 * length * length * HEAD_WIDTH * heads_of_query * 11 // 16
     return pl.pallas_call(
         attend_kernel,
         grid=(heads_of_query,),
@@ -148,7 +150,7 @@
         ),
         cost_estimate=pl.CostEstimate(
             flops=flops,
-            transcendentals=length * length * heads_of_query * 12 // 16,
+            transcendentals=length * length * heads_of_query * 11 // 16,
             bytes_accessed=length * HEAD_WIDTH * (2 * 2 * heads_of_query + 2 * 2 + 2 * heads_of_query + 8),
         ),
     )(seg_row, seg_col, gathered, gathered, gathered, gathered)

time: 203 us -> 204 us (level)
  no operation moved by 1% of the time
where the time goes in v13:
time: 204 us
  waiting for transfers between devices  81 us (40%)
  starting transfers between devices  78.2 us (38%)
  local copies, waits for them, and re-layouts  16.7 us (8%)
  Pallas kernels  12.6 us (6%)
  other arithmetic  10.9 us (5%)
  between operations  4.27 us (2%)
    all_to_all x1, waiting for transfers between devices, per_device(): lax.all_to_all(packed, 'seq', split_axis=1, concat_axis=0, tiled=True)  38.5 us
    all_to_all x1, starting transfers between devices, route(): spread = lax.all_to_all(flat, 'dp', 0, 0, tiled=True)  36 us
    all_to_all x1, starting transfers between devices, route_block(): spread = lax.all_to_all(flat, 'dp', 0, 0, tiled=True)  14.6 us
    all_to_all x1, waiting for transfers between devices, per_device(): lax.all_to_all(low, 'seq', split_axis=0, concat_axis=1, tiled=True)  14.4 us
    pallas_call x1, Pallas kernels, attend_back_kernel(): pl.pallas_call(attend_kernel, grid=(heads_of_query,), in_specs=[pl.BlockS...  12.6 us
    all_to_all x1, waiting for transfers between devices, route(): spread = lax.all_to_all(flat, 'dp', 0, 0, tiled=True)  10 us
    all_to_all x1, starting transfers between devices, per_device(): lax.all_to_all(packed, 'seq', split_axis=1, concat_axis=0, tiled=True)  9.9 us
    all_to_all x1, waiting for transfers between devices, route_block(): back = lax.all_to_all(routed, 'dp', 0, 0, tiled=True)  8.53 us
  transfers between devices with their start and end apart: 6, of which 6 were waited for; matrix products, arithmetic and copies ran while one was open for 6% of the time, Pallas kernels for 0%

profile of v13, /device:TPU:1, one launch (start us, length us, event | category | flops | bytes accessed | tf_op | source)
XLA Modules:
  0.0 203.8 jit_solution(1783434920990245852)
XLA Ops:
  0.7 1.8 copy.134
  2.4 14.6 %all-to-all-start = ((bf16[64,2,8,128]{3,2,1,0:T(8,128)(2,1)}), bf16[64,2,8,128]{3,2,1,0:T(8,128)(2,1)S(1)}, u32[]{:S(2)}, u32[]{:S(2)}) async-start(bf16[64,2,8,128]{3,2,1,0:T(8,128)(2,1)} %bitcast.41), calls=%async_computation | async-start | bytes 524288 | tf_op jit(solution)/shard_map/all_to_all | solution.py:163
  17.0 0.7 compare_select_fusion.2
  17.7 0.8 scatter_custom_fusion
  18.5 0.6 dynamic_slice.16
  20.4 0.7 bitcast_or_fusion
  21.1 0.7 compare_and_fusion.2
  22.4 0.8 constant_dynamic-slice_fusion.2
  23.7 0.6 fusion.5
  24.2 0.7 compare_and_fusion.1
  24.9 1.4 copy_bitcast_fusion
  26.3 2.9 %all-to-all-done = bf16[64,2,8,128]{3,2,1,0:T(8,128)(2,1)S(1)} async-done(((bf16[64,2,8,128]{3,2,1,0:T(8,128)(2,1)}), bf16[64,2,8,128]{3,2,1,0:T(8,128)(2,1)S(1)}, u32[]{:S(2)}, u32[]{:S(2)}) %all-to-all-start) | async-done | bytes 262176 | tf_op jit(solution)/shard_map/all_to_all | solution.py:163
  29.3 0.6 gather_fusion
  30.0 0.2 copy.107
  30.3 0.9 gather_fusion.2
  31.1 0.8 fusion
  32.0 7.8 %all-to-all-start.1 = ((bf16[64,2,2,128]{3,1,2,0:T(2,128)(2,1)}), bf16[64,2,2,128]{3,1,2,0:T(2,128)(2,1)S(1)}, u32[]{:S(2)}, u32[]{:S(2)}) async-start(bf16[64,2,2,128]{3,1,2,0:T(2,128)(2,1)} %fusion), calls=%async_computation.1 | async-start | bytes 131072 | tf_op jit(solution)/shard_map/all_to_all | solution.py:166
  39.8 0.7 iota_compare_fusion.3
  40.4 0.2 copy.111
  40.6 0.6 iota_compare_fusion.4
  41.3 8.5 %all-to-all-done.1 = bf16[64,2,2,128]{3,1,2,0:T(2,128)(2,1)S(1)} async-done(((bf16[64,2,2,128]{3,1,2,0:T(2,128)(2,1)}), bf16[64,2,2,128]{3,1,2,0:T(2,128)(2,1)S(1)}, u32[]{:S(2)}, u32[]{:S(2)}) %all-to-all-start.1) | async-done | bytes 65568 | tf_op jit(solution)/shard_map/all_to_all | solution.py:166
  50.2 0.2 copy.114
  50.4 1.7 pad_maximum_fusion
  52.1 9.9 %all-to-all-start.2 = ((bf16[128,8,1024]{2,0,1:T(8,128)(2,1)}), bf16[128,8,1024]{2,0,1:T(8,128)(2,1)S(1)}, u32[]{:S(2)}, u32[]{:S(2)}) async-start(bf16[128,8,1024]{2,0,1:T(8,128)(2,1)} %pad_maximum_fusion), calls=%async_computation.2 | async-start | bytes 4194304 | tf_op jit(solution)/shard_map/all_to_all | solution.py:218
  62.0 0.2 reduce-window.8
  62.3 0.2 copy.116.seg_row_ref
  62.5 38.5 %all-to-all-done.2 = bf16[128,8,1024]{2,0,1:T(8,128)(2,1)S(1)} async-done(((bf16[128,8,1024]{2,0,1:T(8,128)(2,1)}), bf16[128,8,1024]{2,0,1:T(8,128)(2,1)S(1)}, u32[]{:S(2)}, u32[]{:S(2)}) %all-to-all-start.2) | async-done | bytes 2097184 | tf_op jit(solution)/shard_map/all_to_all | solution.py:218
  101.0 12.6 %shard_map.94 = (bf16[1024,384]{1,0:T(8,128)(2,1)S(1)}, f32[1024,128]{1,0:T(8,128)S(1)}, f32[1024,128]{1,0:T(8,128)S(1)}) custom-call(s32[1024,1]{1,0:T(8,128)S(1)} %copy.116.seg_row_ref, s32[1,1024]{1,0:T(1,128)S(1)} %bitcast.61, bf16[1024,1024]{1,0:T(8,128)(2,1)S(1)} %bitcast.56, bf16[1024,1024]{1,0:T(8,128)(2,1)S(1)} %bitcast.57, ...), custom_call_target="tpu_custom_call" | custom-call | flops 2768240640 | bytes 3932160 | tf_op jit(solution)/shard_map/pallas_call | solution.py:127
  113.8 1.5 copy.117
  115.3 5.5 %all-to-all-start.3 = ((bf16[8,128,640]{1,2,0:T(8,128)(2,1)}), bf16[8,128,640]{1,2,0:T(8,128)(2,1)S(1)}, u32[]{:S(2)}, u32[]{:S(2)}) async-start(bf16[8,128,640]{1,2,0:T(8,128)(2,1)} %copy.117), calls=%async_computation.3 | async-start | bytes 2621440 | tf_op jit(solution)/shard_map/all_to_all | solution.py:235
  122.1 14.4 %all-to-all-done.3 = bf16[8,128,640]{1,2,0:T(8,128)(2,1)S(1)} async-done(((bf16[8,128,640]{1,2,0:T(8,128)(2,1)}), bf16[8,128,640]{1,2,0:T(8,128)(2,1)S(1)}, u32[]{:S(2)}, u32[]{:S(2)}) %all-to-all-start.3) | async-done | bytes 1310752 | tf_op jit(solution)/shard_map/all_to_all | solution.py:235
  136.9 0.5 broadcast.99
  137.4 1.0 reduce.1
  138.4 0.6 reshape.225
  139.1 36.0 %all-to-all-start.4 = ((bf16[64,2,256]{2,1,0:T(2,128)(2,1)}), bf16[64,2,256]{2,1,0:T(2,128)(2,1)S(1)}, u32[]{:S(2)}, u32[]{:S(2)}) async-start(bf16[64,2,256]{2,1,0:T(2,128)(2,1)} %reshape.225), calls=%async_computation.4 | async-start | bytes 131072 | tf_op jit(solution)/shard_map/all_to_all | solution.py:173
  175.1 10.0 %all-to-all-done.4 = bf16[64,2,256]{2,1,0:T(2,128)(2,1)S(1)} async-done(((bf16[64,2,256]{2,1,0:T(2,128)(2,1)}), bf16[64,2,256]{2,1,0:T(2,128)(2,1)S(1)}, u32[]{:S(2)}, u32[]{:S(2)}) %all-to-all-start.4) | async-done | bytes 65568 | tf_op jit(solution)/shard_map/all_to_all | solution.py:173
  185.2 0.7 gather_fusion.1
  186.0 0.7 reduce.2
  186.7 0.6 reshape.227
  187.3 4.4 %all-to-all-start.5 = ((bf16[64,2,256]{2,1,0:T(2,128)(2,1)}), bf16[64,2,256]{2,1,0:T(2,128)(2,1)S(1)}, u32[]{:S(2)}, u32[]{:S(2)}) async-start(bf16[64,2,256]{2,1,0:T(2,128)(2,1)} %reshape.227), calls=%async_computation.5 | async-start | bytes 131072 | tf_op jit(solution)/shard_map/all_to_all | solution.py:175
  191.8 0.7 iota_compare_fusion.1
  192.5 0.7 iota_compare_fusion.2
  193.2 1.2 copy.125
  194.4 0.8 copy.127
  195.2 6.7 %all-to-all-done.5 = bf16[64,2,256]{2,1,0:T(2,128)(2,1)S(1)} async-done(((bf16[64,2,256]{2,1,0:T(2,128)(2,1)}), bf16[64,2,256]{2,1,0:T(2,128)(2,1)S(1)}, u32[]{:S(2)}, u32[]{:S(2)}) %all-to-all-start.5) | async-done | bytes 65568 | tf_op jit(solution)/shard_map/all_to_all | solution.py:175
  202.0 0.4 reduce
  202.7 0.2 add_convert_fusion
  202.9 0.9 copy.126
  (43 shorter events, 2.3 us)
Async XLA Ops:
  0.6 23.0 %copy-start = (bf16[128,1024]{1,0:T(8,128)(2,1)S(1)}, bf16[128,1024]{1,0:T(8,128)(2,1)}, u32[]{:S(2)}) copy-start(bf16[128,1024]{1,0:T(8,128)(2,1)} %param.9) | copy-start | bytes 786436
  0.6 24.3 %copy-start.2 = (bf16[128,3072]{1,0:T(8,128)(2,1)S(1)}, bf16[128,3072]{1,0:T(8,128)(2,1)}, u32[]{:S(2)}) copy-start(bf16[128,3072]{1,0:T(8,128)(2,1)} %param.10) | copy-start | bytes 2359300
  2.4 26.8 %all-to-all-start = ((bf16[64,2,8,128]{3,2,1,0:T(8,128)(2,1)}), bf16[64,2,8,128]{3,2,1,0:T(8,128)(2,1)S(1)}, u32[]{:S(2)}, u32[]{:S(2)}) async-start(bf16[64,2,8,128]{3,2,1,0:T(8,128)(2,1)} %bitcast.41), calls=%async_computation | async-start | bytes 524288 | tf_op jit(solution)/shard_map/all_to_all | solution.py:163
  24.9 15.5 %copy-start.1 = (bf16[128,1024]{1,0:T(8,128)(2,1)S(1)}, bf16[128,1024]{1,0:T(8,128)(2,1)}, u32[]{:S(2)}) copy-start(bf16[128,1024]{1,0:T(8,128)(2,1)} %param.8) | copy-start | bytes 786436
  32.0 17.8 %all-to-all-start.1 = ((bf16[64,2,2,128]{3,1,2,0:T(2,128)(2,1)}), bf16[64,2,2,128]{3,1,2,0:T(2,128)(2,1)S(1)}, u32[]{:S(2)}, u32[]{:S(2)}) async-start(bf16[64,2,2,128]{3,1,2,0:T(2,128)(2,1)} %fusion), calls=%async_computation.1 | async-start | bytes 131072 | tf_op jit(solution)/shard_map/all_to_all | solution.py:166
  52.1 9.9 %copy-start.3 = (s32[1,4]{1,0:T(1,128)S(1)}, s32[1,4]{1,0:T(1,128)}, u32[]{:S(2)}) copy-start(s32[1,4]{1,0:T(1,128)} %param.11) | copy-start | bytes 52
  52.1 48.9 %all-to-all-start.2 = ((bf16[128,8,1024]{2,0,1:T(8,128)(2,1)}), bf16[128,8,1024]{2,0,1:T(8,128)(2,1)S(1)}, u32[]{:S(2)}, u32[]{:S(2)}) async-start(bf16[128,8,1024]{2,0,1:T(8,128)(2,1)} %pad_maximum_fusion), calls=%async_computation.2 | async-start | bytes 4194304 | tf_op jit(solution)/shard_map/all_to_all | solution.py:218
  115.3 21.2 %all-to-all-start.3 = ((bf16[8,128,640]{1,2,0:T(8,128)(2,1)}), bf16[8,128,640]{1,2,0:T(8,128)(2,1)S(1)}, u32[]{:S(2)}, u32[]{:S(2)}) async-start(bf16[8,128,640]{1,2,0:T(8,128)(2,1)} %copy.117), calls=%async_computation.3 | async-start | bytes 2621440 | tf_op jit(solution)/shard_map/all_to_all | solution.py:235
  139.1 46.1 %all-to-all-start.4 = ((bf16[64,2,256]{2,1,0:T(2,128)(2,1)}), bf16[64,2,256]{2,1,0:T(2,128)(2,1)S(1)}, u32[]{:S(2)}, u32[]{:S(2)}) async-start(bf16[64,2,256]{2,1,0:T(2,128)(2,1)} %reshape.225), calls=%async_computation.4 | async-start | bytes 131072 | tf_op jit(solution)/shard_map/all_to_all | solution.py:173
  187.3 14.6 %all-to-all-start.5 = ((bf16[64,2,256]{2,1,0:T(2,128)(2,1)}), bf16[64,2,256]{2,1,0:T(2,128)(2,1)S(1)}, u32[]{:S(2)}, u32[]{:S(2)}) async-start(bf16[64,2,256]{2,1,0:T(2,128)(2,1)} %reshape.227), calls=%async_computation.5 | async-start | bytes 131072 | tf_op jit(solution)/shard_map/all_to_all | solution.py:175
